TPU v7x, 256 devices: a whole 4x4x8 slice. The times are simulated.
256 devices in a mesh: patch: 8 (over z_hi, core), seq: 16 (over y, x), cfg: 2 (over z_lo).
Axes of the slice: x: 4, y: 4, z: 8 (z_hi: 4, z_lo: 2; z = z_hi * 2 + z_lo), core: 2. Of those that a mesh axis runs over, the one named last changes fastest.
Arguments:
- query: bfloat16 [36864, 2048], P(('cfg', 'patch', 'seq')), parts along dimension 0, may hold values from -16 to 16
- fresh_key: bfloat16 [36864, 2048], P(('cfg', 'patch', 'seq')), parts along dimension 0, may hold values from -6 to 6
- fresh_value: bfloat16 [36864, 2048], P(('cfg', 'patch', 'seq')), parts along dimension 0, may hold values from -6 to 6
- stale_key: bfloat16 [36864, 2048], P(('cfg', 'patch', 'seq')), parts along dimension 0, may hold values from -6 to 6
- stale_value: bfloat16 [36864, 2048], P(('cfg', 'patch', 'seq')), parts along dimension 0, may hold values from -6 to 6
- key_tiles: int32 [48, 18], P('patch'), may hold values from 0 to 47, as said below
- tile_count: int32 [48], P('patch'), may hold values from 1 to 18
Outputs:
- attended: bfloat16 [36864, 2048], P(('cfg', 'patch', 'seq')), parts along dimension 0
There are 2 independent parts, one for each index of `cfg`. A program takes and returns all parts, laid end to end along the dimension named above; an argument that names none is the same for every part. Nothing has to cross between parts.
Inputs may be any that keep to these rules, and one draw needn't show every extreme that they name: `key_tiles`: tile numbers are patch * 2 * 3 + row * 3 + column. The first tile_count[t] entries of row t are distinct tiles within one tile of t in patch, row and column (t itself among them); the other entries equal t and are ignored.
All inputs are finite; a program needn't handle non-finite values.
Results may differ from a plain program's by a relative error of at most 0.0049.
Values may be sent and summed in bfloat16 or wider, within the bound.
No kernel may reach another device: no remote copies, remote signals or barrier semaphores. Data moves between devices by JAX's collectives and lax.ppermute only.
A program may use at most 64 MiB of HBM per device.

v0:
```python
import jax
import jax.numpy as jnp
from jax import lax
from jax.sharding import PartitionSpec as P

NUM_HEADS = 16
HEAD_DIM = 128
TILE_TOKENS = 384
TILES_H = 2
TILES_W = 3
KEY_SLOTS = 18


soft_cap = 8.0


def with_halo(x, sides, width):
    for axis, dim in sides:
        size, length = (lax.axis_size(axis), x.shape[dim])
        up = [(i, (i + 1) % size) for i in range(size - 1)]
        down = [(j, i) for i, j in up]
        last = lax.slice_in_dim(x, length - width, length, axis=dim)
        leading = lax.slice_in_dim(x, 0, width, axis=dim)
        before = lax.ppermute(last, axis, up)
        after = lax.ppermute(leading, axis, down)
        x = jnp.concatenate([before, x, after], axis=dim)
    return x


def capped_weights(query_rows, key_rows):
    scores = lax.dot_general(
        query_rows, key_rows, (((1,), (1,)), ((), ())), preferred_element_type=jnp.float32
    )
    scores = scores * (1.0 / HEAD_DIM**0.5)
    return jnp.exp(soft_cap * jnp.tanh(scores / soft_cap) - soft_cap)


def on_device(query, fresh_key, fresh_value, stale_key, stale_value, key_tiles, tile_count):
    seq_count = lax.axis_size("seq")
    local_heads = NUM_HEADS // seq_count
    per_patch = TILES_H * TILES_W
    rows = query.shape[0]
    patch_rows = rows * seq_count
    q_heads, k_fresh, v_fresh = (
        lax.all_to_all(query, "seq", split_axis=1, concat_axis=0, tiled=True),
        lax.all_to_all(fresh_key, "seq", split_axis=1, concat_axis=0, tiled=True),
        lax.all_to_all(fresh_value, "seq", split_axis=1, concat_axis=0, tiled=True),
    )
    stale = jnp.stack([stale_key, stale_value])
    regrouped = lax.all_to_all(stale, "seq", split_axis=2, concat_axis=1, tiled=True)
    framed = with_halo(regrouped, (("patch", 1),), patch_rows)
    before = framed[:, :patch_rows]
    after = framed[:, 2 * patch_rows :]
    keys_all = jnp.concatenate([before[0], k_fresh, after[0]], 0)
    values_all = jnp.concatenate([before[1], v_fresh, after[1]], 0)
    first_tile = (lax.axis_index("patch") - 1) * per_patch
    local_ids = key_tiles - first_tile
    query_blocks = q_heads.reshape(per_patch, TILE_TOKENS, local_heads * HEAD_DIM)
    key_blocks = keys_all.reshape(3 * per_patch, TILE_TOKENS, local_heads, HEAD_DIM)
    value_blocks = values_all.reshape(3 * per_patch, TILE_TOKENS, local_heads, HEAD_DIM)

    def per_tile(inputs):
        query_tile, listed, count = inputs
        keys = key_blocks[listed]
        values = value_blocks[listed]
        valid = jnp.repeat(jnp.arange(KEY_SLOTS, dtype=jnp.int32) < count, TILE_TOKENS)

        def per_head(head):
            key_rows = lax.dynamic_index_in_dim(keys, head, 2, False).reshape(
                KEY_SLOTS * TILE_TOKENS, HEAD_DIM
            )
            value_rows = lax.dynamic_index_in_dim(values, head, 2, False).reshape(
                KEY_SLOTS * TILE_TOKENS, HEAD_DIM
            )
            weight = jnp.where(valid[None, :], capped_weights(query_tile, key_rows), 0.0)
            total = jnp.sum(weight, axis=1)
            numer = jnp.dot(
                weight.astype(jnp.bfloat16), value_rows, preferred_element_type=jnp.float32
            )
            return (numer / total[:, None]).astype(jnp.bfloat16)

        return lax.map(per_head, jnp.arange(local_heads, dtype=jnp.int32))

    outputs = lax.map(per_tile, (query_blocks, local_ids, tile_count))
    merged = jnp.transpose(outputs, (0, 2, 1, 3)).reshape(patch_rows, local_heads * HEAD_DIM)
    return lax.all_to_all(merged, "seq", split_axis=0, concat_axis=1, tiled=True)


def solution(mesh):
    return jax.shard_map(
        on_device,
        mesh=mesh,
        in_specs=(
            P(("cfg", "patch", "seq"), None),
            P(("cfg", "patch", "seq"), None),
            P(("cfg", "patch", "seq"), None),
            P(("cfg", "patch", "seq"), None),
            P(("cfg", "patch", "seq"), None),
            P("patch", None),
            P("patch"),
        ),
        out_specs=P(("cfg", "patch", "seq"), None),
        check_vma=False,
    )
```

profile of v0, /device:TPU:128, one launch (start us, length us, event | category | flops | bytes accessed | tf_op | source)
XLA Modules:
  0.0 261.7 jit_solution(5273997661690695232)
XLA Ops:
  0.0 2.4 pad_maximum_fusion.2
  2.4 4.6 %copy.25 = bf16[2,144,2048]{1,0,2:T(2,128)(2,1)S(1)} copy(bf16[2,144,2048]{2,1,0:T(8,128)(2,1)} %pad_maximum_fusion.2) | data formatting | bytes 2359296 | tf_op jit(solution)/shard_map/stack | solution.py:49
  7.1 35.3 %all_to_all.91 = bf16[2,144,2048]{1,0,2:T(2,128)(2,1)} all-to-all(bf16[2,144,2048]{1,0,2:T(2,128)(2,1)S(1)} %copy.25), channel_id=1, replica_groups=mesh['patch'=8,'seq'=16,'cfg'=2] {'seq'}, dimensions={2} | all-to-all | bytes 2359296 | tf_op jit(solution)/shard_map/all_to_all | solution.py:50
  42.4 4.8 %copy.26 = bf16[2,144,16,128]{3,1,2,0:T(8,128)(2,1)S(1)} copy(bf16[2,144,16,128]{1,0,3,2:T(2,128)(2,1)} %bitcast.102) | data formatting | bytes 2359296 | tf_op jit(solution)/shard_map/all_to_all | solution.py:50
  47.3 2.1 collective-permute-start
  49.3 0.9 copy_bitcast_fusion.1
  50.3 3.6 %all-to-all-start.3 = ((bf16[144,16,128]{2,0,1:T(8,128)(2,1)}), bf16[144,16,128]{2,0,1:T(8,128)(2,1)S(1)}, u32[]{:S(2)}, u32[]{:S(2)}) async-start(bf16[144,16,128]{2,0,1:T(8,128)(2,1)} %copy_bitcast_fusion.1), calls=%async_computation.3 | async-start | bytes 1179648 | tf_op jit(solution)/shard_map/all_to_all | solution.py:47
  53.9 0.9 copy_bitcast_fusion.2
  54.8 5.7 %collective-permute-start.1 = (bf16[2,2304,128]{2,1,0:T(8,128)(2,1)S(1)}, bf16[2,2304,128]{2,1,0:T(8,128)(2,1)S(1)}, u32[]{:S(2)}, u32[]{:S(2)}) collective-permute-start(bf16[2,2304,128]{2,1,0:T(8,128)(2,1)S(1)} %bitcast.106), channel_id=1, source_target_pairs={{32,0},{64,32},{96,64},{128,96},{160,128},{192,160},{224,192},{33,... | collective-permute-start | bytes 3538952 | tf_op jit(solution)/shard_map/ppermute | solution.py:25
  60.6 0.9 copy_bitcast_fusion.3
  61.5 18.2 %collective-permute-done = bf16[2,2304,128]{2,1,0:T(8,128)(2,1)} collective-permute-done((bf16[2,2304,128]{2,1,0:T(8,128)(2,1)S(1)}, bf16[2,2304,128]{2,1,0:T(8,128)(2,1)}, u32[]{:S(2)}, u32[]{:S(2)}) %collective-permute-start) | collective-permute-done | bytes 1179680 | tf_op jit(solution)/shard_map/ppermute | solution.py:24
  79.7 2.3 slice_bitcast_fusion.1
  82.1 4.7 %collective-permute-done.1 = bf16[2,2304,128]{2,1,0:T(8,128)(2,1)S(1)} collective-permute-done((bf16[2,2304,128]{2,1,0:T(8,128)(2,1)S(1)}, bf16[2,2304,128]{2,1,0:T(8,128)(2,1)S(1)}, u32[]{:S(2)}, u32[]{:S(2)}) %collective-permute-start.1) | collective-permute-done | bytes 1179680 | tf_op jit(solution)/shard_map/ppermute | solution.py:25
  86.7 1.1 slice_bitcast_fusion
  87.8 6.9 %all-to-all-start.2 = ((bf16[144,16,128]{2,0,1:T(8,128)(2,1)}), bf16[144,16,128]{2,0,1:T(8,128)(2,1)S(1)}, u32[]{:S(2)}, u32[]{:S(2)}) async-start(bf16[144,16,128]{2,0,1:T(8,128)(2,1)} %copy_bitcast_fusion.2), calls=%async_computation.2 | async-start | bytes 1179648 | tf_op jit(solution)/shard_map/all_to_all | solution.py:46
  94.7 1.4 pad_maximum_fusion.1
  96.1 11.8 %all-to-all-done.2 = bf16[144,16,128]{2,0,1:T(8,128)(2,1)S(1)} async-done(((bf16[144,16,128]{2,0,1:T(8,128)(2,1)}), bf16[144,16,128]{2,0,1:T(8,128)(2,1)S(1)}, u32[]{:S(2)}, u32[]{:S(2)}) %all-to-all-start.2) | async-done | bytes 589856 | tf_op jit(solution)/shard_map/all_to_all | solution.py:46
  107.9 3.6 %all-to-all-start = ((bf16[144,16,128]{2,0,1:T(8,128)(2,1)}), bf16[144,16,128]{2,0,1:T(8,128)(2,1)S(1)}, u32[]{:S(2)}, u32[]{:S(2)}) async-start(bf16[144,16,128]{2,0,1:T(8,128)(2,1)} %copy_bitcast_fusion.3), calls=%async_computation | async-start | bytes 1179648 | tf_op jit(solution)/shard_map/all_to_all | solution.py:45
  111.5 2.6 pad_maximum_fusion
  114.1 9.7 %all-to-all-done = bf16[144,16,128]{2,0,1:T(8,128)(2,1)S(1)} async-done(((bf16[144,16,128]{2,0,1:T(8,128)(2,1)}), bf16[144,16,128]{2,0,1:T(8,128)(2,1)S(1)}, u32[]{:S(2)}, u32[]{:S(2)}) %all-to-all-start) | async-done | bytes 589856 | tf_op jit(solution)/shard_map/all_to_all | solution.py:45
  123.9 122.0 %while.16 = (s32[]{:T(128)}, bf16[6,1,384,128]{3,2,1,0:T(8,128)(2,1)}, s32[6]{0:T(128)S(1)}, bf16[6,384,128]{2,1,0:T(8,128)(2,1)S(1)}, s32[6,18]{1,0:T(8,128)S(1...) while((s32[]{:T(128)}, bf16[6,1,384,128]{3,2,1,0:T(8,128)(2,1)}, ...), condition=%wide.region_2.3_spmd, body=%wide.region_0.2_spmd.sunk | while | flops 1374978816 | bytes 26185260 | solution.py:84
  123.9 3.9 %gather_fusion.1 = bf16[18,384,128]{2,1,0:T(8,128)(2,1)} fusion(bf16[18,384,128]{2,1,0:T(8,128)(2,1)} %bitcast.99, s32[1024]{0:T(1024)S(1)} %pad_clamp_fusion.2), kind=kCustom, calls=%fused_computation.clone.1 | custom fusion | bytes 3539016 | tf_op jit(solution)/shard_map/while/body/eval_jaxpr/gather | solution.py:64
  128.4 0.6 iota_compare_fusion.2
  129.1 7.6 %fusion.37 = (f32[384]{0:T(512)S(1)}, bf16[384,6912]{1,0:T(8,128)(2,1)}) fusion(bf16[6912,128]{1,0:T(8,128)(2,1)} %bitcast.100, bf16[6,384,128]{2,1,0:T(8,128)(2,1)} %copy-done.3, s32[]{:T(128)} %get-tuple-element.191, pred[6912]{0:T(1024)(128)(4,1)S(1)} %broadcast_in_dim.56), kind=kOutput, calls=%fused_computation.30.clone.1 | convolution fusion | flops 695402112 | bytes 7185152 | tf_op jit(solution)/shard_map/while/body/eval_jaxpr/while/body/eval_jaxpr/dot_general | solution.py:31
  136.7 2.2 gather_fusion
  138.9 5.3 %fusion.38 = bf16[6,1,384,128]{3,2,1,0:T(8,128)(2,1)} fusion(bf16[6,1,384,128]{3,2,1,0:T(8,128)(2,1)} %get-tuple-element.192, s32[]{:T(128)} %get-tuple-element.191, bf16[6912,128]{1,0:T(8,128)(2,1)} %bitcast.101, bf16[384,6912]{1,0:T(8,128)(2,1)} %get-tuple-element.181, f32[384]{0:T(512)S(1)} %get-tuple-element.182), kind=kOutput, calls=%fused_computation.8.clone.1 | convolution fusion | flops 679575552 | bytes 7178240 | tf_op jit(solution)/shard_map/while/body/eval_jaxpr/while/body/eval_jaxpr/dot_general | solution.py:77
  144.2 3.9 %gather_fusion.1 = bf16[18,384,128]{2,1,0:T(8,128)(2,1)} fusion(bf16[18,384,128]{2,1,0:T(8,128)(2,1)} %bitcast.99, s32[1024]{0:T(1024)S(1)} %pad_clamp_fusion.2), kind=kCustom, calls=%fused_computation.clone.1 | custom fusion | bytes 3539016 | tf_op jit(solution)/shard_map/while/body/eval_jaxpr/gather | solution.py:64
  149.5 7.5 %fusion.37 = (f32[384]{0:T(512)S(1)}, bf16[384,6912]{1,0:T(8,128)(2,1)}) fusion(bf16[6912,128]{1,0:T(8,128)(2,1)} %bitcast.100, bf16[6,384,128]{2,1,0:T(8,128)(2,1)} %copy-done.3, s32[]{:T(128)} %get-tuple-element.191, pred[6912]{0:T(1024)(128)(4,1)S(1)} %broadcast_in_dim.56), kind=kOutput, calls=%fused_computation.30.clone.1 | convolution fusion | flops 695402112 | bytes 7185152 | tf_op jit(solution)/shard_map/while/body/eval_jaxpr/while/body/eval_jaxpr/dot_general | solution.py:31
  157.0 2.2 gather_fusion
  159.2 5.3 %fusion.38 = bf16[6,1,384,128]{3,2,1,0:T(8,128)(2,1)} fusion(bf16[6,1,384,128]{3,2,1,0:T(8,128)(2,1)} %get-tuple-element.192, s32[]{:T(128)} %get-tuple-element.191, bf16[6912,128]{1,0:T(8,128)(2,1)} %bitcast.101, bf16[384,6912]{1,0:T(8,128)(2,1)} %get-tuple-element.181, f32[384]{0:T(512)S(1)} %get-tuple-element.182), kind=kOutput, calls=%fused_computation.8.clone.1 | convolution fusion | flops 679575552 | bytes 7178240 | tf_op jit(solution)/shard_map/while/body/eval_jaxpr/while/body/eval_jaxpr/dot_general | solution.py:77
  164.6 3.9 %gather_fusion.1 = bf16[18,384,128]{2,1,0:T(8,128)(2,1)} fusion(bf16[18,384,128]{2,1,0:T(8,128)(2,1)} %bitcast.99, s32[1024]{0:T(1024)S(1)} %pad_clamp_fusion.2), kind=kCustom, calls=%fused_computation.clone.1 | custom fusion | bytes 3539016 | tf_op jit(solution)/shard_map/while/body/eval_jaxpr/gather | solution.py:64
  169.8 7.5 %fusion.37 = (f32[384]{0:T(512)S(1)}, bf16[384,6912]{1,0:T(8,128)(2,1)}) fusion(bf16[6912,128]{1,0:T(8,128)(2,1)} %bitcast.100, bf16[6,384,128]{2,1,0:T(8,128)(2,1)} %copy-done.3, s32[]{:T(128)} %get-tuple-element.191, pred[6912]{0:T(1024)(128)(4,1)S(1)} %broadcast_in_dim.56), kind=kOutput, calls=%fused_computation.30.clone.1 | convolution fusion | flops 695402112 | bytes 7185152 | tf_op jit(solution)/shard_map/while/body/eval_jaxpr/while/body/eval_jaxpr/dot_general | solution.py:31
  177.4 2.2 gather_fusion
  179.6 5.3 %fusion.38 = bf16[6,1,384,128]{3,2,1,0:T(8,128)(2,1)} fusion(bf16[6,1,384,128]{3,2,1,0:T(8,128)(2,1)} %get-tuple-element.192, s32[]{:T(128)} %get-tuple-element.191, bf16[6912,128]{1,0:T(8,128)(2,1)} %bitcast.101, bf16[384,6912]{1,0:T(8,128)(2,1)} %get-tuple-element.181, f32[384]{0:T(512)S(1)} %get-tuple-element.182), kind=kOutput, calls=%fused_computation.8.clone.1 | convolution fusion | flops 679575552 | bytes 7178240 | tf_op jit(solution)/shard_map/while/body/eval_jaxpr/while/body/eval_jaxpr/dot_general | solution.py:77
  184.9 3.9 %gather_fusion.1 = bf16[18,384,128]{2,1,0:T(8,128)(2,1)} fusion(bf16[18,384,128]{2,1,0:T(8,128)(2,1)} %bitcast.99, s32[1024]{0:T(1024)S(1)} %pad_clamp_fusion.2), kind=kCustom, calls=%fused_computation.clone.1 | custom fusion | bytes 3539016 | tf_op jit(solution)/shard_map/while/body/eval_jaxpr/gather | solution.py:64
  190.1 7.5 %fusion.37 = (f32[384]{0:T(512)S(1)}, bf16[384,6912]{1,0:T(8,128)(2,1)}) fusion(bf16[6912,128]{1,0:T(8,128)(2,1)} %bitcast.100, bf16[6,384,128]{2,1,0:T(8,128)(2,1)} %copy-done.3, s32[]{:T(128)} %get-tuple-element.191, pred[6912]{0:T(1024)(128)(4,1)S(1)} %broadcast_in_dim.56), kind=kOutput, calls=%fused_computation.30.clone.1 | convolution fusion | flops 695402112 | bytes 7185152 | tf_op jit(solution)/shard_map/while/body/eval_jaxpr/while/body/eval_jaxpr/dot_general | solution.py:31
  197.7 2.2 gather_fusion
  199.9 5.3 %fusion.38 = bf16[6,1,384,128]{3,2,1,0:T(8,128)(2,1)} fusion(bf16[6,1,384,128]{3,2,1,0:T(8,128)(2,1)} %get-tuple-element.192, s32[]{:T(128)} %get-tuple-element.191, bf16[6912,128]{1,0:T(8,128)(2,1)} %bitcast.101, bf16[384,6912]{1,0:T(8,128)(2,1)} %get-tuple-element.181, f32[384]{0:T(512)S(1)} %get-tuple-element.182), kind=kOutput, calls=%fused_computation.8.clone.1 | convolution fusion | flops 679575552 | bytes 7178240 | tf_op jit(solution)/shard_map/while/body/eval_jaxpr/while/body/eval_jaxpr/dot_general | solution.py:77
  205.2 3.9 %gather_fusion.1 = bf16[18,384,128]{2,1,0:T(8,128)(2,1)} fusion(bf16[18,384,128]{2,1,0:T(8,128)(2,1)} %bitcast.99, s32[1024]{0:T(1024)S(1)} %pad_clamp_fusion.2), kind=kCustom, calls=%fused_computation.clone.1 | custom fusion | bytes 3539016 | tf_op jit(solution)/shard_map/while/body/eval_jaxpr/gather | solution.py:64
  210.5 7.5 %fusion.37 = (f32[384]{0:T(512)S(1)}, bf16[384,6912]{1,0:T(8,128)(2,1)}) fusion(bf16[6912,128]{1,0:T(8,128)(2,1)} %bitcast.100, bf16[6,384,128]{2,1,0:T(8,128)(2,1)} %copy-done.3, s32[]{:T(128)} %get-tuple-element.191, pred[6912]{0:T(1024)(128)(4,1)S(1)} %broadcast_in_dim.56), kind=kOutput, calls=%fused_computation.30.clone.1 | convolution fusion | flops 695402112 | bytes 7185152 | tf_op jit(solution)/shard_map/while/body/eval_jaxpr/while/body/eval_jaxpr/dot_general | solution.py:31
  218.0 2.2 gather_fusion
  220.2 5.3 %fusion.38 = bf16[6,1,384,128]{3,2,1,0:T(8,128)(2,1)} fusion(bf16[6,1,384,128]{3,2,1,0:T(8,128)(2,1)} %get-tuple-element.192, s32[]{:T(128)} %get-tuple-element.191, bf16[6912,128]{1,0:T(8,128)(2,1)} %bitcast.101, bf16[384,6912]{1,0:T(8,128)(2,1)} %get-tuple-element.181, f32[384]{0:T(512)S(1)} %get-tuple-element.182), kind=kOutput, calls=%fused_computation.8.clone.1 | convolution fusion | flops 679575552 | bytes 7178240 | tf_op jit(solution)/shard_map/while/body/eval_jaxpr/while/body/eval_jaxpr/dot_general | solution.py:77
  225.5 3.9 %gather_fusion.1 = bf16[18,384,128]{2,1,0:T(8,128)(2,1)} fusion(bf16[18,384,128]{2,1,0:T(8,128)(2,1)} %bitcast.99, s32[1024]{0:T(1024)S(1)} %pad_clamp_fusion.2), kind=kCustom, calls=%fused_computation.clone.1 | custom fusion | bytes 3539016 | tf_op jit(solution)/shard_map/while/body/eval_jaxpr/gather | solution.py:64
  230.8 7.5 %fusion.37 = (f32[384]{0:T(512)S(1)}, bf16[384,6912]{1,0:T(8,128)(2,1)}) fusion(bf16[6912,128]{1,0:T(8,128)(2,1)} %bitcast.100, bf16[6,384,128]{2,1,0:T(8,128)(2,1)} %copy-done.3, s32[]{:T(128)} %get-tuple-element.191, pred[6912]{0:T(1024)(128)(4,1)S(1)} %broadcast_in_dim.56), kind=kOutput, calls=%fused_computation.30.clone.1 | convolution fusion | flops 695402112 | bytes 7185152 | tf_op jit(solution)/shard_map/while/body/eval_jaxpr/while/body/eval_jaxpr/dot_general | solution.py:31
  238.3 2.2 gather_fusion
  240.6 5.3 %fusion.38 = bf16[6,1,384,128]{3,2,1,0:T(8,128)(2,1)} fusion(bf16[6,1,384,128]{3,2,1,0:T(8,128)(2,1)} %get-tuple-element.192, s32[]{:T(128)} %get-tuple-element.191, bf16[6912,128]{1,0:T(8,128)(2,1)} %bitcast.101, bf16[384,6912]{1,0:T(8,128)(2,1)} %get-tuple-element.181, f32[384]{0:T(512)S(1)} %get-tuple-element.182), kind=kOutput, calls=%fused_computation.8.clone.1 | convolution fusion | flops 679575552 | bytes 7178240 | tf_op jit(solution)/shard_map/while/body/eval_jaxpr/while/body/eval_jaxpr/dot_general | solution.py:77
  245.8 15.0 %all_to_all.92 = bf16[16,144,128]{2,1,0:T(8,128)(2,1)S(1)} all-to-all(bf16[16,144,128]{2,1,0:T(8,128)(2,1)} %bitcast.107), channel_id=1, replica_groups=mesh['patch'=8,'seq'=16,'cfg'=2] {'seq'}, dimensions={0} | all-to-all | bytes 1179648 | tf_op jit(solution)/shard_map/all_to_all | solution.py:86
  260.9 0.9 copy_bitcast_fusion
  (72 shorter events, 7.6 us)
Async XLA Ops:
  0.0 49.3 %copy-start = (bf16[144,2048]{1,0:T(8,128)(2,1)S(1)}, bf16[144,2048]{1,0:T(8,128)(2,1)}, u32[]{:S(2)}) copy-start(bf16[144,2048]{1,0:T(8,128)(2,1)} %param.11) | copy-start | bytes 1769476
  47.2 6.6 %copy-start.1 = (bf16[144,2048]{1,0:T(8,128)(2,1)S(1)}, bf16[144,2048]{1,0:T(8,128)(2,1)}, u32[]{:S(2)}) copy-start(bf16[144,2048]{1,0:T(8,128)(2,1)} %param.10) | copy-start | bytes 1769476
  47.2 13.3 %copy-start.5 = (s32[6,18]{1,0:T(8,128)S(1)}, s32[6,18]{1,0:T(8,128)}, u32[]{:S(2)}) copy-start(s32[6,18]{1,0:T(8,128)} %param.14) | copy-start | bytes 1300
  47.3 13.3 %copy-start.2 = (bf16[144,2048]{1,0:T(8,128)(2,1)S(1)}, bf16[144,2048]{1,0:T(8,128)(2,1)}, u32[]{:S(2)}) copy-start(bf16[144,2048]{1,0:T(8,128)(2,1)} %param.9) | copy-start | bytes 1769476
  47.3 32.5 %collective-permute-start = (bf16[2,2304,128]{2,1,0:T(8,128)(2,1)S(1)}, bf16[2,2304,128]{2,1,0:T(8,128)(2,1)}, u32[]{:S(2)}, u32[]{:S(2)}) collective-permute-start(bf16[2,2304,128]{2,1,0:T(8,128)(2,1)S(1)} %bitcast.105), channel_id=1, source_target_pairs={{0,32},{32,64},{64,96},{96,128},{128,160},{160,192},{192,224},{1,3... | collective-permute-start | bytes 3538952 | tf_op jit(solution)/shard_map/ppermute | solution.py:24
  50.3 37.6 %all-to-all-start.3 = ((bf16[144,16,128]{2,0,1:T(8,128)(2,1)}), bf16[144,16,128]{2,0,1:T(8,128)(2,1)S(1)}, u32[]{:S(2)}, u32[]{:S(2)}) async-start(bf16[144,16,128]{2,0,1:T(8,128)(2,1)} %copy_bitcast_fusion.1), calls=%async_computation.3 | async-start | bytes 1179648 | tf_op jit(solution)/shard_map/all_to_all | solution.py:47
  54.8 31.9 %collective-permute-start.1 = (bf16[2,2304,128]{2,1,0:T(8,128)(2,1)S(1)}, bf16[2,2304,128]{2,1,0:T(8,128)(2,1)S(1)}, u32[]{:S(2)}, u32[]{:S(2)}) collective-permute-start(bf16[2,2304,128]{2,1,0:T(8,128)(2,1)S(1)} %bitcast.106), channel_id=1, source_target_pairs={{32,0},{64,32},{96,64},{128,96},{160,128},{192,160},{224,192},{33,... | collective-permute-start | bytes 3538952 | tf_op jit(solution)/shard_map/ppermute | solution.py:25
  87.8 20.1 %all-to-all-start.2 = ((bf16[144,16,128]{2,0,1:T(8,128)(2,1)}), bf16[144,16,128]{2,0,1:T(8,128)(2,1)S(1)}, u32[]{:S(2)}, u32[]{:S(2)}) async-start(bf16[144,16,128]{2,0,1:T(8,128)(2,1)} %copy_bitcast_fusion.2), calls=%async_computation.2 | async-start | bytes 1179648 | tf_op jit(solution)/shard_map/all_to_all | solution.py:46
  107.9 16.0 %all-to-all-start = ((bf16[144,16,128]{2,0,1:T(8,128)(2,1)}), bf16[144,16,128]{2,0,1:T(8,128)(2,1)S(1)}, u32[]{:S(2)}, u32[]{:S(2)}) async-start(bf16[144,16,128]{2,0,1:T(8,128)(2,1)} %copy_bitcast_fusion.3), calls=%async_computation | async-start | bytes 1179648 | tf_op jit(solution)/shard_map/all_to_all | solution.py:45
  111.5 12.4 %copy-start.6 = (s32[6]{0:T(128)S(1)}, s32[6]{0:T(128)}, u32[]{:S(2)}) copy-start(s32[6]{0:T(128)} %param.15) | copy-start | bytes 76
  123.9 3.9 %copy-start.3 = (bf16[6,384,128]{2,1,0:T(8,128)(2,1)}, bf16[6,384,128]{2,1,0:T(8,128)(2,1)S(1)}, u32[]{:S(2)}) copy-start(bf16[6,384,128]{2,1,0:T(8,128)(2,1)S(1)} %get-tuple-element.202) | copy-start | bytes 1769476 | tf_op jit(solution)/shard_map/while
  138.9 5.3 %copy-start.4 = (bf16[6,384,128]{2,1,0:T(8,128)(2,1)S(1)}, bf16[6,384,128]{2,1,0:T(8,128)(2,1)}, u32[]{:S(2)}) copy-start(bf16[6,384,128]{2,1,0:T(8,128)(2,1)} %copy-done.3) | copy-start | bytes 1769476 | tf_op jit(solution)/shard_map/while
  144.2 3.9 %copy-start.3 = (bf16[6,384,128]{2,1,0:T(8,128)(2,1)}, bf16[6,384,128]{2,1,0:T(8,128)(2,1)S(1)}, u32[]{:S(2)}) copy-start(bf16[6,384,128]{2,1,0:T(8,128)(2,1)S(1)} %get-tuple-element.202) | copy-start | bytes 1769476 | tf_op jit(solution)/shard_map/while
  159.2 5.3 %copy-start.4 = (bf16[6,384,128]{2,1,0:T(8,128)(2,1)S(1)}, bf16[6,384,128]{2,1,0:T(8,128)(2,1)}, u32[]{:S(2)}) copy-start(bf16[6,384,128]{2,1,0:T(8,128)(2,1)} %copy-done.3) | copy-start | bytes 1769476 | tf_op jit(solution)/shard_map/while
  164.5 3.9 %copy-start.3 = (bf16[6,384,128]{2,1,0:T(8,128)(2,1)}, bf16[6,384,128]{2,1,0:T(8,128)(2,1)S(1)}, u32[]{:S(2)}) copy-start(bf16[6,384,128]{2,1,0:T(8,128)(2,1)S(1)} %get-tuple-element.202) | copy-start | bytes 1769476 | tf_op jit(solution)/shard_map/while
  179.6 5.3 %copy-start.4 = (bf16[6,384,128]{2,1,0:T(8,128)(2,1)S(1)}, bf16[6,384,128]{2,1,0:T(8,128)(2,1)}, u32[]{:S(2)}) copy-start(bf16[6,384,128]{2,1,0:T(8,128)(2,1)} %copy-done.3) | copy-start | bytes 1769476 | tf_op jit(solution)/shard_map/while
  184.9 3.9 %copy-start.3 = (bf16[6,384,128]{2,1,0:T(8,128)(2,1)}, bf16[6,384,128]{2,1,0:T(8,128)(2,1)S(1)}, u32[]{:S(2)}) copy-start(bf16[6,384,128]{2,1,0:T(8,128)(2,1)S(1)} %get-tuple-element.202) | copy-start | bytes 1769476 | tf_op jit(solution)/shard_map/while
  199.9 5.3 %copy-start.4 = (bf16[6,384,128]{2,1,0:T(8,128)(2,1)S(1)}, bf16[6,384,128]{2,1,0:T(8,128)(2,1)}, u32[]{:S(2)}) copy-start(bf16[6,384,128]{2,1,0:T(8,128)(2,1)} %copy-done.3) | copy-start | bytes 1769476 | tf_op jit(solution)/shard_map/while
  205.2 3.9 %copy-start.3 = (bf16[6,384,128]{2,1,0:T(8,128)(2,1)}, bf16[6,384,128]{2,1,0:T(8,128)(2,1)S(1)}, u32[]{:S(2)}) copy-start(bf16[6,384,128]{2,1,0:T(8,128)(2,1)S(1)} %get-tuple-element.202) | copy-start | bytes 1769476 | tf_op jit(solution)/shard_map/while
  220.2 5.3 %copy-start.4 = (bf16[6,384,128]{2,1,0:T(8,128)(2,1)S(1)}, bf16[6,384,128]{2,1,0:T(8,128)(2,1)}, u32[]{:S(2)}) copy-start(bf16[6,384,128]{2,1,0:T(8,128)(2,1)} %copy-done.3) | copy-start | bytes 1769476 | tf_op jit(solution)/shard_map/while
  225.5 3.9 %copy-start.3 = (bf16[6,384,128]{2,1,0:T(8,128)(2,1)}, bf16[6,384,128]{2,1,0:T(8,128)(2,1)S(1)}, u32[]{:S(2)}) copy-start(bf16[6,384,128]{2,1,0:T(8,128)(2,1)S(1)} %get-tuple-element.202) | copy-start | bytes 1769476 | tf_op jit(solution)/shard_map/while
  240.5 5.3 %copy-start.4 = (bf16[6,384,128]{2,1,0:T(8,128)(2,1)S(1)}, bf16[6,384,128]{2,1,0:T(8,128)(2,1)}, u32[]{:S(2)}) copy-start(bf16[6,384,128]{2,1,0:T(8,128)(2,1)} %copy-done.3) | copy-start | bytes 1769476 | tf_op jit(solution)/shard_map/while
where the time goes:
time: 263 us; the launch traced here: 262 us
  matrix products  77.1 us (29%)
  local copies, waits for them, and re-layouts  57.4 us (22%)
  blocking collectives  50.3 us (19%)
  waiting for transfers between devices  44.5 us (17%)
  starting transfers between devices  21.8 us (8%)
  other arithmetic  10.3 us (4%)
    dot_general x6, matrix products, capped_weights(): lax.dot_general(query_rows, key_rows, (((1,), (1,)), ((), ())), preferred...  45.3 us
    all_to_all x1, blocking collectives, on_device(): lax.all_to_all(stale, 'seq', split_axis=2, concat_axis=1, tiled=True)  35.3 us
    dot_general x6, matrix products, per_head(): jnp.dot(weight.astype(jnp.bfloat16), value_rows, preferred_element_type=j...  31.8 us
    gather x6, local copies, waits for them, and re-layouts, per_tile(): keys = key_blocks[listed]  23.4 us
    ppermute x1, waiting for transfers between devices, with_halo(): before = lax.ppermute(last, axis, up)  18.2 us
    all_to_all x1, blocking collectives, on_device(): lax.all_to_all(merged, 'seq', split_axis=0, concat_axis=1, tiled=True)  15 us
    gather x6, local copies, waits for them, and re-layouts, per_tile(): values = value_blocks[listed]  13.3 us
    all_to_all x1, waiting for transfers between devices, on_device(): lax.all_to_all(fresh_key, 'seq', split_axis=1, concat_axis=0, tiled=True)  11.8 us
  transfers between devices with their start and end apart: 5, of which 4 were waited for; matrix products, arithmetic and copies ran while one was open for 4% of the time, Pallas kernels for 0%

commit v1 on v0

v1 whole, which is shorter than its diff:
```python
import functools

import jax
import jax.numpy as jnp
from jax import lax
from jax.experimental import pallas as pl
from jax.experimental.pallas import tpu as pltpu
from jax.sharding import PartitionSpec as P

NUM_HEADS = 16
HEAD_DIM = 128
TILE_TOKENS = 384
TILES_H = 2
TILES_W = 3
KEY_SLOTS = 18


soft_cap = 8.0


def with_halo(x, sides, width):
    for axis, dim in sides:
        size, length = (lax.axis_size(axis), x.shape[dim])
        up = [(i, (i + 1) % size) for i in range(size - 1)]
        down = [(j, i) for i, j in up]
        last = lax.slice_in_dim(x, length - width, length, axis=dim)
        leading = lax.slice_in_dim(x, 0, width, axis=dim)
        before = lax.ppermute(last, axis, up)
        after = lax.ppermute(leading, axis, down)
        x = jnp.concatenate([before, x, after], axis=dim)
    return x


def attention_kernel(local_heads, per_patch, ids_ref, count_ref, q_ref, kb_ref, kf_ref, ka_ref,
                     vb_ref, vf_ref, va_ref, o_ref, acc_ref, tot_ref):
    t = pl.program_id(0)
    factor = 1.0 / (HEAD_DIM**0.5) / soft_cap
    for h in range(local_heads):
        cols = slice(h * HEAD_DIM, (h + 1) * HEAD_DIM)
        query = q_ref[:, cols]
        acc_ref[...] = jnp.zeros_like(acc_ref)
        tot_ref[...] = jnp.zeros_like(tot_ref)

        def accumulate(k_ref, v_ref, row):
            start = pl.multiple_of(row * TILE_TOKENS, TILE_TOKENS)
            keys = k_ref[pl.ds(start, TILE_TOKENS), cols]
            values = v_ref[pl.ds(start, TILE_TOKENS), cols]
            scores = lax.dot_general(
                query, keys, (((1,), (1,)), ((), ())), preferred_element_type=jnp.float32
            )
            weight = jnp.exp(soft_cap * jnp.tanh(scores * factor) - soft_cap)
            part = weight[:, 0:HEAD_DIM]
            for c in range(1, TILE_TOKENS // HEAD_DIM):
                part = part + weight[:, c * HEAD_DIM:(c + 1) * HEAD_DIM]
            tot_ref[...] += part
            acc_ref[...] += jnp.dot(
                weight.astype(jnp.bfloat16), values, preferred_element_type=jnp.float32
            )

        def body(j, carry):
            u = ids_ref[t, j]
            which = u // per_patch
            row = u - which * per_patch

            @pl.when(which == 0)
            def _():
                accumulate(kb_ref, vb_ref, row)

            @pl.when(which == 1)
            def _():
                accumulate(kf_ref, vf_ref, row)

            @pl.when(which == 2)
            def _():
                accumulate(ka_ref, va_ref, row)

            return carry

        lax.fori_loop(0, count_ref[t], body, 0)
        total = jnp.sum(tot_ref[...], axis=1, keepdims=True)
        o_ref[:, cols] = (acc_ref[...] / total).astype(o_ref.dtype)


def tile_attention(q_heads, kb, kf, ka, vb, vf, va, local_ids, tile_count, local_heads, per_patch):
    rows, width = q_heads.shape
    tiles = rows // TILE_TOKENS
    whole = pl.BlockSpec((rows, width), lambda t, ids, cnt: (0, 0))
    tile = pl.BlockSpec((TILE_TOKENS, width), lambda t, ids, cnt: (t, 0))
    return pl.pallas_call(
        functools.partial(attention_kernel, local_heads, per_patch),
        out_shape=jax.ShapeDtypeStruct((rows, width), jnp.bfloat16),
        grid_spec=pltpu.PrefetchScalarGridSpec(
            num_scalar_prefetch=2,
            grid=(tiles,),
            in_specs=[tile, whole, whole, whole, whole, whole, whole],
            out_specs=tile,
            scratch_shapes=[
                pltpu.VMEM((TILE_TOKENS, HEAD_DIM), jnp.float32),
                pltpu.VMEM((TILE_TOKENS, HEAD_DIM), jnp.float32),
            ],
        ),
    )(local_ids, tile_count, q_heads, kb, kf, ka, vb, vf, va)


def on_device(query, fresh_key, fresh_value, stale_key, stale_value, key_tiles, tile_count):
    seq_count = lax.axis_size("seq")
    local_heads = NUM_HEADS // seq_count
    per_patch = TILES_H * TILES_W
    rows = query.shape[0]
    patch_rows = rows * seq_count
    q_heads, k_fresh, v_fresh = (
        lax.all_to_all(query, "seq", split_axis=1, concat_axis=0, tiled=True),
        lax.all_to_all(fresh_key, "seq", split_axis=1, concat_axis=0, tiled=True),
        lax.all_to_all(fresh_value, "seq", split_axis=1, concat_axis=0, tiled=True),
    )
    stale = jnp.stack([stale_key, stale_value])
    regrouped = lax.all_to_all(stale, "seq", split_axis=2, concat_axis=1, tiled=True)
    framed = with_halo(regrouped, (("patch", 1),), patch_rows)
    before = framed[:, :patch_rows]
    after = framed[:, 2 * patch_rows :]
    first_tile = (lax.axis_index("patch") - 1) * per_patch
    local_ids = (key_tiles - first_tile).astype(jnp.int32)
    merged = tile_attention(
        q_heads, before[0], k_fresh, after[0], before[1], v_fresh, after[1],
        local_ids, tile_count.astype(jnp.int32), local_heads, per_patch,
    )
    return lax.all_to_all(merged, "seq", split_axis=0, concat_axis=1, tiled=True)


def solution(mesh):
    return jax.shard_map(
        on_device,
        mesh=mesh,
        in_specs=(
            P(("cfg", "patch", "seq"), None),
            P(("cfg", "patch", "seq"), None),
            P(("cfg", "patch", "seq"), None),
            P(("cfg", "patch", "seq"), None),
            P(("cfg", "patch", "seq"), None),
            P("patch", None),
            P("patch"),
        ),
        out_specs=P(("cfg", "patch", "seq"), None),
        check_vma=False,
    )
```

time: 263 us -> 153 us (0.58)
  the two profiles are of different devices: /device:TPU:128 before, /device:TPU:64 now
where the time goes in v1:
time: 153 us; the launch traced here: 152 us
  blocking collectives  51.2 us (33%)
  Pallas kernels  35 us (23%)
  waiting for transfers between devices  28.6 us (19%)
  local copies, waits for them, and re-layouts  18.6 us (12%)
  starting transfers between devices  15.3 us (10%)
  other arithmetic  3.04 us (2%)
    all_to_all x1, blocking collectives, on_device(): lax.all_to_all(stale, 'seq', split_axis=2, concat_axis=1, tiled=True)  35.3 us
    pallas_call x1, Pallas kernels, tile_attention(): pl.pallas_call(functools.partial(attention_kernel, local_heads, per_patch...  35 us
    all_to_all x1, blocking collectives, on_device(): lax.all_to_all(merged, 'seq', split_axis=0, concat_axis=1, tiled=True)  15.9 us
    all_to_all x1, waiting for transfers between devices, on_device(): lax.all_to_all(fresh_key, 'seq', split_axis=1, concat_axis=0, tiled=True)  10.6 us
    all_to_all x1, waiting for transfers between devices, on_device(): lax.all_to_all(query, 'seq', split_axis=1, concat_axis=0, tiled=True)  8.27 us
    ppermute x1, waiting for transfers between devices, with_halo(): after = lax.ppermute(leading, axis, down)  4.95 us
    all_to_all x1, local copies, waits for them, and re-layouts, on_device(): lax.all_to_all(stale, 'seq', split_axis=2, concat_axis=1, tiled=True)  4.81 us
    all_to_all x1, waiting for transfers between devices, on_device(): lax.all_to_all(fresh_value, 'seq', split_axis=1, concat_axis=0, tiled=True)  4.77 us
  transfers between devices with their start and end apart: 5, of which 4 were waited for; matrix products, arithmetic and copies ran while one was open for 5% of the time, Pallas kernels for 0%

profile of v1, /device:TPU:64, one launch (start us, length us, event | category | flops | bytes accessed | tf_op | source)
XLA Modules:
  0.0 151.9 jit_solution(7050721230436735736)
XLA Ops:
  0.0 0.0 copy-start
  0.0 2.4 %pad_maximum_fusion = bf16[2,144,2048]{2,1,0:T(8,128)(2,1)} fusion(bf16[1,144,2048]{2,1,0:T(8,128)(2,1)} %bitcast.52, bf16[1,144,2048]{2,1,0:T(8,128)(2,1)} %bitcast.53), kind=kLoop, calls=%fused_computation | loop fusion | flops 589824 | bytes 2359296 | tf_op jit(solution)/shard_map/stack | solution.py:116
  2.4 4.6 %copy.21 = bf16[2,144,2048]{1,0,2:T(2,128)(2,1)S(1)} copy(bf16[2,144,2048]{2,1,0:T(8,128)(2,1)} %pad_maximum_fusion) | data formatting | bytes 2359296 | tf_op jit(solution)/shard_map/stack | solution.py:116
  7.1 35.3 %all_to_all.94 = bf16[2,144,2048]{1,0,2:T(2,128)(2,1)} all-to-all(bf16[2,144,2048]{1,0,2:T(2,128)(2,1)S(1)} %copy.21), channel_id=1, replica_groups=mesh['patch'=8,'seq'=16,'cfg'=2] {'seq'}, dimensions={2} | all-to-all | bytes 2359296 | tf_op jit(solution)/shard_map/all_to_all | solution.py:117
  42.4 4.8 %copy.22 = bf16[2,144,16,128]{3,1,2,0:T(8,128)(2,1)S(1)} copy(bf16[2,144,16,128]{1,0,3,2:T(2,128)(2,1)} %bitcast.45) | data formatting | bytes 2359296 | tf_op jit(solution)/shard_map/all_to_all | solution.py:117
  47.2 0.0 copy-start.4
  47.2 2.1 %collective-permute-start.1 = (bf16[2,2304,128]{2,1,0:T(8,128)(2,1)S(1)}, bf16[2,2304,128]{2,1,0:T(8,128)(2,1)}, u32[]{:S(2)}, u32[]{:S(2)}) collective-permute-start(bf16[2,2304,128]{2,1,0:T(8,128)(2,1)S(1)} %bitcast.50), channel_id=1, source_target_pairs={{32,0},{64,32},{96,64},{128,96},{160,128},{192,160},{224,192},{33,... | collective-permute-start | bytes 3538952 | tf_op jit(solution)/shard_map/ppermute | solution.py:29
  49.3 0.0 copy-done
  49.3 0.9 copy_bitcast_fusion.3
  50.2 0.0 copy-start.6
  50.2 0.0 copy-start.5
  50.2 3.7 %all-to-all-start = ((bf16[144,16,128]{2,0,1:T(8,128)(2,1)}), bf16[144,16,128]{2,0,1:T(8,128)(2,1)S(1)}, u32[]{:S(2)}, u32[]{:S(2)}) async-start(bf16[144,16,128]{2,0,1:T(8,128)(2,1)} %copy_bitcast_fusion.3), calls=%async_computation | async-start | bytes 1179648 | tf_op jit(solution)/shard_map/all_to_all | solution.py:112
  54.0 0.0 copy-done.4
  54.0 0.9 copy_bitcast_fusion.1
  54.9 2.4 %collective-permute-start = (bf16[2,2304,128]{2,1,0:T(8,128)(2,1)S(1)}, bf16[2,2304,128]{2,1,0:T(8,128)(2,1)}, u32[]{:S(2)}, u32[]{:S(2)}) collective-permute-start(bf16[2,2304,128]{2,1,0:T(8,128)(2,1)S(1)} %bitcast.51), channel_id=1, source_target_pairs={{0,32},{32,64},{64,96},{96,128},{128,160},{160,192},{192,224},{1,3... | collective-permute-start | bytes 3538952 | tf_op jit(solution)/shard_map/ppermute | solution.py:28
  57.3 0.0 copy-done.6
  57.3 0.6 broadcast_subtract_fusion.ids_ref
  57.9 0.0 copy-done.5
  57.9 0.9 copy_bitcast_fusion.2
  58.8 8.3 %all-to-all-done = bf16[144,16,128]{2,0,1:T(8,128)(2,1)S(1)} async-done(((bf16[144,16,128]{2,0,1:T(8,128)(2,1)}), bf16[144,16,128]{2,0,1:T(8,128)(2,1)S(1)}, u32[]{:S(2)}, u32[]{:S(2)}) %all-to-all-start) | async-done | bytes 589856 | tf_op jit(solution)/shard_map/all_to_all | solution.py:112
  67.1 0.0 copy-start.1
  67.1 3.6 %all-to-all-start.3 = ((bf16[144,16,128]{2,0,1:T(8,128)(2,1)}), bf16[144,16,128]{2,0,1:T(8,128)(2,1)S(1)}, u32[]{:S(2)}, u32[]{:S(2)}) async-start(bf16[144,16,128]{2,0,1:T(8,128)(2,1)} %copy_bitcast_fusion.1), calls=%async_computation.3 | async-start | bytes 1179648 | tf_op jit(solution)/shard_map/all_to_all | solution.py:114
  70.7 5.0 %collective-permute-done.1 = bf16[2,2304,128]{2,1,0:T(8,128)(2,1)} collective-permute-done((bf16[2,2304,128]{2,1,0:T(8,128)(2,1)S(1)}, bf16[2,2304,128]{2,1,0:T(8,128)(2,1)}, u32[]{:S(2)}, u32[]{:S(2)}) %collective-permute-start.1) | collective-permute-done | bytes 1179680 | tf_op jit(solution)/shard_map/ppermute | solution.py:29
  75.6 2.3 %slice_bitcast_fusion = (bf16[2304,128]{1,0:T(8,128)(2,1)}, bf16[2304,128]{1,0:T(8,128)(2,1)}) fusion(bf16[2,2304,128]{2,1,0:T(8,128)(2,1)} %collective-permute-done.1), kind=kLoop, calls=%fused_computation.5 | loop fusion | bytes 2359296 | tf_op jit(solution)/shard_map/squeeze | solution.py:124
  78.0 0.0 copy-done.1
  78.0 4.8 %all-to-all-done.3 = bf16[144,16,128]{2,0,1:T(8,128)(2,1)S(1)} async-done(((bf16[144,16,128]{2,0,1:T(8,128)(2,1)}), bf16[144,16,128]{2,0,1:T(8,128)(2,1)S(1)}, u32[]{:S(2)}, u32[]{:S(2)}) %all-to-all-start.3) | async-done | bytes 589856 | tf_op jit(solution)/shard_map/all_to_all | solution.py:114
  82.8 0.0 copy-start.2
  82.8 3.6 %all-to-all-start.2 = ((bf16[144,16,128]{2,0,1:T(8,128)(2,1)}), bf16[144,16,128]{2,0,1:T(8,128)(2,1)S(1)}, u32[]{:S(2)}, u32[]{:S(2)}) async-start(bf16[144,16,128]{2,0,1:T(8,128)(2,1)} %copy_bitcast_fusion.2), calls=%async_computation.2 | async-start | bytes 1179648 | tf_op jit(solution)/shard_map/all_to_all | solution.py:113
  86.3 0.0 collective-permute-done
  86.4 2.3 %slice_bitcast_fusion.1 = (bf16[2304,128]{1,0:T(8,128)(2,1)}, bf16[2304,128]{1,0:T(8,128)(2,1)}) fusion(bf16[2,2304,128]{2,1,0:T(8,128)(2,1)} %collective-permute-done), kind=kLoop, calls=%fused_computation.6 | loop fusion | bytes 2359296 | tf_op jit(solution)/shard_map/squeeze | solution.py:124
  88.7 0.0 copy-done.2
  88.7 10.6 %all-to-all-done.2 = bf16[144,16,128]{2,0,1:T(8,128)(2,1)S(1)} async-done(((bf16[144,16,128]{2,0,1:T(8,128)(2,1)}), bf16[144,16,128]{2,0,1:T(8,128)(2,1)S(1)}, u32[]{:S(2)}, u32[]{:S(2)}) %all-to-all-start.2) | async-done | bytes 589856 | tf_op jit(solution)/shard_map/all_to_all | solution.py:113
  99.3 0.0 copy-start.3
  99.3 0.8 copy-done.3
  100.1 35.0 %shard_map.73 = bf16[2304,128]{1,0:T(8,128)(2,1)} custom-call(s32[6,18]{1,0:T(8,128)} %broadcast_subtract_fusion.ids_ref, s32[6]{0:T(128)} %count_ref.1, bf16[2304,128]{1,0:T(8,128)(2,1)} %bitcast.46, bf16[2304,128]{1,0:T(8,128)(2,1)} %get-tuple-element.8.kb_ref, bf16[2304,128]{1,0:T(8,128)(2,1)} %bitcast.48, bf16[2304,128]{1,0:T(8,128)(2,1)} %get-tuple-element.6.ka_ref, ...), custom_call_target="tpu_custom_call" | custom-call | tf_op jit(solution)/shard_map/pallas_call | solution.py:89
  135.1 15.9 %all_to_all.95 = bf16[16,144,128]{2,1,0:T(8,128)(2,1)S(1)} all-to-all(bf16[16,144,128]{2,1,0:T(8,128)(2,1)} %bitcast.49), channel_id=1, replica_groups=mesh['patch'=8,'seq'=16,'cfg'=2] {'seq'}, dimensions={0} | all-to-all | bytes 1179648 | tf_op jit(solution)/shard_map/all_to_all | solution.py:127
  151.1 0.9 copy_bitcast_fusion
Async XLA Ops:
  0.0 49.3 %copy-start = (bf16[144,2048]{1,0:T(8,128)(2,1)S(1)}, bf16[144,2048]{1,0:T(8,128)(2,1)}, u32[]{:S(2)}) copy-start(bf16[144,2048]{1,0:T(8,128)(2,1)} %param.7) | copy-start | bytes 1769476
  47.2 6.7 %copy-start.4 = (bf16[144,2048]{1,0:T(8,128)(2,1)S(1)}, bf16[144,2048]{1,0:T(8,128)(2,1)}, u32[]{:S(2)}) copy-start(bf16[144,2048]{1,0:T(8,128)(2,1)} %param.9) | copy-start | bytes 1769476
  47.2 28.4 %collective-permute-start.1 = (bf16[2,2304,128]{2,1,0:T(8,128)(2,1)S(1)}, bf16[2,2304,128]{2,1,0:T(8,128)(2,1)}, u32[]{:S(2)}, u32[]{:S(2)}) collective-permute-start(bf16[2,2304,128]{2,1,0:T(8,128)(2,1)S(1)} %bitcast.50), channel_id=1, source_target_pairs={{32,0},{64,32},{96,64},{128,96},{160,128},{192,160},{224,192},{33,... | collective-permute-start | bytes 3538952 | tf_op jit(solution)/shard_map/ppermute | solution.py:29
  50.2 7.1 %copy-start.6 = (s32[6,18]{1,0:T(8,128)S(1)}, s32[6,18]{1,0:T(8,128)}, u32[]{:S(2)}) copy-start(s32[6,18]{1,0:T(8,128)} %param.12) | copy-start | bytes 1300
  50.2 7.7 %copy-start.5 = (bf16[144,2048]{1,0:T(8,128)(2,1)S(1)}, bf16[144,2048]{1,0:T(8,128)(2,1)}, u32[]{:S(2)}) copy-start(bf16[144,2048]{1,0:T(8,128)(2,1)} %param.8) | copy-start | bytes 1769476
  50.2 16.9 %all-to-all-start = ((bf16[144,16,128]{2,0,1:T(8,128)(2,1)}), bf16[144,16,128]{2,0,1:T(8,128)(2,1)S(1)}, u32[]{:S(2)}, u32[]{:S(2)}) async-start(bf16[144,16,128]{2,0,1:T(8,128)(2,1)} %copy_bitcast_fusion.3), calls=%async_computation | async-start | bytes 1179648 | tf_op jit(solution)/shard_map/all_to_all | solution.py:112
  54.9 31.5 %collective-permute-start = (bf16[2,2304,128]{2,1,0:T(8,128)(2,1)S(1)}, bf16[2,2304,128]{2,1,0:T(8,128)(2,1)}, u32[]{:S(2)}, u32[]{:S(2)}) collective-permute-start(bf16[2,2304,128]{2,1,0:T(8,128)(2,1)S(1)} %bitcast.51), channel_id=1, source_target_pairs={{0,32},{32,64},{64,96},{96,128},{128,160},{160,192},{192,224},{1,3... | collective-permute-start | bytes 3538952 | tf_op jit(solution)/shard_map/ppermute | solution.py:28
  67.1 10.9 %copy-start.1 = (bf16[144,16,128]{2,0,1:T(8,128)(2,1)}, bf16[144,16,128]{2,0,1:T(8,128)(2,1)S(1)}, u32[]{:S(2)}) copy-start(bf16[144,16,128]{2,0,1:T(8,128)(2,1)S(1)} %all-to-all-done) | copy-start | bytes 1769476
  67.1 15.7 %all-to-all-start.3 = ((bf16[144,16,128]{2,0,1:T(8,128)(2,1)}), bf16[144,16,128]{2,0,1:T(8,128)(2,1)S(1)}, u32[]{:S(2)}, u32[]{:S(2)}) async-start(bf16[144,16,128]{2,0,1:T(8,128)(2,1)} %copy_bitcast_fusion.1), calls=%async_computation.3 | async-start | bytes 1179648 | tf_op jit(solution)/shard_map/all_to_all | solution.py:114
  82.8 6.0 %copy-start.2 = (bf16[144,16,128]{2,0,1:T(8,128)(2,1)}, bf16[144,16,128]{2,0,1:T(8,128)(2,1)S(1)}, u32[]{:S(2)}) copy-start(bf16[144,16,128]{2,0,1:T(8,128)(2,1)S(1)} %all-to-all-done.3) | copy-start | bytes 1769476
  82.8 16.5 %all-to-all-start.2 = ((bf16[144,16,128]{2,0,1:T(8,128)(2,1)}), bf16[144,16,128]{2,0,1:T(8,128)(2,1)S(1)}, u32[]{:S(2)}, u32[]{:S(2)}) async-start(bf16[144,16,128]{2,0,1:T(8,128)(2,1)} %copy_bitcast_fusion.2), calls=%async_computation.2 | async-start | bytes 1179648 | tf_op jit(solution)/shard_map/all_to_all | solution.py:113
  99.3 0.8 copy-start.3

commit v2 on v1

v2 whole, which is shorter than its diff:
```python
import functools

import jax
import jax.numpy as jnp
from jax import lax
from jax.experimental import pallas as pl
from jax.experimental.pallas import tpu as pltpu
from jax.sharding import PartitionSpec as P

NUM_HEADS = 16
HEAD_DIM = 128
TILE_TOKENS = 384
TILES_H = 2
TILES_W = 3
KEY_SLOTS = 18


soft_cap = 8.0


def with_halo(x, sides, width):
    for axis, dim in sides:
        size, length = (lax.axis_size(axis), x.shape[dim])
        up = [(i, (i + 1) % size) for i in range(size - 1)]
        down = [(j, i) for i, j in up]
        last = lax.slice_in_dim(x, length - width, length, axis=dim)
        leading = lax.slice_in_dim(x, 0, width, axis=dim)
        before = lax.ppermute(last, axis, up)
        after = lax.ppermute(leading, axis, down)
        x = jnp.concatenate([before, x, after], axis=dim)
    return x


def attention_kernel(local_heads, per_patch, ids_ref, count_ref, fresh_ref, before_ref, after_ref,
                     o_ref, acc_ref, tot_ref):
    t = pl.program_id(0)
    width = local_heads * HEAD_DIM
    factor = 1.0 / (HEAD_DIM**0.5) / soft_cap
    for h in range(local_heads):
        q_cols = pl.ds(2 * width + h * HEAD_DIM, HEAD_DIM)
        start_q = pl.multiple_of(t * TILE_TOKENS, TILE_TOKENS)
        query = fresh_ref[pl.ds(start_q, TILE_TOKENS), q_cols]
        acc_ref[...] = jnp.zeros_like(acc_ref)
        tot_ref[...] = jnp.zeros_like(tot_ref)

        def accumulate(ref, k_col, v_col, row):
            start = pl.multiple_of(row * TILE_TOKENS, TILE_TOKENS)
            keys = ref[pl.ds(start, TILE_TOKENS), pl.ds(k_col, HEAD_DIM)]
            values = ref[pl.ds(start, TILE_TOKENS), pl.ds(v_col, HEAD_DIM)]
            scores = lax.dot_general(
                query, keys, (((1,), (1,)), ((), ())), preferred_element_type=jnp.float32
            )
            weight = jnp.exp(soft_cap * jnp.tanh(scores * factor) - soft_cap)
            part = weight[:, 0:HEAD_DIM]
            for c in range(1, TILE_TOKENS // HEAD_DIM):
                part = part + weight[:, c * HEAD_DIM:(c + 1) * HEAD_DIM]
            tot_ref[...] += part
            acc_ref[...] += jnp.dot(
                weight.astype(jnp.bfloat16), values, preferred_element_type=jnp.float32
            )

        def body(j, carry):
            u = ids_ref[t, j]
            which = u // per_patch
            row = u - which * per_patch
            stale_k, stale_v = h * HEAD_DIM, width + h * HEAD_DIM

            @pl.when(which == 0)
            def _():
                accumulate(before_ref, stale_k, stale_v, row)

            @pl.when(which == 1)
            def _():
                accumulate(fresh_ref, 3 * width + h * HEAD_DIM, 4 * width + h * HEAD_DIM, row)

            @pl.when(which == 2)
            def _():
                accumulate(after_ref, stale_k, stale_v, row)

            return carry

        lax.fori_loop(0, count_ref[t], body, 0)
        total = jnp.sum(tot_ref[...], axis=1, keepdims=True)
        o_ref[:, pl.ds(h * HEAD_DIM, HEAD_DIM)] = (acc_ref[...] / total).astype(o_ref.dtype)


def tile_attention(fresh, before, after, local_ids, tile_count, local_heads, per_patch):
    rows = fresh.shape[0]
    width = local_heads * HEAD_DIM
    tiles = rows // TILE_TOKENS

    def whole(array):
        return pl.BlockSpec(array.shape, lambda t, ids, cnt: (0, 0))

    return pl.pallas_call(
        functools.partial(attention_kernel, local_heads, per_patch),
        out_shape=jax.ShapeDtypeStruct((rows, width), jnp.bfloat16),
        grid_spec=pltpu.PrefetchScalarGridSpec(
            num_scalar_prefetch=2,
            grid=(tiles,),
            in_specs=[whole(fresh), whole(before), whole(after)],
            out_specs=pl.BlockSpec((TILE_TOKENS, width), lambda t, ids, cnt: (t, 0)),
            scratch_shapes=[
                pltpu.VMEM((TILE_TOKENS, HEAD_DIM), jnp.float32),
                pltpu.VMEM((TILE_TOKENS, HEAD_DIM), jnp.float32),
            ],
        ),
    )(local_ids, tile_count, fresh, before, after)


def on_device(query, fresh_key, fresh_value, stale_key, stale_value, key_tiles, tile_count):
    seq_count = lax.axis_size("seq")
    local_heads = NUM_HEADS // seq_count
    width = local_heads * HEAD_DIM
    per_patch = TILES_H * TILES_W
    rows = query.shape[0]
    patch_rows = rows * seq_count
    stacked = jnp.stack([stale_key, stale_value, query, fresh_key, fresh_value], axis=1)
    stacked = stacked.reshape(rows, 5, seq_count, width)
    regrouped = lax.all_to_all(stacked, "seq", split_axis=2, concat_axis=0, tiled=True)
    fresh = regrouped.reshape(patch_rows, 5 * width)
    stale = fresh[:, : 2 * width]
    framed = with_halo(stale, (("patch", 0),), patch_rows)
    before = framed[:patch_rows]
    after = framed[2 * patch_rows :]
    first_tile = (lax.axis_index("patch") - 1) * per_patch
    local_ids = (key_tiles - first_tile).astype(jnp.int32)
    merged = tile_attention(
        fresh, before, after, local_ids, tile_count.astype(jnp.int32), local_heads, per_patch
    )
    return lax.all_to_all(merged, "seq", split_axis=0, concat_axis=1, tiled=True)


def solution(mesh):
    return jax.shard_map(
        on_device,
        mesh=mesh,
        in_specs=(
            P(("cfg", "patch", "seq"), None),
            P(("cfg", "patch", "seq"), None),
            P(("cfg", "patch", "seq"), None),
            P(("cfg", "patch", "seq"), None),
            P(("cfg", "patch", "seq"), None),
            P("patch", None),
            P("patch"),
        ),
        out_specs=P(("cfg", "patch", "seq"), None),
        check_vma=False,
    )
```

time: 153 us -> 142 us (0.928)
  the two profiles are of different devices: /device:TPU:64 before, /device:TPU:1 now
where the time goes in v2:
time: 142 us; the launch traced here: 143 us
  blocking collectives  56.9 us (40%)
  Pallas kernels  39.6 us (28%)
  waiting for transfers between devices  28.9 us (20%)
  starting transfers between devices  8.52 us (6%)
  local copies, waits for them, and re-layouts  8.33 us (6%)
    all_to_all x1, blocking collectives, on_device(): lax.all_to_all(stacked, 'seq', split_axis=2, concat_axis=0, tiled=True)  44 us
    pallas_call x1, Pallas kernels, tile_attention(): pl.pallas_call(functools.partial(attention_kernel, local_heads, per_patch...  39.6 us
    ppermute x1, waiting for transfers between devices, with_halo(): after = lax.ppermute(leading, axis, down)  17.9 us
    all_to_all x1, blocking collectives, on_device(): lax.all_to_all(merged, 'seq', split_axis=0, concat_axis=1, tiled=True)  12.9 us
    ppermute x1, waiting for transfers between devices, with_halo(): before = lax.ppermute(last, axis, up)  11 us
    ppermute x1, starting transfers between devices, with_halo(): before = lax.ppermute(last, axis, up)  6.6 us
    unnamed x20, local copies, waits for them, and re-layouts  4.1 us
  transfers between devices with their start and end apart: 2, of which 2 were waited for; matrix products, arithmetic and copies ran while one was open for 0% of the time, Pallas kernels for 0%

profile of v2, /device:TPU:1, one launch (start us, length us, event | category | flops | bytes accessed | tf_op | source)
XLA Modules:
  0.0 143.0 jit_solution(3467986675367237972)
XLA Ops:
  0.0 0.0 copy-start.1
  0.0 0.0 copy-start.2
  0.0 0.0 copy-start.3
  0.0 1.3 copy.26
  1.3 0.1 constant_dynamic-update-slice_fusion.4
  1.4 1.2 copy.27
  2.6 0.0 copy-done.1
  2.6 0.1 copy.28
  2.7 0.0 copy-done.2
  2.8 0.1 copy.29
  2.9 0.0 copy-done.3
  2.9 0.1 copy.30
  3.0 0.1 constant_dynamic-update-slice_fusion.3
  3.1 0.1 constant_dynamic-update-slice_fusion.2
  3.3 0.1 constant_dynamic-update-slice_fusion.1
  3.4 0.1 constant_dynamic-update-slice_fusion
  3.6 0.8 copy.22
  4.4 44.0 %all_to_all.34 = bf16[144,5,16,128]{3,0,1,2:T(8,128)(2,1)S(1)} all-to-all(bf16[144,5,16,128]{3,0,1,2:T(8,128)(2,1)S(1)} %copy.22), channel_id=1, replica_groups=mesh['patch'=8,'seq'=16,'cfg'=2] {'seq'}, dimensions={2} | all-to-all | bytes 5898240 | tf_op jit(solution)/shard_map/all_to_all | solution.py:120
  48.4 1.2 copy.23
  49.6 0.0 copy-start.4
  49.6 0.7 copy.34
  50.4 0.0 copy-start
  50.4 1.2 slice.4
  51.6 6.6 %collective-permute-start = (bf16[2304,256]{1,0:T(8,128)(2,1)}, bf16[2304,256]{1,0:T(8,128)(2,1)}, u32[]{:S(2)}, u32[]{:S(2)}) collective-permute-start(bf16[2304,256]{1,0:T(8,128)(2,1)} %slice.4), channel_id=1, source_target_pairs={{0,32},{32,64},{64,96},{96,128},{128,160},{160,192},{192,224},{1,3... | collective-permute-start | bytes 3538952 | tf_op jit(solution)/shard_map/ppermute | solution.py:28
  58.2 1.9 %collective-permute-start.1 = (bf16[2304,256]{1,0:T(8,128)(2,1)}, bf16[2304,256]{1,0:T(8,128)(2,1)}, u32[]{:S(2)}, u32[]{:S(2)}) collective-permute-start(bf16[2304,256]{1,0:T(8,128)(2,1)} %slice.4), channel_id=1, source_target_pairs={{32,0},{64,32},{96,64},{128,96},{160,128},{192,160},{224,192},{33,... | collective-permute-start | bytes 3538952 | tf_op jit(solution)/shard_map/ppermute | solution.py:29
  60.2 0.0 copy-done.4
  60.2 0.6 broadcast_subtract_fusion.ids_ref
  60.8 11.0 %collective-permute-done.before_ref = bf16[2304,256]{1,0:T(8,128)(2,1)} collective-permute-done((bf16[2304,256]{1,0:T(8,128)(2,1)}, bf16[2304,256]{1,0:T(8,128)(2,1)}, u32[]{:S(2)}, u32[]{:S(2)}) %collective-permute-start) | collective-permute-done | bytes 1179680 | tf_op jit(solution)/shard_map/ppermute | solution.py:28
  71.7 17.9 %collective-permute-done.1.after_ref = bf16[2304,256]{1,0:T(8,128)(2,1)} collective-permute-done((bf16[2304,256]{1,0:T(8,128)(2,1)}, bf16[2304,256]{1,0:T(8,128)(2,1)}, u32[]{:S(2)}, u32[]{:S(2)}) %collective-permute-start.1) | collective-permute-done | bytes 1179680 | tf_op jit(solution)/shard_map/ppermute | solution.py:29
  89.6 0.0 copy-done
  89.6 39.6 %shard_map.73 = bf16[2304,128]{1,0:T(8,128)(2,1)} custom-call(s32[6,18]{1,0:T(8,128)} %broadcast_subtract_fusion.ids_ref, s32[6]{0:T(128)} %count_ref.1, bf16[2304,640]{1,0:T(8,128)(2,1)} %bitcast.38, bf16[2304,256]{1,0:T(8,128)(2,1)} %collective-permute-done.before_ref, bf16[2304,256]{1,0:T(8,128)(2,1)} %collective-permute-done.1.after_ref), custom_call_target="tpu_custom_call" | custom-call | tf_op jit(solution)/shard_map/pallas_call | solution.py:95
  129.3 12.9 %all_to_all.35 = bf16[16,144,128]{2,1,0:T(8,128)(2,1)S(1)} all-to-all(bf16[16,144,128]{2,1,0:T(8,128)(2,1)} %bitcast.45), channel_id=1, replica_groups=mesh['patch'=8,'seq'=16,'cfg'=2] {'seq'}, dimensions={0} | all-to-all | bytes 1179648 | tf_op jit(solution)/shard_map/all_to_all | solution.py:131
  142.1 0.9 copy_bitcast_fusion.1
Async XLA Ops:
  0.0 2.6 %copy-start.1 = (bf16[144,2048]{1,0:T(8,128)(2,1)S(1)}, bf16[144,2048]{1,0:T(8,128)(2,1)}, u32[]{:S(2)}) copy-start(bf16[144,2048]{1,0:T(8,128)(2,1)} %param.7) | copy-start | bytes 1769476
  0.0 2.7 %copy-start.2 = (bf16[144,2048]{1,0:T(8,128)(2,1)S(1)}, bf16[144,2048]{1,0:T(8,128)(2,1)}, u32[]{:S(2)}) copy-start(bf16[144,2048]{1,0:T(8,128)(2,1)} %param.8) | copy-start | bytes 1769476
  0.0 2.9 %copy-start.3 = (bf16[144,2048]{1,0:T(8,128)(2,1)S(1)}, bf16[144,2048]{1,0:T(8,128)(2,1)}, u32[]{:S(2)}) copy-start(bf16[144,2048]{1,0:T(8,128)(2,1)} %param.9) | copy-start | bytes 1769476
  49.6 10.6 %copy-start.4 = (s32[6,18]{1,0:T(8,128)S(1)}, s32[6,18]{1,0:T(8,128)}, u32[]{:S(2)}) copy-start(s32[6,18]{1,0:T(8,128)} %param.12) | copy-start | bytes 1300
  50.4 39.2 %copy-start = (bf16[288,8,5,128]{3,1,2,0:T(8,128)(2,1)}, bf16[288,8,5,128]{3,1,2,0:T(8,128)(2,1)S(1)}, u32[]{:S(2)}) copy-start(bf16[288,8,5,128]{3,1,2,0:T(8,128)(2,1)S(1)} %copy.34) | copy-start | bytes 8847364
  51.6 20.1 %collective-permute-start = (bf16[2304,256]{1,0:T(8,128)(2,1)}, bf16[2304,256]{1,0:T(8,128)(2,1)}, u32[]{:S(2)}, u32[]{:S(2)}) collective-permute-start(bf16[2304,256]{1,0:T(8,128)(2,1)} %slice.4), channel_id=1, source_target_pairs={{0,32},{32,64},{64,96},{96,128},{128,160},{160,192},{192,224},{1,3... | collective-permute-start | bytes 3538952 | tf_op jit(solution)/shard_map/ppermute | solution.py:28
  58.2 31.4 %collective-permute-start.1 = (bf16[2304,256]{1,0:T(8,128)(2,1)}, bf16[2304,256]{1,0:T(8,128)(2,1)}, u32[]{:S(2)}, u32[]{:S(2)}) collective-permute-start(bf16[2304,256]{1,0:T(8,128)(2,1)} %slice.4), channel_id=1, source_target_pairs={{32,0},{64,32},{96,64},{128,96},{160,128},{192,160},{224,192},{33,... | collective-permute-start | bytes 3538952 | tf_op jit(solution)/shard_map/ppermute | solution.py:29

commit v3 on v2

--- a/solution.py
+++ b/solution.py
@@ -37,7 +37,7 @@
     width = local_heads * HEAD_DIM
     factor = 1.0 / (HEAD_DIM**0.5) / soft_cap
     for h in range(local_heads):
-        q_cols = pl.ds(2 * width + h * HEAD_DIM, HEAD_DIM)
+        q_cols = pl.ds(h * HEAD_DIM, HEAD_DIM)
         start_q = pl.multiple_of(t * TILE_TOKENS, TILE_TOKENS)
         query = fresh_ref[pl.ds(start_q, TILE_TOKENS), q_cols]
         acc_ref[...] = jnp.zeros_like(acc_ref)
@@ -71,7 +71,7 @@
 
             @pl.when(which == 1)
             def _():
-                accumulate(fresh_ref, 3 * width + h * HEAD_DIM, 4 * width + h * HEAD_DIM, row)
+                accumulate(fresh_ref, width + h * HEAD_DIM, 2 * width + h * HEAD_DIM, row)
 
             @pl.when(which == 2)
             def _():
@@ -115,14 +115,15 @@
     per_patch = TILES_H * TILES_W
     rows = query.shape[0]
     patch_rows = rows * seq_count
-    stacked = jnp.stack([stale_key, stale_value, query, fresh_key, fresh_value], axis=1)
-    stacked = stacked.reshape(rows, 5, seq_count, width)
-    regrouped = lax.all_to_all(stacked, "seq", split_axis=2, concat_axis=0, tiled=True)
-    fresh = regrouped.reshape(patch_rows, 5 * width)
-    stale = fresh[:, : 2 * width]
+    stale = jnp.stack([stale_key, stale_value], axis=1).reshape(rows, 2, seq_count, width)
+    stale = lax.all_to_all(stale, "seq", split_axis=2, concat_axis=0, tiled=True)
+    stale = stale.reshape(patch_rows, 2 * width)
     framed = with_halo(stale, (("patch", 0),), patch_rows)
     before = framed[:patch_rows]
     after = framed[2 * patch_rows :]
+    current = jnp.stack([query, fresh_key, fresh_value], axis=1).reshape(rows, 3, seq_count, width)
+    current = lax.all_to_all(current, "seq", split_axis=2, concat_axis=0, tiled=True)
+    fresh = current.reshape(patch_rows, 3 * width)
     first_tile = (lax.axis_index("patch") - 1) * per_patch
     local_ids = (key_tiles - first_tile).astype(jnp.int32)
     merged = tile_attention(

time: 142 us -> 130 us (0.915)
  the two profiles are of different devices: /device:TPU:1 before, /device:TPU:128 now
where the time goes in v3:
time: 130 us
  waiting for transfers between devices  43 us (33%)
  Pallas kernels  38.3 us (29%)
  blocking collectives  17.7 us (14%)
  starting transfers between devices  15.2 us (12%)
  local copies, waits for them, and re-layouts  10.7 us (8%)
  other arithmetic  4.49 us (3%)
    pallas_call x1, Pallas kernels, tile_attention(): pl.pallas_call(functools.partial(attention_kernel, local_heads, per_patch...  38.3 us
    all_to_all x1, waiting for transfers between devices, on_device(): lax.all_to_all(current, 'seq', split_axis=2, concat_axis=0, tiled=True)  20 us
    all_to_all x1, blocking collectives, on_device(): lax.all_to_all(merged, 'seq', split_axis=0, concat_axis=1, tiled=True)  17.7 us
    all_to_all x1, waiting for transfers between devices, on_device(): lax.all_to_all(stale, 'seq', split_axis=2, concat_axis=0, tiled=True)  16.2 us
    all_to_all x1, starting transfers between devices, on_device(): lax.all_to_all(stale, 'seq', split_axis=2, concat_axis=0, tiled=True)  7.17 us
    ppermute x1, waiting for transfers between devices, with_halo(): before = lax.ppermute(last, axis, up)  5.87 us
    unnamed x19, local copies, waits for them, and re-layouts  5.2 us
    all_to_all x1, starting transfers between devices, on_device(): lax.all_to_all(current, 'seq', split_axis=2, concat_axis=0, tiled=True)  3.71 us
  transfers between devices with their start and end apart: 4, of which 4 were waited for; matrix products, arithmetic and copies ran while one was open for 5% of the time, Pallas kernels for 0%

profile of v3, /device:TPU:128, one launch (start us, length us, event | category | flops | bytes accessed | tf_op | source)
XLA Modules:
  0.0 129.5 jit_solution(11381981238744790163)
XLA Ops:
  0.0 0.0 copy-start.1
  0.0 1.2 copy.34
  1.2 0.9 copy.26
  2.2 0.0 copy-done.1
  2.2 0.1 copy.35
  2.3 0.9 copy.27
  3.2 3.7 %pad_maximum_fusion.1 = bf16[144,2,16,128]{3,1,0,2:T(2,128)(2,1)} fusion(bf16[144,1,16,128]{3,1,0,2:T(2,128)(2,1)S(1)} %copy.27, bf16[144,1,16,128]{3,1,0,2:T(2,128)(2,1)S(1)} %copy.26), kind=kLoop, calls=%fused_computation.3 | loop fusion | flops 2359296 | bytes 2359296 | tf_op jit(solution)/shard_map/stack | solution.py:118
  6.9 0.0 copy-start.2
  6.9 0.0 copy-start.3
  6.9 7.2 %all-to-all-start.1 = ((bf16[144,2,16,128]{3,1,0,2:T(2,128)(2,1)}), bf16[144,2,16,128]{3,1,0,2:T(2,128)(2,1)S(1)}, u32[]{:S(2)}, u32[]{:S(2)}) async-start(bf16[144,2,16,128]{3,1,0,2:T(2,128)(2,1)} %pad_maximum_fusion.1), calls=%async_computation.1 | async-start | bytes 2359296 | tf_op jit(solution)/shard_map/all_to_all | solution.py:119
  14.1 0.0 copy-start.4
  14.1 0.0 copy-done.2
  14.1 0.1 copy.30
  14.2 0.0 copy-done.3
  14.2 0.1 copy.31
  14.3 0.8 copy-done.4
  15.2 0.1 copy.32
  15.3 0.2 pad_maximum_fusion
  15.5 1.7 %copy.24 = bf16[144,3,16,128]{3,0,1,2:T(8,128)(2,1)} copy(bf16[144,3,16,128]{3,2,0,1:T(8,128)(2,1)S(1)} %pad_maximum_fusion) | data formatting | bytes 3538944 | tf_op jit(solution)/shard_map/stack | solution.py:124
  17.1 16.2 %all-to-all-done.1 = bf16[144,2,16,128]{3,1,0,2:T(2,128)(2,1)S(1)} async-done(((bf16[144,2,16,128]{3,1,0,2:T(2,128)(2,1)}), bf16[144,2,16,128]{3,1,0,2:T(2,128)(2,1)S(1)}, u32[]{:S(2)}, u32[]{:S(2)}) %all-to-all-start.1) | async-done | bytes 1179680 | tf_op jit(solution)/shard_map/all_to_all | solution.py:119
  33.3 3.7 %all-to-all-start = ((bf16[144,3,16,128]{3,0,1,2:T(8,128)(2,1)}), bf16[144,3,16,128]{3,0,1,2:T(8,128)(2,1)S(1)}, u32[]{:S(2)}, u32[]{:S(2)}) async-start(bf16[144,3,16,128]{3,0,1,2:T(8,128)(2,1)} %copy.24), calls=%async_computation | async-start | bytes 3538944 | tf_op jit(solution)/shard_map/all_to_all | solution.py:125
  37.0 0.0 copy-start.5
  37.0 1.2 copy.41
  38.2 1.9 %collective-permute-start.1 = (bf16[2304,256]{1,0:T(8,128)(2,1)}, bf16[2304,256]{1,0:T(8,128)(2,1)S(1)}, u32[]{:S(2)}, u32[]{:S(2)}) collective-permute-start(bf16[2304,256]{1,0:T(8,128)(2,1)} %bitcast.44), channel_id=1, source_target_pairs={{32,0},{64,32},{96,64},{128,96},{160,128},{192,160},{224,192},{33,... | collective-permute-start | bytes 3538952 | tf_op jit(solution)/shard_map/ppermute | solution.py:29
  40.1 2.4 %collective-permute-start = (bf16[2304,256]{1,0:T(8,128)(2,1)}, bf16[2304,256]{1,0:T(8,128)(2,1)}, u32[]{:S(2)}, u32[]{:S(2)}) collective-permute-start(bf16[2304,256]{1,0:T(8,128)(2,1)} %bitcast.44), channel_id=1, source_target_pairs={{0,32},{32,64},{64,96},{96,128},{128,160},{160,192},{192,224},{1,3... | collective-permute-start | bytes 3538952 | tf_op jit(solution)/shard_map/ppermute | solution.py:28
  42.6 0.0 copy-done.5
  42.6 0.6 broadcast_subtract_fusion.ids_ref
  43.2 20.0 %all-to-all-done = bf16[144,3,16,128]{3,0,1,2:T(8,128)(2,1)S(1)} async-done(((bf16[144,3,16,128]{3,0,1,2:T(8,128)(2,1)}), bf16[144,3,16,128]{3,0,1,2:T(8,128)(2,1)S(1)}, u32[]{:S(2)}, u32[]{:S(2)}) %all-to-all-start) | async-done | bytes 1769504 | tf_op jit(solution)/shard_map/all_to_all | solution.py:125
  63.2 1.1 copy.25
  64.3 1.5 %copy.40 = bf16[288,8,3,128]{3,1,2,0:T(8,128)(2,1)} copy(bf16[288,8,3,128]{3,2,1,0:T(4,128)(2,1)S(1)} %bitcast.45) | data formatting | bytes 3538944
  65.8 1.0 collective-permute-done.1.after_ref
  66.8 0.0 copy-start
  66.8 5.9 %collective-permute-done.before_ref = bf16[2304,256]{1,0:T(8,128)(2,1)} collective-permute-done((bf16[2304,256]{1,0:T(8,128)(2,1)}, bf16[2304,256]{1,0:T(8,128)(2,1)}, u32[]{:S(2)}, u32[]{:S(2)}) %collective-permute-start) | collective-permute-done | bytes 1179680 | tf_op jit(solution)/shard_map/ppermute | solution.py:28
  72.7 0.0 copy-done
  72.7 38.3 %shard_map.73 = bf16[2304,128]{1,0:T(8,128)(2,1)} custom-call(s32[6,18]{1,0:T(8,128)} %broadcast_subtract_fusion.ids_ref, s32[6]{0:T(128)} %count_ref.1, bf16[2304,384]{1,0:T(8,128)(2,1)} %bitcast.47, bf16[2304,256]{1,0:T(8,128)(2,1)} %collective-permute-done.before_ref, bf16[2304,256]{1,0:T(8,128)(2,1)} %copy-done), custom_call_target="tpu_custom_call" | custom-call | tf_op jit(solution)/shard_map/pallas_call | solution.py:95
  111.0 17.7 %all_to_all.49 = bf16[16,144,128]{2,1,0:T(8,128)(2,1)S(1)} all-to-all(bf16[16,144,128]{2,1,0:T(8,128)(2,1)} %bitcast.54), channel_id=1, replica_groups=mesh['patch'=8,'seq'=16,'cfg'=2] {'seq'}, dimensions={0} | all-to-all | bytes 1179648 | tf_op jit(solution)/shard_map/all_to_all | solution.py:132
  128.7 0.9 copy_bitcast_fusion.2
Async XLA Ops:
  0.0 2.2 %copy-start.1 = (bf16[144,2048]{1,0:T(8,128)(2,1)S(1)}, bf16[144,2048]{1,0:T(8,128)(2,1)}, u32[]{:S(2)}) copy-start(bf16[144,2048]{1,0:T(8,128)(2,1)} %param.11) | copy-start | bytes 1769476
  6.9 7.2 %copy-start.2 = (bf16[144,2048]{1,0:T(8,128)(2,1)S(1)}, bf16[144,2048]{1,0:T(8,128)(2,1)}, u32[]{:S(2)}) copy-start(bf16[144,2048]{1,0:T(8,128)(2,1)} %param.7) | copy-start | bytes 1769476
  6.9 7.3 %copy-start.3 = (bf16[144,2048]{1,0:T(8,128)(2,1)S(1)}, bf16[144,2048]{1,0:T(8,128)(2,1)}, u32[]{:S(2)}) copy-start(bf16[144,2048]{1,0:T(8,128)(2,1)} %param.8) | copy-start | bytes 1769476
  6.9 26.4 %all-to-all-start.1 = ((bf16[144,2,16,128]{3,1,0,2:T(2,128)(2,1)}), bf16[144,2,16,128]{3,1,0,2:T(2,128)(2,1)S(1)}, u32[]{:S(2)}, u32[]{:S(2)}) async-start(bf16[144,2,16,128]{3,1,0,2:T(2,128)(2,1)} %pad_maximum_fusion.1), calls=%async_computation.1 | async-start | bytes 2359296 | tf_op jit(solution)/shard_map/all_to_all | solution.py:119
  14.1 1.1 copy-start.4
  33.3 29.9 %all-to-all-start = ((bf16[144,3,16,128]{3,0,1,2:T(8,128)(2,1)}), bf16[144,3,16,128]{3,0,1,2:T(8,128)(2,1)S(1)}, u32[]{:S(2)}, u32[]{:S(2)}) async-start(bf16[144,3,16,128]{3,0,1,2:T(8,128)(2,1)} %copy.24), calls=%async_computation | async-start | bytes 3538944 | tf_op jit(solution)/shard_map/all_to_all | solution.py:125
  37.0 5.5 %copy-start.5 = (s32[6,18]{1,0:T(8,128)S(1)}, s32[6,18]{1,0:T(8,128)}, u32[]{:S(2)}) copy-start(s32[6,18]{1,0:T(8,128)} %param.12) | copy-start | bytes 1300
  38.2 28.6 %collective-permute-start.1 = (bf16[2304,256]{1,0:T(8,128)(2,1)}, bf16[2304,256]{1,0:T(8,128)(2,1)S(1)}, u32[]{:S(2)}, u32[]{:S(2)}) collective-permute-start(bf16[2304,256]{1,0:T(8,128)(2,1)} %bitcast.44), channel_id=1, source_target_pairs={{32,0},{64,32},{96,64},{128,96},{160,128},{192,160},{224,192},{33,... | collective-permute-start | bytes 3538952 | tf_op jit(solution)/shard_map/ppermute | solution.py:29
  40.1 32.5 %collective-permute-start = (bf16[2304,256]{1,0:T(8,128)(2,1)}, bf16[2304,256]{1,0:T(8,128)(2,1)}, u32[]{:S(2)}, u32[]{:S(2)}) collective-permute-start(bf16[2304,256]{1,0:T(8,128)(2,1)} %bitcast.44), channel_id=1, source_target_pairs={{0,32},{32,64},{64,96},{96,128},{128,160},{160,192},{192,224},{1,3... | collective-permute-start | bytes 3538952 | tf_op jit(solution)/shard_map/ppermute | solution.py:28
  66.8 5.9 %copy-start = (bf16[2304,256]{1,0:T(8,128)(2,1)}, bf16[2304,256]{1,0:T(8,128)(2,1)S(1)}, u32[]{:S(2)}) copy-start(bf16[2304,256]{1,0:T(8,128)(2,1)S(1)} %collective-permute-done.1.after_ref) | copy-start | bytes 3538948

commit v4 on v2

--- a/solution.py
+++ b/solution.py
@@ -31,17 +31,25 @@
     return x
 
 
-def attention_kernel(local_heads, per_patch, ids_ref, count_ref, fresh_ref, before_ref, after_ref,
-                     o_ref, acc_ref, tot_ref):
+def attention_kernel(local_heads, per_patch, stale_phase, ids_ref, count_ref, fresh_ref, *refs):
+    if stale_phase:
+        before_ref, after_ref, acc_in, tot_in, o_ref, acc_ref, tot_ref = refs
+    else:
+        acc_ref, tot_ref = refs
     t = pl.program_id(0)
     width = local_heads * HEAD_DIM
     factor = 1.0 / (HEAD_DIM**0.5) / soft_cap
     for h in range(local_heads):
-        q_cols = pl.ds(2 * width + h * HEAD_DIM, HEAD_DIM)
+        head = pl.ds(h * HEAD_DIM, HEAD_DIM)
         start_q = pl.multiple_of(t * TILE_TOKENS, TILE_TOKENS)
-        query = fresh_ref[pl.ds(start_q, TILE_TOKENS), q_cols]
-        acc_ref[...] = jnp.zeros_like(acc_ref)
-        tot_ref[...] = jnp.zeros_like(tot_ref)
+        query = fresh_ref[pl.ds(start_q, TILE_TOKENS), pl.ds(h * 3 * HEAD_DIM, HEAD_DIM)]
+        if stale_phase:
+            acc_ref[...] = acc_in[:, head]
+            tot_ref[...] = tot_in[:, head]
+        else:
+            acc_ref[:, head] = jnp.zeros((TILE_TOKENS, HEAD_DIM), jnp.float32)
+            tot_ref[:, head] = jnp.zeros((TILE_TOKENS, HEAD_DIM), jnp.float32)
+        acc_at = slice(None) if stale_phase else head
 
         def accumulate(ref, k_col, v_col, row):
             start = pl.multiple_of(row * TILE_TOKENS, TILE_TOKENS)
@@ -54,8 +62,8 @@
             part = weight[:, 0:HEAD_DIM]
             for c in range(1, TILE_TOKENS // HEAD_DIM):
                 part = part + weight[:, c * HEAD_DIM:(c + 1) * HEAD_DIM]
-            tot_ref[...] += part
-            acc_ref[...] += jnp.dot(
+            tot_ref[:, acc_at] += part
+            acc_ref[:, acc_at] += jnp.dot(
                 weight.astype(jnp.bfloat16), values, preferred_element_type=jnp.float32
             )
 
@@ -63,25 +71,28 @@
             u = ids_ref[t, j]
             which = u // per_patch
             row = u - which * per_patch
-            stale_k, stale_v = h * HEAD_DIM, width + h * HEAD_DIM
+            if stale_phase:
+                stale_k, stale_v = h * 2 * HEAD_DIM, (h * 2 + 1) * HEAD_DIM
 
-            @pl.when(which == 0)
-            def _():
-                accumulate(before_ref, stale_k, stale_v, row)
+                @pl.when(which == 0)
+                def _():
+                    accumulate(before_ref, stale_k, stale_v, row)
 
-            @pl.when(which == 1)
-            def _():
-                accumulate(fresh_ref, 3 * width + h * HEAD_DIM, 4 * width + h * HEAD_DIM, row)
+                @pl.when(which == 2)
+                def _():
+                    accumulate(after_ref, stale_k, stale_v, row)
+            else:
 
-            @pl.when(which == 2)
-            def _():
-                accumulate(after_ref, stale_k, stale_v, row)
+                @pl.when(which == 1)
+                def _():
+                    accumulate(fresh_ref, (h * 3 + 1) * HEAD_DIM, (h * 3 + 2) * HEAD_DIM, row)
 
             return carry
 
         lax.fori_loop(0, count_ref[t], body, 0)
-        total = jnp.sum(tot_ref[...], axis=1, keepdims=True)
-        o_ref[:, pl.ds(h * HEAD_DIM, HEAD_DIM)] = (acc_ref[...] / total).astype(o_ref.dtype)
+        if stale_phase:
+            total = jnp.sum(tot_ref[...], axis=1, keepdims=True)
+            o_ref[:, head] = (acc_ref[...] / total).astype(o_ref.dtype)
 
 
 def tile_attention(fresh, before, after, local_ids, tile_count, local_heads, per_patch):
@@ -92,20 +103,29 @@
     def whole(array):
         return pl.BlockSpec(array.shape, lambda t, ids, cnt: (0, 0))
 
+    tile = pl.BlockSpec((TILE_TOKENS, width), lambda t, ids, cnt: (t, 0))
+    partial = jax.ShapeDtypeStruct((rows, width), jnp.float32)
+    acc, tot = pl.pallas_call(
+        functools.partial(attention_kernel, local_heads, per_patch, False),
+        out_shape=(partial, partial),
+        grid_spec=pltpu.PrefetchScalarGridSpec(
+            num_scalar_prefetch=2, grid=(tiles,), in_specs=[whole(fresh)], out_specs=(tile, tile),
+        ),
+    )(local_ids, tile_count, fresh)
     return pl.pallas_call(
-        functools.partial(attention_kernel, local_heads, per_patch),
+        functools.partial(attention_kernel, local_heads, per_patch, True),
         out_shape=jax.ShapeDtypeStruct((rows, width), jnp.bfloat16),
         grid_spec=pltpu.PrefetchScalarGridSpec(
             num_scalar_prefetch=2,
             grid=(tiles,),
-            in_specs=[whole(fresh), whole(before), whole(after)],
-            out_specs=pl.BlockSpec((TILE_TOKENS, width), lambda t, ids, cnt: (t, 0)),
+            in_specs=[whole(fresh), whole(before), whole(after), tile, tile],
+            out_specs=tile,
             scratch_shapes=[
                 pltpu.VMEM((TILE_TOKENS, HEAD_DIM), jnp.float32),
                 pltpu.VMEM((TILE_TOKENS, HEAD_DIM), jnp.float32),
             ],
         ),
-    )(local_ids, tile_count, fresh, before, after)
+    )(local_ids, tile_count, fresh, before, after, acc, tot)
 
 
 def on_device(query, fresh_key, fresh_value, stale_key, stale_value, key_tiles, tile_count):
@@ -115,14 +135,17 @@
     per_patch = TILES_H * TILES_W
     rows = query.shape[0]
     patch_rows = rows * seq_count
-    stacked = jnp.stack([stale_key, stale_value, query, fresh_key, fresh_value], axis=1)
-    stacked = stacked.reshape(rows, 5, seq_count, width)
-    regrouped = lax.all_to_all(stacked, "seq", split_axis=2, concat_axis=0, tiled=True)
-    fresh = regrouped.reshape(patch_rows, 5 * width)
-    stale = fresh[:, : 2 * width]
+
+    def interleaved(arrays):
+        parts = [a.reshape(rows, NUM_HEADS, HEAD_DIM) for a in arrays]
+        joined = jnp.stack(parts, axis=2).reshape(rows, NUM_HEADS * len(arrays) * HEAD_DIM)
+        return lax.all_to_all(joined, "seq", split_axis=1, concat_axis=0, tiled=True)
+
+    stale = interleaved([stale_key, stale_value])
     framed = with_halo(stale, (("patch", 0),), patch_rows)
     before = framed[:patch_rows]
     after = framed[2 * patch_rows :]
+    fresh = interleaved([query, fresh_key, fresh_value])
     first_tile = (lax.axis_index("patch") - 1) * per_patch
     local_ids = (key_tiles - first_tile).astype(jnp.int32)
     merged = tile_attention(

time: 142 us -> 123 us (0.87)
  blocking collectives: 56.9 us -> 15.2 us
  starting transfers between devices: 8.52 us -> 22.1 us
  waiting for transfers between devices: 28.9 us -> 15.7 us
  local copies, waits for them, and re-layouts: 8.33 us -> 18.8 us
  Pallas kernels: 39.6 us -> 45.4 us
  other arithmetic: 0.58 us -> 5.92 us
    all_to_all x1 -> x0, blocking collectives: 44 us -> none  [on_device(): lax.all_to_all(stacked, 'seq', split_axis=2, concat_axis=0, tiled=True)]
    ppermute x1, waiting for transfers between devices: 17.9 us -> 0.01 us  [with_halo(): after = lax.ppermute(leading, axis, down)]
    all_to_all x0 -> x2, waiting for transfers between devices: none -> 15.7 us  [interleaved(): lax.all_to_all(joined, 'seq', split_axis=1, concat_axis=0, tiled=True)]
    all_to_all x0 -> x2, starting transfers between devices: none -> 13.9 us  [interleaved(): lax.all_to_all(joined, 'seq', split_axis=1, concat_axis=0, tiled=True)]
    ppermute x1, waiting for transfers between devices: 11 us -> 0.01 us  [with_halo(): before = lax.ppermute(last, axis, up)]
    all_to_all x1 -> x3, local copies, waits for them, and re-layouts: 1.22 us -> 7.88 us  [interleaved(): lax.all_to_all(joined, 'seq', split_axis=1, concat_axis=0, tiled=True)]
    pallas_call x1 -> x2, Pallas kernels: 39.6 us -> 45.4 us  [tile_attention(): pl.pallas_call(functools.partial(attention_kernel, local_heads, per_patch...]
    another operation x2 -> x4, local copies, waits for them, and re-layouts: 0.9 us -> 6.38 us  [interleaved(): jnp.stack(parts, axis=2).reshape(rows, NUM_HEADS * len(arrays) * HEAD_DIM)]
  transfers between devices with their start and end apart: 2 -> 4, of which waited for: 2 -> 2; matrix products, arithmetic and copies ran while one was open for 0% -> 11% of each run, Pallas kernels for 0% -> 13%
where the time goes in v4:
time: 123 us
  Pallas kernels  45.4 us (37%)
  starting transfers between devices  22.1 us (18%)
  local copies, waits for them, and re-layouts  18.8 us (15%)
  waiting for transfers between devices  15.7 us (13%)
  blocking collectives  15.2 us (12%)
  other arithmetic  5.92 us (5%)
    pallas_call x2, Pallas kernels, tile_attention(): pl.pallas_call(functools.partial(attention_kernel, local_heads, per_patch...  45.4 us
    all_to_all x2, waiting for transfers between devices, interleaved(): lax.all_to_all(joined, 'seq', split_axis=1, concat_axis=0, tiled=True)  15.7 us
    all_to_all x1, blocking collectives, on_device(): lax.all_to_all(merged, 'seq', split_axis=0, concat_axis=1, tiled=True)  15.2 us
    all_to_all x2, starting transfers between devices, interleaved(): lax.all_to_all(joined, 'seq', split_axis=1, concat_axis=0, tiled=True)  13.9 us
    all_to_all x3, local copies, waits for them, and re-layouts, interleaved(): lax.all_to_all(joined, 'seq', split_axis=1, concat_axis=0, tiled=True)  7.88 us
    another operation x4, local copies, waits for them, and re-layouts, interleaved(): jnp.stack(parts, axis=2).reshape(rows, NUM_HEADS * len(arrays) * HEAD_DIM)  6.38 us
    another operation x2, other arithmetic, interleaved(): jnp.stack(parts, axis=2).reshape(rows, NUM_HEADS * len(arrays) * HEAD_DIM)  5.34 us
    ppermute x1, starting transfers between devices, with_halo(): before = lax.ppermute(last, axis, up)  4.8 us
  transfers between devices with their start and end apart: 4, of which 2 were waited for; matrix products, arithmetic and copies ran while one was open for 11% of the time, Pallas kernels for 13%

profile of v4, /device:TPU:1, one launch (start us, length us, event | category | flops | bytes accessed | tf_op | source)
XLA Modules:
  0.0 123.3 jit_solution(13506733644784762377)
XLA Ops:
  0.0 0.0 copy-start.5
  0.0 1.2 %copy.24 = bf16[18,8,16,128]{3,2,1,0:T(8,128)(2,1)S(1)} copy(bf16[18,8,16,128]{3,1,2,0:T(8,128)(2,1)} %bitcast.28) | data formatting | bytes 1179648
  1.2 0.0 copy-done.5
  1.3 0.1 copy.25
  1.4 0.1 pad_maximum_fusion.1
  1.5 1.2 copy.21
  2.7 1.6 %all_to_all.46 = bf16[144,16,256]{2,0,1:T(8,128)(2,1)} reshape(bf16[144,16,2,128]{3,2,0,1:T(2,128)(2,1)S(1)} %copy.21) | data formatting | bytes 2359296 | tf_op jit(solution)/shard_map/all_to_all | solution.py:142
  4.3 0.0 copy-start.2
  4.3 7.8 %all-to-all-start.1 = ((bf16[144,16,256]{2,0,1:T(8,128)(2,1)}), bf16[144,16,256]{2,0,1:T(8,128)(2,1)}, u32[]{:S(2)}, u32[]{:S(2)}) async-start(bf16[144,16,256]{2,0,1:T(8,128)(2,1)} %all_to_all.46), calls=%async_computation.1 | async-start | bytes 2359296 | tf_op jit(solution)/shard_map/all_to_all | solution.py:142
  12.1 0.0 copy-done.2
  12.1 0.0 copy-start.3
  12.1 0.9 stack_reshape.20
  13.1 0.1 copy-done.3
  13.2 0.0 copy-start.4
  13.2 2.1 %stack_reshape.21 = bf16[144,16,1,128]{3,2,1,0:T(2,128)(2,1)} reshape(bf16[144,2048]{1,0:T(8,128)(2,1)S(1)} %copy-done.3) | data formatting | bytes 1179648 | tf_op jit(solution)/shard_map/stack;reshape | solution.py:141
  15.3 0.0 copy-done.4
  15.3 2.1 %stack_reshape.22 = bf16[144,16,1,128]{3,2,1,0:T(2,128)(2,1)} reshape(bf16[144,2048]{1,0:T(8,128)(2,1)S(1)} %copy-done.4) | data formatting | bytes 1179648 | tf_op jit(solution)/shard_map/stack;reshape | solution.py:141
  17.4 5.2 %pad_maximum_fusion = bf16[144,16,3,128]{3,2,1,0:T(4,128)(2,1)S(1)} fusion(bf16[144,16,1,128]{3,2,1,0:T(2,128)(2,1)} %stack_reshape.22, bf16[144,16,1,128]{3,2,1,0:T(2,128)(2,1)} %stack_reshape.21, bf16[144,16,1,128]{3,2,1,0:T(2,128)(2,1)S(1)} %stack_reshape.20), kind=kLoop, calls=%fused_computation | loop fusion | flops 5308416 | bytes 3538944 | tf_op jit(solution)/shard_map/stack | solution.py:141
  22.6 3.2 %all_to_all.42 = bf16[144,16,384]{2,1,0:T(8,128)(2,1)} reshape(bf16[144,16,3,128]{3,2,1,0:T(4,128)(2,1)S(1)} %pad_maximum_fusion) | data formatting | bytes 3538944 | tf_op jit(solution)/shard_map/all_to_all | solution.py:142
  25.8 3.1 %copy.20 = bf16[144,16,384]{2,0,1:T(8,128)(2,1)} copy(bf16[144,16,384]{2,1,0:T(8,128)(2,1)} %all_to_all.42) | data formatting | bytes 3538944 | tf_op jit(solution)/shard_map/all_to_all | solution.py:142
  28.9 0.0 copy-start.6
  28.9 0.6 all-to-all-done.1
  29.5 6.1 %all-to-all-start = ((bf16[144,16,384]{2,0,1:T(8,128)(2,1)}), bf16[144,16,384]{2,0,1:T(8,128)(2,1)S(1)}, u32[]{:S(2)}, u32[]{:S(2)}) async-start(bf16[144,16,384]{2,0,1:T(8,128)(2,1)} %copy.20), calls=%async_computation | async-start | bytes 3538944 | tf_op jit(solution)/shard_map/all_to_all | solution.py:142
  35.7 3.4 %collective-permute-start.1 = (bf16[2304,256]{1,0:T(8,128)(2,1)}, bf16[2304,256]{1,0:T(8,128)(2,1)S(1)}, u32[]{:S(2)}, u32[]{:S(2)}) collective-permute-start(bf16[2304,256]{1,0:T(8,128)(2,1)} %bitcast.3), channel_id=1, source_target_pairs={{32,0},{64,32},{96,64},{128,96},{160,128},{192,160},{224,192},{33,... | collective-permute-start | bytes 3538952 | tf_op jit(solution)/shard_map/ppermute | solution.py:29
  39.1 4.8 %collective-permute-start = (bf16[2304,256]{1,0:T(8,128)(2,1)}, bf16[2304,256]{1,0:T(8,128)(2,1)}, u32[]{:S(2)}, u32[]{:S(2)}) collective-permute-start(bf16[2304,256]{1,0:T(8,128)(2,1)} %bitcast.3), channel_id=1, source_target_pairs={{0,32},{32,64},{64,96},{96,128},{128,160},{160,192},{192,224},{1,3... | collective-permute-start | bytes 3538952 | tf_op jit(solution)/shard_map/ppermute | solution.py:28
  43.9 0.0 copy-done.6
  43.9 0.6 broadcast_subtract_fusion.ids_ref
  44.5 15.1 %all-to-all-done = bf16[144,16,384]{2,0,1:T(8,128)(2,1)S(1)} async-done(((bf16[144,16,384]{2,0,1:T(8,128)(2,1)}), bf16[144,16,384]{2,0,1:T(8,128)(2,1)S(1)}, u32[]{:S(2)}, u32[]{:S(2)}) %all-to-all-start) | async-done | bytes 1769504 | tf_op jit(solution)/shard_map/all_to_all | solution.py:142
  59.6 0.0 copy-start
  59.6 1.2 copy-done
  60.8 16.4 %shard_map.73 = (f32[2304,128]{1,0:T(8,128)}, f32[2304,128]{1,0:T(8,128)}) custom-call(s32[6,18]{1,0:T(8,128)} %broadcast_subtract_fusion.ids_ref, s32[6]{0:T(128)} %count_ref.3, bf16[2304,384]{1,0:T(8,128)(2,1)} %bitcast.23), custom_call_target="tpu_custom_call" | custom-call | tf_op jit(solution)/shard_map/pallas_call | solution.py:108
  77.2 0.0 collective-permute-done.1.refs_1_
  77.2 0.0 copy-start.1
  77.2 0.0 collective-permute-done.refs_0_
  77.2 1.0 copy-done.1
  78.2 29.0 %shard_map.74 = bf16[2304,128]{1,0:T(8,128)(2,1)} custom-call(s32[6,18]{1,0:T(8,128)} %broadcast_subtract_fusion.ids_ref, s32[6]{0:T(128)} %count_ref.3, bf16[2304,384]{1,0:T(8,128)(2,1)} %bitcast.24, bf16[2304,256]{1,0:T(8,128)(2,1)} %collective-permute-done.refs_0_, bf16[2304,256]{1,0:T(8,128)(2,1)} %copy-done.1, f32[2304,128]{1,0:T(8,128)} %get-tuple-element.7.refs_2_, ...), custom_call_target="tpu_custom_call" | custom-call | tf_op jit(solution)/shard_map/pallas_call | solution.py:115
  107.2 15.2 %all_to_all.57 = bf16[16,144,128]{2,1,0:T(8,128)(2,1)S(1)} all-to-all(bf16[16,144,128]{2,1,0:T(8,128)(2,1)} %bitcast.25), channel_id=1, replica_groups=mesh['patch'=8,'seq'=16,'cfg'=2] {'seq'}, dimensions={0} | all-to-all | bytes 1179648 | tf_op jit(solution)/shard_map/all_to_all | solution.py:154
  122.4 0.9 copy_bitcast_fusion
Async XLA Ops:
  0.0 1.2 %copy-start.5 = (bf16[144,2048]{1,0:T(8,128)(2,1)S(1)}, bf16[144,2048]{1,0:T(8,128)(2,1)}, u32[]{:S(2)}) copy-start(bf16[144,2048]{1,0:T(8,128)(2,1)} %param.11) | copy-start | bytes 1769476
  4.3 7.8 %copy-start.2 = (bf16[144,2048]{1,0:T(8,128)(2,1)S(1)}, bf16[144,2048]{1,0:T(8,128)(2,1)}, u32[]{:S(2)}) copy-start(bf16[144,2048]{1,0:T(8,128)(2,1)} %param.7) | copy-start | bytes 1769476
  4.3 25.2 %all-to-all-start.1 = ((bf16[144,16,256]{2,0,1:T(8,128)(2,1)}), bf16[144,16,256]{2,0,1:T(8,128)(2,1)}, u32[]{:S(2)}, u32[]{:S(2)}) async-start(bf16[144,16,256]{2,0,1:T(8,128)(2,1)} %all_to_all.46), calls=%async_computation.1 | async-start | bytes 2359296 | tf_op jit(solution)/shard_map/all_to_all | solution.py:142
  12.1 1.1 copy-start.3
  13.2 2.1 %copy-start.4 = (bf16[144,2048]{1,0:T(8,128)(2,1)S(1)}, bf16[144,2048]{1,0:T(8,128)(2,1)}, u32[]{:S(2)}) copy-start(bf16[144,2048]{1,0:T(8,128)(2,1)} %param.9) | copy-start | bytes 1769476
  28.9 15.0 %copy-start.6 = (s32[6,18]{1,0:T(8,128)S(1)}, s32[6,18]{1,0:T(8,128)}, u32[]{:S(2)}) copy-start(s32[6,18]{1,0:T(8,128)} %param.12) | copy-start | bytes 1300
  29.5 30.0 %all-to-all-start = ((bf16[144,16,384]{2,0,1:T(8,128)(2,1)}), bf16[144,16,384]{2,0,1:T(8,128)(2,1)S(1)}, u32[]{:S(2)}, u32[]{:S(2)}) async-start(bf16[144,16,384]{2,0,1:T(8,128)(2,1)} %copy.20), calls=%async_computation | async-start | bytes 3538944 | tf_op jit(solution)/shard_map/all_to_all | solution.py:142
  35.7 41.5 %collective-permute-start.1 = (bf16[2304,256]{1,0:T(8,128)(2,1)}, bf16[2304,256]{1,0:T(8,128)(2,1)S(1)}, u32[]{:S(2)}, u32[]{:S(2)}) collective-permute-start(bf16[2304,256]{1,0:T(8,128)(2,1)} %bitcast.3), channel_id=1, source_target_pairs={{32,0},{64,32},{96,64},{128,96},{160,128},{192,160},{224,192},{33,... | collective-permute-start | bytes 3538952 | tf_op jit(solution)/shard_map/ppermute | solution.py:29
  39.1 38.1 %collective-permute-start = (bf16[2304,256]{1,0:T(8,128)(2,1)}, bf16[2304,256]{1,0:T(8,128)(2,1)}, u32[]{:S(2)}, u32[]{:S(2)}) collective-permute-start(bf16[2304,256]{1,0:T(8,128)(2,1)} %bitcast.3), channel_id=1, source_target_pairs={{0,32},{32,64},{64,96},{96,128},{128,160},{160,192},{192,224},{1,3... | collective-permute-start | bytes 3538952 | tf_op jit(solution)/shard_map/ppermute | solution.py:28
  59.6 1.2 copy-start
  77.2 1.0 copy-start.1

commit v5 on v4

--- a/solution.py
+++ b/solution.py
@@ -42,7 +42,7 @@
     for h in range(local_heads):
         head = pl.ds(h * HEAD_DIM, HEAD_DIM)
         start_q = pl.multiple_of(t * TILE_TOKENS, TILE_TOKENS)
-        query = fresh_ref[pl.ds(start_q, TILE_TOKENS), pl.ds(h * 3 * HEAD_DIM, HEAD_DIM)]
+        query = fresh_ref[pl.ds(start_q, TILE_TOKENS), pl.ds(h * HEAD_DIM, HEAD_DIM)]
         if stale_phase:
             acc_ref[...] = acc_in[:, head]
             tot_ref[...] = tot_in[:, head]
@@ -72,7 +72,7 @@
             which = u // per_patch
             row = u - which * per_patch
             if stale_phase:
-                stale_k, stale_v = h * 2 * HEAD_DIM, (h * 2 + 1) * HEAD_DIM
+                stale_k, stale_v = h * HEAD_DIM, width + h * HEAD_DIM
 
                 @pl.when(which == 0)
                 def _():
@@ -85,7 +85,7 @@
 
                 @pl.when(which == 1)
                 def _():
-                    accumulate(fresh_ref, (h * 3 + 1) * HEAD_DIM, (h * 3 + 2) * HEAD_DIM, row)
+                    accumulate(fresh_ref, width + h * HEAD_DIM, 2 * width + h * HEAD_DIM, row)
 
             return carry
 
@@ -137,9 +137,10 @@
     patch_rows = rows * seq_count
 
     def interleaved(arrays):
-        parts = [a.reshape(rows, NUM_HEADS, HEAD_DIM) for a in arrays]
-        joined = jnp.stack(parts, axis=2).reshape(rows, NUM_HEADS * len(arrays) * HEAD_DIM)
-        return lax.all_to_all(joined, "seq", split_axis=1, concat_axis=0, tiled=True)
+        parts = [a.reshape(rows, seq_count, width) for a in arrays]
+        joined = jnp.concatenate(parts, axis=2).transpose(1, 0, 2)
+        moved = lax.all_to_all(joined, "seq", split_axis=0, concat_axis=0, tiled=True)
+        return moved.reshape(patch_rows, len(arrays) * width)
 
     stale = interleaved([stale_key, stale_value])
     framed = with_halo(stale, (("patch", 0),), patch_rows)

time: 123 us -> 120 us (0.976)
  the two profiles are of different devices: /device:TPU:1 before, /device:TPU:128 now
where the time goes in v5:
time: 120 us
  Pallas kernels  41.9 us (35%)
  waiting for transfers between devices  38.6 us (32%)
  starting transfers between devices  15.2 us (13%)
  blocking collectives  15 us (12%)
  local copies, waits for them, and re-layouts  5.78 us (5%)
  other arithmetic  3.22 us (3%)
    pallas_call x2, Pallas kernels, tile_attention(): pl.pallas_call(functools.partial(attention_kernel, local_heads, per_patch...  41.9 us
    all_to_all x2, waiting for transfers between devices, interleaved(): lax.all_to_all(joined, 'seq', split_axis=0, concat_axis=0, tiled=True)  38.6 us
    all_to_all x1, blocking collectives, on_device(): lax.all_to_all(merged, 'seq', split_axis=0, concat_axis=1, tiled=True)  15 us
    all_to_all x2, starting transfers between devices, interleaved(): lax.all_to_all(joined, 'seq', split_axis=0, concat_axis=0, tiled=True)  10.9 us
    unnamed x16, local copies, waits for them, and re-layouts  3.33 us
    transpose x2, other arithmetic, interleaved(): joined = jnp.concatenate(parts, axis=2).transpose(1, 0, 2)  2.63 us
    ppermute x1, starting transfers between devices, with_halo(): before = lax.ppermute(last, axis, up)  2.41 us
  transfers between devices with their start and end apart: 4, of which 2 were waited for; matrix products, arithmetic and copies ran while one was open for 2% of the time, Pallas kernels for 12%

profile of v5, /device:TPU:128, one launch (start us, length us, event | category | flops | bytes accessed | tf_op | source)
XLA Modules:
  0.0 119.8 jit_solution(13155180484995412653)
XLA Ops:
  0.0 0.0 copy-start
  0.0 1.1 copy-done
  1.1 1.3 %copy_bitcast_fusion.1 = (bf16[144,16,128]{2,0,1:T(8,128)(2,1)S(1)}, bf16[144,16,128]{2,0,1:T(8,128)(2,1)S(1)}) fusion(bf16[144,2048]{1,0:T(8,128)(2,1)S(1)} %copy-done, bf16[144,2048]{1,0:T(8,128)(2,1)} %param.11), kind=kLoop, calls=%fused_computation.3 | loop fusion | bytes 2359296 | tf_op jit(solution)/shard_map/reshape | solution.py:140
  2.3 0.0 copy-start.4
  2.3 1.2 maximum_bitcast_fusion.1
  3.5 0.0 copy-start.5
  3.5 0.0 copy-start.6
  3.5 7.2 %all-to-all-start.1 = ((bf16[16,144,256]{2,1,0:T(8,128)(2,1)}), bf16[16,144,256]{2,1,0:T(8,128)(2,1)S(1)}, u32[]{:S(2)}, u32[]{:S(2)}) async-start(bf16[16,144,256]{2,1,0:T(8,128)(2,1)} %maximum_bitcast_fusion.1), calls=%async_computation.1 | async-start | bytes 2359296 | tf_op jit(solution)/shard_map/all_to_all | solution.py:142
  10.7 0.0 copy-done.4
  10.7 0.1 copy_bitcast_fusion.5
  10.8 0.0 copy-done.5
  10.8 0.0 copy-done.6
  10.8 0.2 copy_bitcast_fusion.3
  11.0 1.5 %maximum_bitcast_fusion = bf16[16,144,384]{2,1,0:T(8,128)(2,1)} fusion(bf16[144,16,128]{2,0,1:T(8,128)(2,1)S(1)} %get-tuple-element.9, bf16[144,16,128]{2,0,1:T(8,128)(2,1)S(1)} %get-tuple-element.10, bf16[144,16,128]{2,0,1:T(8,128)(2,1)S(1)} %copy_bitcast_fusion.5), kind=kLoop, calls=%fused_computation | loop fusion | flops 5308416 | bytes 3538944 | tf_op jit(solution)/shard_map/transpose | solution.py:141
  12.5 0.0 copy-start.7
  12.5 17.4 %all-to-all-done.1 = bf16[16,144,256]{2,1,0:T(8,128)(2,1)S(1)} async-done(((bf16[16,144,256]{2,1,0:T(8,128)(2,1)}), bf16[16,144,256]{2,1,0:T(8,128)(2,1)S(1)}, u32[]{:S(2)}, u32[]{:S(2)}) %all-to-all-start.1) | async-done | bytes 1179680 | tf_op jit(solution)/shard_map/all_to_all | solution.py:142
  29.9 0.0 copy-start.3
  29.9 3.7 %all-to-all-start = ((bf16[16,144,384]{2,1,0:T(8,128)(2,1)}), bf16[16,144,384]{2,1,0:T(8,128)(2,1)S(1)}, u32[]{:S(2)}, u32[]{:S(2)}) async-start(bf16[16,144,384]{2,1,0:T(8,128)(2,1)} %maximum_bitcast_fusion), calls=%async_computation | async-start | bytes 3538944 | tf_op jit(solution)/shard_map/all_to_all | solution.py:142
  33.6 0.0 copy-done.3
  33.6 1.9 %collective-permute-start.1 = (bf16[2304,256]{1,0:T(8,128)(2,1)}, bf16[2304,256]{1,0:T(8,128)(2,1)S(1)}, u32[]{:S(2)}, u32[]{:S(2)}) collective-permute-start(bf16[2304,256]{1,0:T(8,128)(2,1)} %bitcast.41), channel_id=1, source_target_pairs={{32,0},{64,32},{96,64},{128,96},{160,128},{192,160},{224,192},{33,... | collective-permute-start | bytes 3538952 | tf_op jit(solution)/shard_map/ppermute | solution.py:29
  35.6 2.4 %collective-permute-start = (bf16[2304,256]{1,0:T(8,128)(2,1)}, bf16[2304,256]{1,0:T(8,128)(2,1)}, u32[]{:S(2)}, u32[]{:S(2)}) collective-permute-start(bf16[2304,256]{1,0:T(8,128)(2,1)} %bitcast.42), channel_id=1, source_target_pairs={{0,32},{32,64},{64,96},{96,128},{128,160},{160,192},{192,224},{1,3... | collective-permute-start | bytes 3538952 | tf_op jit(solution)/shard_map/ppermute | solution.py:28
  38.0 0.0 copy-done.7
  38.0 0.6 broadcast_subtract_fusion.ids_ref
  38.6 21.2 %all-to-all-done = bf16[16,144,384]{2,1,0:T(8,128)(2,1)S(1)} async-done(((bf16[16,144,384]{2,1,0:T(8,128)(2,1)}), bf16[16,144,384]{2,1,0:T(8,128)(2,1)S(1)}, u32[]{:S(2)}, u32[]{:S(2)}) %all-to-all-start) | async-done | bytes 1769504 | tf_op jit(solution)/shard_map/all_to_all | solution.py:142
  59.8 0.0 copy-start.1
  59.8 1.2 %copy-done.1 = bf16[16,144,384]{2,1,0:T(8,128)(2,1)} copy-done((bf16[16,144,384]{2,1,0:T(8,128)(2,1)}, bf16[16,144,384]{2,1,0:T(8,128)(2,1)S(1)}, u32[]{:S(2)}) %copy-start.1) | copy-done | bytes 1769496
  61.0 14.4 %shard_map.73 = (f32[2304,128]{1,0:T(8,128)}, f32[2304,128]{1,0:T(8,128)}) custom-call(s32[6,18]{1,0:T(8,128)} %broadcast_subtract_fusion.ids_ref, s32[6]{0:T(128)} %count_ref.3, bf16[2304,384]{1,0:T(8,128)(2,1)} %bitcast.38), custom_call_target="tpu_custom_call" | custom-call | tf_op jit(solution)/shard_map/pallas_call | solution.py:108
  75.4 0.0 collective-permute-done.1.refs_1_
  75.4 0.0 copy-start.2
  75.4 0.0 collective-permute-done.refs_0_
  75.4 1.0 copy-done.2
  76.4 27.5 %shard_map.74 = bf16[2304,128]{1,0:T(8,128)(2,1)} custom-call(s32[6,18]{1,0:T(8,128)} %broadcast_subtract_fusion.ids_ref, s32[6]{0:T(128)} %count_ref.3, bf16[2304,384]{1,0:T(8,128)(2,1)} %bitcast.39, bf16[2304,256]{1,0:T(8,128)(2,1)} %collective-permute-done.refs_0_, bf16[2304,256]{1,0:T(8,128)(2,1)} %copy-done.2, f32[2304,128]{1,0:T(8,128)} %get-tuple-element.7.refs_2_, ...), custom_call_target="tpu_custom_call" | custom-call | tf_op jit(solution)/shard_map/pallas_call | solution.py:115
  103.9 15.0 %all_to_all.29 = bf16[16,144,128]{2,1,0:T(8,128)(2,1)S(1)} all-to-all(bf16[16,144,128]{2,1,0:T(8,128)(2,1)} %bitcast.40), channel_id=1, replica_groups=mesh['patch'=8,'seq'=16,'cfg'=2] {'seq'}, dimensions={0} | all-to-all | bytes 1179648 | tf_op jit(solution)/shard_map/all_to_all | solution.py:155
  118.9 0.9 copy_bitcast_fusion
Async XLA Ops:
  0.0 1.1 copy-start
  2.3 8.4 %copy-start.4 = (bf16[144,2048]{1,0:T(8,128)(2,1)S(1)}, bf16[144,2048]{1,0:T(8,128)(2,1)}, u32[]{:S(2)}) copy-start(bf16[144,2048]{1,0:T(8,128)(2,1)} %param.7) | copy-start | bytes 1769476
  3.5 7.3 %copy-start.5 = (bf16[144,2048]{1,0:T(8,128)(2,1)S(1)}, bf16[144,2048]{1,0:T(8,128)(2,1)}, u32[]{:S(2)}) copy-start(bf16[144,2048]{1,0:T(8,128)(2,1)} %param.8) | copy-start | bytes 1769476
  3.5 7.3 %copy-start.6 = (bf16[144,2048]{1,0:T(8,128)(2,1)S(1)}, bf16[144,2048]{1,0:T(8,128)(2,1)}, u32[]{:S(2)}) copy-start(bf16[144,2048]{1,0:T(8,128)(2,1)} %param.9) | copy-start | bytes 1769476
  3.5 26.4 %all-to-all-start.1 = ((bf16[16,144,256]{2,1,0:T(8,128)(2,1)}), bf16[16,144,256]{2,1,0:T(8,128)(2,1)S(1)}, u32[]{:S(2)}, u32[]{:S(2)}) async-start(bf16[16,144,256]{2,1,0:T(8,128)(2,1)} %maximum_bitcast_fusion.1), calls=%async_computation.1 | async-start | bytes 2359296 | tf_op jit(solution)/shard_map/all_to_all | solution.py:142
  12.5 25.5 %copy-start.7 = (s32[6,18]{1,0:T(8,128)S(1)}, s32[6,18]{1,0:T(8,128)}, u32[]{:S(2)}) copy-start(s32[6,18]{1,0:T(8,128)} %param.12) | copy-start | bytes 1300
  29.9 3.7 %copy-start.3 = (bf16[16,144,256]{2,1,0:T(8,128)(2,1)}, bf16[16,144,256]{2,1,0:T(8,128)(2,1)S(1)}, u32[]{:S(2)}) copy-start(bf16[16,144,256]{2,1,0:T(8,128)(2,1)S(1)} %all-to-all-done.1) | copy-start | bytes 3538948
  29.9 29.9 %all-to-all-start = ((bf16[16,144,384]{2,1,0:T(8,128)(2,1)}), bf16[16,144,384]{2,1,0:T(8,128)(2,1)S(1)}, u32[]{:S(2)}, u32[]{:S(2)}) async-start(bf16[16,144,384]{2,1,0:T(8,128)(2,1)} %maximum_bitcast_fusion), calls=%async_computation | async-start | bytes 3538944 | tf_op jit(solution)/shard_map/all_to_all | solution.py:142
  33.6 41.8 %collective-permute-start.1 = (bf16[2304,256]{1,0:T(8,128)(2,1)}, bf16[2304,256]{1,0:T(8,128)(2,1)S(1)}, u32[]{:S(2)}, u32[]{:S(2)}) collective-permute-start(bf16[2304,256]{1,0:T(8,128)(2,1)} %bitcast.41), channel_id=1, source_target_pairs={{32,0},{64,32},{96,64},{128,96},{160,128},{192,160},{224,192},{33,... | collective-permute-start | bytes 3538952 | tf_op jit(solution)/shard_map/ppermute | solution.py:29
  35.6 39.9 %collective-permute-start = (bf16[2304,256]{1,0:T(8,128)(2,1)}, bf16[2304,256]{1,0:T(8,128)(2,1)}, u32[]{:S(2)}, u32[]{:S(2)}) collective-permute-start(bf16[2304,256]{1,0:T(8,128)(2,1)} %bitcast.42), channel_id=1, source_target_pairs={{0,32},{32,64},{64,96},{96,128},{128,160},{160,192},{192,224},{1,3... | collective-permute-start | bytes 3538952 | tf_op jit(solution)/shard_map/ppermute | solution.py:28
  59.8 1.2 %copy-start.1 = (bf16[16,144,384]{2,1,0:T(8,128)(2,1)}, bf16[16,144,384]{2,1,0:T(8,128)(2,1)S(1)}, u32[]{:S(2)}) copy-start(bf16[16,144,384]{2,1,0:T(8,128)(2,1)S(1)} %all-to-all-done) | copy-start | bytes 5308420
  75.4 1.0 copy-start.2

commit v6 on v5

--- a/solution.py
+++ b/solution.py
@@ -33,12 +33,49 @@
 
 def attention_kernel(local_heads, per_patch, stale_phase, ids_ref, count_ref, fresh_ref, *refs):
     if stale_phase:
-        before_ref, after_ref, acc_in, tot_in, o_ref, acc_ref, tot_ref = refs
+        before_hbm, after_hbm, acc_in, tot_in, o_ref, stale_ref, copy_sem, list_ref, acc_ref, tot_ref = refs
+        keys_ref = stale_ref
     else:
-        acc_ref, tot_ref = refs
+        acc_ref, tot_ref, list_ref = refs
+        keys_ref = fresh_ref
     t = pl.program_id(0)
     width = local_heads * HEAD_DIM
+    patch_rows = fresh_ref.shape[0]
     factor = 1.0 / (HEAD_DIM**0.5) / soft_cap
+    lift = soft_cap * 1.4426950408889634
+
+    if stale_phase:
+
+        @pl.when(t == 0)
+        def _():
+            first = pltpu.make_async_copy(before_hbm, stale_ref.at[pl.ds(0, patch_rows)], copy_sem.at[0])
+            second = pltpu.make_async_copy(
+                after_hbm, stale_ref.at[pl.ds(patch_rows, patch_rows)], copy_sem.at[1]
+            )
+            first.start()
+            second.start()
+            first.wait()
+            second.wait()
+
+    def compact(j, n):
+        u = ids_ref[t, j]
+        which = u // per_patch
+        row = u - which * per_patch
+        if stale_phase:
+            keep = which != 1
+            index = (which // 2) * per_patch + row
+        else:
+            keep = which == 1
+            index = row
+
+        @pl.when(keep)
+        def _():
+            list_ref[n] = index
+
+        return n + keep.astype(jnp.int32)
+
+    used = lax.fori_loop(0, count_ref[t], compact, jnp.int32(0))
+
     for h in range(local_heads):
         head = pl.ds(h * HEAD_DIM, HEAD_DIM)
         start_q = pl.multiple_of(t * TILE_TOKENS, TILE_TOKENS)
@@ -46,50 +83,48 @@
         if stale_phase:
             acc_ref[...] = acc_in[:, head]
             tot_ref[...] = tot_in[:, head]
+            k_col, v_col = h * HEAD_DIM, width + h * HEAD_DIM
         else:
             acc_ref[:, head] = jnp.zeros((TILE_TOKENS, HEAD_DIM), jnp.float32)
             tot_ref[:, head] = jnp.zeros((TILE_TOKENS, HEAD_DIM), jnp.float32)
+            k_col, v_col = width + h * HEAD_DIM, 2 * width + h * HEAD_DIM
         acc_at = slice(None) if stale_phase else head
 
-        def accumulate(ref, k_col, v_col, row):
-            start = pl.multiple_of(row * TILE_TOKENS, TILE_TOKENS)
-            keys = ref[pl.ds(start, TILE_TOKENS), pl.ds(k_col, HEAD_DIM)]
-            values = ref[pl.ds(start, TILE_TOKENS), pl.ds(v_col, HEAD_DIM)]
+        def weights(index):
+            start = pl.multiple_of(index * TILE_TOKENS, TILE_TOKENS)
+            keys = keys_ref[pl.ds(start, TILE_TOKENS), pl.ds(k_col, HEAD_DIM)]
+            values = keys_ref[pl.ds(start, TILE_TOKENS), pl.ds(v_col, HEAD_DIM)]
             scores = lax.dot_general(
                 query, keys, (((1,), (1,)), ((), ())), preferred_element_type=jnp.float32
             )
-            weight = jnp.exp(soft_cap * jnp.tanh(scores * factor) - soft_cap)
+            weight = jnp.exp2(jnp.tanh(scores * factor) * lift - lift)
             part = weight[:, 0:HEAD_DIM]
             for c in range(1, TILE_TOKENS // HEAD_DIM):
                 part = part + weight[:, c * HEAD_DIM:(c + 1) * HEAD_DIM]
+            return weight.astype(jnp.bfloat16), part, values
+
+        def accumulate(indices):
+            got = [weights(i) for i in indices]
+            part = got[0][1]
+            for g in got[1:]:
+                part = part + g[1]
             tot_ref[:, acc_at] += part
             acc_ref[:, acc_at] += jnp.dot(
-                weight.astype(jnp.bfloat16), values, preferred_element_type=jnp.float32
+                jnp.concatenate([g[0] for g in got], axis=1),
+                jnp.concatenate([g[2] for g in got], axis=0),
+                preferred_element_type=jnp.float32,
             )
 
-        def body(j, carry):
-            u = ids_ref[t, j]
-            which = u // per_patch
-            row = u - which * per_patch
-            if stale_phase:
-                stale_k, stale_v = h * HEAD_DIM, width + h * HEAD_DIM
-
-                @pl.when(which == 0)
-                def _():
-                    accumulate(before_ref, stale_k, stale_v, row)
-
-                @pl.when(which == 2)
-                def _():
-                    accumulate(after_ref, stale_k, stale_v, row)
-            else:
-
-                @pl.when(which == 1)
-                def _():
-                    accumulate(fresh_ref, width + h * HEAD_DIM, 2 * width + h * HEAD_DIM, row)
-
+        def two(p, carry):
+            accumulate([list_ref[2 * p], list_ref[2 * p + 1]])
             return carry
 
-        lax.fori_loop(0, count_ref[t], body, 0)
+        lax.fori_loop(0, used // 2, two, 0)
+
+        @pl.when(used % 2 == 1)
+        def _():
+            accumulate([list_ref[used - 1]])
+
         if stale_phase:
             total = jnp.sum(tot_ref[...], axis=1, keepdims=True)
             o_ref[:, head] = (acc_ref[...] / total).astype(o_ref.dtype)
@@ -109,22 +144,31 @@
         functools.partial(attention_kernel, local_heads, per_patch, False),
         out_shape=(partial, partial),
         grid_spec=pltpu.PrefetchScalarGridSpec(
-            num_scalar_prefetch=2, grid=(tiles,), in_specs=[whole(fresh)], out_specs=(tile, tile),
+            num_scalar_prefetch=2,
+            grid=(tiles,),
+            in_specs=[whole(fresh)],
+            out_specs=(tile, tile),
+            scratch_shapes=[pltpu.SMEM((KEY_SLOTS,), jnp.int32)],
         ),
     )(local_ids, tile_count, fresh)
+    hbm = pl.BlockSpec(memory_space=pl.ANY)
     return pl.pallas_call(
         functools.partial(attention_kernel, local_heads, per_patch, True),
         out_shape=jax.ShapeDtypeStruct((rows, width), jnp.bfloat16),
         grid_spec=pltpu.PrefetchScalarGridSpec(
             num_scalar_prefetch=2,
             grid=(tiles,),
-            in_specs=[whole(fresh), whole(before), whole(after), tile, tile],
+            in_specs=[whole(fresh), hbm, hbm, tile, tile],
             out_specs=tile,
             scratch_shapes=[
+                pltpu.VMEM((2 * rows, before.shape[1]), before.dtype),
+                pltpu.SemaphoreType.DMA((2,)),
+                pltpu.SMEM((KEY_SLOTS,), jnp.int32),
                 pltpu.VMEM((TILE_TOKENS, HEAD_DIM), jnp.float32),
                 pltpu.VMEM((TILE_TOKENS, HEAD_DIM), jnp.float32),
             ],
         ),
+        compiler_params=pltpu.CompilerParams(dimension_semantics=("arbitrary",)),
     )(local_ids, tile_count, fresh, before, after, acc, tot)
 
 

time: 120 us -> 113 us (0.942); the launches traced: 120 us -> 111 us
  Pallas kernels: 41.9 us -> 31.8 us
  blocking collectives: 15 us -> 16.5 us
    pallas_call x2, Pallas kernels: 41.9 us -> 31.8 us  [tile_attention(): pl.pallas_call(functools.partial(attention_kernel, local_heads, per_patch...]
    all_to_all x1, blocking collectives: 15 us -> 16.5 us  [on_device(): lax.all_to_all(merged, 'seq', split_axis=0, concat_axis=1, tiled=True)]
  transfers between devices with their start and end apart: 4 -> 4, of which waited for: 2 -> 2; matrix products, arithmetic and copies ran while one was open for 2% -> 2% of each run, Pallas kernels for 12% -> 11%
where the time goes in v6:
time: 113 us; the launch traced here: 111 us
  waiting for transfers between devices  38.6 us (34%)
  Pallas kernels  31.8 us (28%)
  blocking collectives  16.5 us (15%)
  starting transfers between devices  15.2 us (13%)
  local copies, waits for them, and re-layouts  5.78 us (5%)
  other arithmetic  3.22 us (3%)
    all_to_all x2, waiting for transfers between devices, interleaved(): lax.all_to_all(joined, 'seq', split_axis=0, concat_axis=0, tiled=True)  38.6 us
    pallas_call x2, Pallas kernels, tile_attention(): pl.pallas_call(functools.partial(attention_kernel, local_heads, per_patch...  31.8 us
    all_to_all x1, blocking collectives, on_device(): lax.all_to_all(merged, 'seq', split_axis=0, concat_axis=1, tiled=True)  16.5 us
    all_to_all x2, starting transfers between devices, interleaved(): lax.all_to_all(joined, 'seq', split_axis=0, concat_axis=0, tiled=True)  10.9 us
    unnamed x16, local copies, waits for them, and re-layouts  3.33 us
    transpose x2, other arithmetic, interleaved(): joined = jnp.concatenate(parts, axis=2).transpose(1, 0, 2)  2.63 us
    ppermute x1, starting transfers between devices, with_halo(): before = lax.ppermute(last, axis, up)  2.41 us
  transfers between devices with their start and end apart: 4, of which 2 were waited for; matrix products, arithmetic and copies ran while one was open for 2% of the time, Pallas kernels for 11%

profile of v6, /device:TPU:128, one launch (start us, length us, event | category | flops | bytes accessed | tf_op | source)
XLA Modules:
  0.0 111.3 jit_solution(12702002011832818180)
XLA Ops:
  0.0 0.0 copy-start
  0.0 1.1 copy-done
  1.1 1.3 %copy_bitcast_fusion.1 = (bf16[144,16,128]{2,0,1:T(8,128)(2,1)S(1)}, bf16[144,16,128]{2,0,1:T(8,128)(2,1)S(1)}) fusion(bf16[144,2048]{1,0:T(8,128)(2,1)S(1)} %copy-done, bf16[144,2048]{1,0:T(8,128)(2,1)} %param.11), kind=kLoop, calls=%fused_computation.3 | loop fusion | bytes 2359296 | tf_op jit(solution)/shard_map/reshape | solution.py:184
  2.3 0.0 copy-start.4
  2.3 1.2 %maximum_bitcast_fusion.1 = bf16[16,144,256]{2,1,0:T(8,128)(2,1)} fusion(bf16[144,16,128]{2,0,1:T(8,128)(2,1)S(1)} %get-tuple-element.11, bf16[144,16,128]{2,0,1:T(8,128)(2,1)S(1)} %get-tuple-element.12), kind=kLoop, calls=%fused_computation.1 | loop fusion | flops 2359296 | bytes 2359296 | tf_op jit(solution)/shard_map/transpose | solution.py:185
  3.5 0.0 copy-start.5
  3.5 0.0 copy-start.6
  3.5 7.2 %all-to-all-start.1 = ((bf16[16,144,256]{2,1,0:T(8,128)(2,1)}), bf16[16,144,256]{2,1,0:T(8,128)(2,1)S(1)}, u32[]{:S(2)}, u32[]{:S(2)}) async-start(bf16[16,144,256]{2,1,0:T(8,128)(2,1)} %maximum_bitcast_fusion.1), calls=%async_computation.1 | async-start | bytes 2359296 | tf_op jit(solution)/shard_map/all_to_all | solution.py:186
  10.7 0.0 copy-done.4
  10.7 0.1 copy_bitcast_fusion.5
  10.8 0.0 copy-done.5
  10.8 0.0 copy-done.6
  10.8 0.2 copy_bitcast_fusion.3
  11.0 1.5 %maximum_bitcast_fusion = bf16[16,144,384]{2,1,0:T(8,128)(2,1)} fusion(bf16[144,16,128]{2,0,1:T(8,128)(2,1)S(1)} %get-tuple-element.9, bf16[144,16,128]{2,0,1:T(8,128)(2,1)S(1)} %get-tuple-element.10, bf16[144,16,128]{2,0,1:T(8,128)(2,1)S(1)} %copy_bitcast_fusion.5), kind=kLoop, calls=%fused_computation | loop fusion | flops 5308416 | bytes 3538944 | tf_op jit(solution)/shard_map/transpose | solution.py:185
  12.5 0.0 copy-start.7
  12.5 17.4 %all-to-all-done.1 = bf16[16,144,256]{2,1,0:T(8,128)(2,1)S(1)} async-done(((bf16[16,144,256]{2,1,0:T(8,128)(2,1)}), bf16[16,144,256]{2,1,0:T(8,128)(2,1)S(1)}, u32[]{:S(2)}, u32[]{:S(2)}) %all-to-all-start.1) | async-done | bytes 1179680 | tf_op jit(solution)/shard_map/all_to_all | solution.py:186
  29.9 0.0 copy-start.3
  29.9 3.7 %all-to-all-start = ((bf16[16,144,384]{2,1,0:T(8,128)(2,1)}), bf16[16,144,384]{2,1,0:T(8,128)(2,1)S(1)}, u32[]{:S(2)}, u32[]{:S(2)}) async-start(bf16[16,144,384]{2,1,0:T(8,128)(2,1)} %maximum_bitcast_fusion), calls=%async_computation | async-start | bytes 3538944 | tf_op jit(solution)/shard_map/all_to_all | solution.py:186
  33.6 0.0 copy-done.3
  33.6 1.9 %collective-permute-start.1 = (bf16[2304,256]{1,0:T(8,128)(2,1)}, bf16[2304,256]{1,0:T(8,128)(2,1)S(1)}, u32[]{:S(2)}, u32[]{:S(2)}) collective-permute-start(bf16[2304,256]{1,0:T(8,128)(2,1)} %bitcast.41), channel_id=1, source_target_pairs={{32,0},{64,32},{96,64},{128,96},{160,128},{192,160},{224,192},{33,... | collective-permute-start | bytes 3538952 | tf_op jit(solution)/shard_map/ppermute | solution.py:29
  35.6 2.4 %collective-permute-start = (bf16[2304,256]{1,0:T(8,128)(2,1)}, bf16[2304,256]{1,0:T(8,128)(2,1)}, u32[]{:S(2)}, u32[]{:S(2)}) collective-permute-start(bf16[2304,256]{1,0:T(8,128)(2,1)} %bitcast.42), channel_id=1, source_target_pairs={{0,32},{32,64},{64,96},{96,128},{128,160},{160,192},{192,224},{1,3... | collective-permute-start | bytes 3538952 | tf_op jit(solution)/shard_map/ppermute | solution.py:28
  38.0 0.0 copy-done.7
  38.0 0.6 broadcast_subtract_fusion.ids_ref
  38.6 21.2 %all-to-all-done = bf16[16,144,384]{2,1,0:T(8,128)(2,1)S(1)} async-done(((bf16[16,144,384]{2,1,0:T(8,128)(2,1)}), bf16[16,144,384]{2,1,0:T(8,128)(2,1)S(1)}, u32[]{:S(2)}, u32[]{:S(2)}) %all-to-all-start) | async-done | bytes 1769504 | tf_op jit(solution)/shard_map/all_to_all | solution.py:186
  59.8 0.0 copy-start.1
  59.8 1.2 %copy-done.1 = bf16[16,144,384]{2,1,0:T(8,128)(2,1)} copy-done((bf16[16,144,384]{2,1,0:T(8,128)(2,1)}, bf16[16,144,384]{2,1,0:T(8,128)(2,1)S(1)}, u32[]{:S(2)}) %copy-start.1) | copy-done | bytes 1769496
  61.0 11.7 %shard_map.73 = (f32[2304,128]{1,0:T(8,128)}, f32[2304,128]{1,0:T(8,128)}) custom-call(s32[6,18]{1,0:T(8,128)} %broadcast_subtract_fusion.ids_ref, s32[6]{0:T(128)} %count_ref.3, bf16[2304,384]{1,0:T(8,128)(2,1)} %bitcast.38), custom_call_target="tpu_custom_call" | custom-call | tf_op jit(solution)/shard_map/pallas_call | solution.py:143
  72.7 0.0 collective-permute-done.1.refs_1_
  72.7 0.0 copy-start.2
  72.7 0.0 collective-permute-done.refs_0_
  72.7 1.0 copy-done.2
  73.8 20.1 %shard_map.74 = bf16[2304,128]{1,0:T(8,128)(2,1)} custom-call(s32[6,18]{1,0:T(8,128)} %broadcast_subtract_fusion.ids_ref, s32[6]{0:T(128)} %count_ref.3, bf16[2304,384]{1,0:T(8,128)(2,1)} %bitcast.39, bf16[2304,256]{1,0:T(8,128)(2,1)} %collective-permute-done.refs_0_, bf16[2304,256]{1,0:T(8,128)(2,1)} %copy-done.2, f32[2304,128]{1,0:T(8,128)} %get-tuple-element.7.refs_2_, ...), custom_call_target="tpu_custom_call" | custom-call | tf_op jit(solution)/shard_map/pallas_call | solution.py:155
  93.9 16.5 %all_to_all.29 = bf16[16,144,128]{2,1,0:T(8,128)(2,1)S(1)} all-to-all(bf16[16,144,128]{2,1,0:T(8,128)(2,1)} %bitcast.40), channel_id=1, replica_groups=mesh['patch'=8,'seq'=16,'cfg'=2] {'seq'}, dimensions={0} | all-to-all | bytes 1179648 | tf_op jit(solution)/shard_map/all_to_all | solution.py:199
  110.4 0.9 copy_bitcast_fusion
Async XLA Ops:
  0.0 1.1 copy-start
  2.3 8.4 %copy-start.4 = (bf16[144,2048]{1,0:T(8,128)(2,1)S(1)}, bf16[144,2048]{1,0:T(8,128)(2,1)}, u32[]{:S(2)}) copy-start(bf16[144,2048]{1,0:T(8,128)(2,1)} %param.7) | copy-start | bytes 1769476
  3.5 7.3 %copy-start.5 = (bf16[144,2048]{1,0:T(8,128)(2,1)S(1)}, bf16[144,2048]{1,0:T(8,128)(2,1)}, u32[]{:S(2)}) copy-start(bf16[144,2048]{1,0:T(8,128)(2,1)} %param.8) | copy-start | bytes 1769476
  3.5 7.3 %copy-start.6 = (bf16[144,2048]{1,0:T(8,128)(2,1)S(1)}, bf16[144,2048]{1,0:T(8,128)(2,1)}, u32[]{:S(2)}) copy-start(bf16[144,2048]{1,0:T(8,128)(2,1)} %param.9) | copy-start | bytes 1769476
  3.5 26.4 %all-to-all-start.1 = ((bf16[16,144,256]{2,1,0:T(8,128)(2,1)}), bf16[16,144,256]{2,1,0:T(8,128)(2,1)S(1)}, u32[]{:S(2)}, u32[]{:S(2)}) async-start(bf16[16,144,256]{2,1,0:T(8,128)(2,1)} %maximum_bitcast_fusion.1), calls=%async_computation.1 | async-start | bytes 2359296 | tf_op jit(solution)/shard_map/all_to_all | solution.py:186
  12.5 25.5 %copy-start.7 = (s32[6,18]{1,0:T(8,128)S(1)}, s32[6,18]{1,0:T(8,128)}, u32[]{:S(2)}) copy-start(s32[6,18]{1,0:T(8,128)} %param.12) | copy-start | bytes 1300
  29.9 3.7 %copy-start.3 = (bf16[16,144,256]{2,1,0:T(8,128)(2,1)}, bf16[16,144,256]{2,1,0:T(8,128)(2,1)S(1)}, u32[]{:S(2)}) copy-start(bf16[16,144,256]{2,1,0:T(8,128)(2,1)S(1)} %all-to-all-done.1) | copy-start | bytes 3538948
  29.9 29.9 %all-to-all-start = ((bf16[16,144,384]{2,1,0:T(8,128)(2,1)}), bf16[16,144,384]{2,1,0:T(8,128)(2,1)S(1)}, u32[]{:S(2)}, u32[]{:S(2)}) async-start(bf16[16,144,384]{2,1,0:T(8,128)(2,1)} %maximum_bitcast_fusion), calls=%async_computation | async-start | bytes 3538944 | tf_op jit(solution)/shard_map/all_to_all | solution.py:186
  33.6 39.1 %collective-permute-start.1 = (bf16[2304,256]{1,0:T(8,128)(2,1)}, bf16[2304,256]{1,0:T(8,128)(2,1)S(1)}, u32[]{:S(2)}, u32[]{:S(2)}) collective-permute-start(bf16[2304,256]{1,0:T(8,128)(2,1)} %bitcast.41), channel_id=1, source_target_pairs={{32,0},{64,32},{96,64},{128,96},{160,128},{192,160},{224,192},{33,... | collective-permute-start | bytes 3538952 | tf_op jit(solution)/shard_map/ppermute | solution.py:29
  35.6 37.2 %collective-permute-start = (bf16[2304,256]{1,0:T(8,128)(2,1)}, bf16[2304,256]{1,0:T(8,128)(2,1)}, u32[]{:S(2)}, u32[]{:S(2)}) collective-permute-start(bf16[2304,256]{1,0:T(8,128)(2,1)} %bitcast.42), channel_id=1, source_target_pairs={{0,32},{32,64},{64,96},{96,128},{128,160},{160,192},{192,224},{1,3... | collective-permute-start | bytes 3538952 | tf_op jit(solution)/shard_map/ppermute | solution.py:28
  59.8 1.2 %copy-start.1 = (bf16[16,144,384]{2,1,0:T(8,128)(2,1)}, bf16[16,144,384]{2,1,0:T(8,128)(2,1)S(1)}, u32[]{:S(2)}) copy-start(bf16[16,144,384]{2,1,0:T(8,128)(2,1)S(1)} %all-to-all-done) | copy-start | bytes 5308420
  72.7 1.0 copy-start.2

commit v7 on v6

--- a/solution.py
+++ b/solution.py
@@ -13,6 +13,7 @@
 TILES_H = 2
 TILES_W = 3
 KEY_SLOTS = 18
+SLOT_GROUP = 3
 
 
 soft_cap = 8.0
@@ -115,15 +116,16 @@
                 preferred_element_type=jnp.float32,
             )
 
-        def two(p, carry):
-            accumulate([list_ref[2 * p], list_ref[2 * p + 1]])
+        def group(p, carry):
+            accumulate([list_ref[SLOT_GROUP * p + i] for i in range(SLOT_GROUP)])
             return carry
 
-        lax.fori_loop(0, used // 2, two, 0)
-
-        @pl.when(used % 2 == 1)
-        def _():
-            accumulate([list_ref[used - 1]])
+        lax.fori_loop(0, used // SLOT_GROUP, group, 0)
+        for left in range(1, SLOT_GROUP):
+
+            @pl.when(used % SLOT_GROUP == left)
+            def _():
+                accumulate([list_ref[used - left + i] for i in range(left)])
 
         if stale_phase:
             total = jnp.sum(tot_ref[...], axis=1, keepdims=True)

time: 113 us -> 110 us (0.973); the launches traced: 111 us -> 110 us
  blocking collectives: 16.5 us -> 14.9 us
    all_to_all x1, blocking collectives: 16.5 us -> 14.9 us  [on_device(): lax.all_to_all(merged, 'seq', split_axis=0, concat_axis=1, tiled=True)]
where the time goes in v7:
time: 110 us
  waiting for transfers between devices  38.6 us (35%)
  Pallas kernels  32.3 us (29%)
  starting transfers between devices  15.2 us (14%)
  blocking collectives  14.9 us (14%)
  local copies, waits for them, and re-layouts  5.78 us (5%)
  other arithmetic  3.22 us (3%)
    all_to_all x2, waiting for transfers between devices, interleaved(): lax.all_to_all(joined, 'seq', split_axis=0, concat_axis=0, tiled=True)  38.6 us
    pallas_call x2, Pallas kernels, tile_attention(): pl.pallas_call(functools.partial(attention_kernel, local_heads, per_patch...  32.3 us
    all_to_all x1, blocking collectives, on_device(): lax.all_to_all(merged, 'seq', split_axis=0, concat_axis=1, tiled=True)  14.9 us
    all_to_all x2, starting transfers between devices, interleaved(): lax.all_to_all(joined, 'seq', split_axis=0, concat_axis=0, tiled=True)  10.9 us
    unnamed x16, local copies, waits for them, and re-layouts  3.33 us
    transpose x2, other arithmetic, interleaved(): joined = jnp.concatenate(parts, axis=2).transpose(1, 0, 2)  2.63 us
    ppermute x1, starting transfers between devices, with_halo(): before = lax.ppermute(last, axis, up)  2.41 us
  transfers between devices with their start and end apart: 4, of which 2 were waited for; matrix products, arithmetic and copies ran while one was open for 2% of the time, Pallas kernels for 11%

profile of v7, /device:TPU:128, one launch (start us, length us, event | category | flops | bytes accessed | tf_op | source)
XLA Modules:
  0.0 110.1 jit_solution(4510586464702353589)
XLA Ops:
  0.0 0.0 copy-start
  0.0 1.1 copy-done
  1.1 1.3 %copy_bitcast_fusion.1 = (bf16[144,16,128]{2,0,1:T(8,128)(2,1)S(1)}, bf16[144,16,128]{2,0,1:T(8,128)(2,1)S(1)}) fusion(bf16[144,2048]{1,0:T(8,128)(2,1)S(1)} %copy-done, bf16[144,2048]{1,0:T(8,128)(2,1)} %param.11), kind=kLoop, calls=%fused_computation.3 | loop fusion | bytes 2359296 | tf_op jit(solution)/shard_map/reshape | solution.py:186
  2.3 0.0 copy-start.4
  2.3 1.2 %maximum_bitcast_fusion.1 = bf16[16,144,256]{2,1,0:T(8,128)(2,1)} fusion(bf16[144,16,128]{2,0,1:T(8,128)(2,1)S(1)} %get-tuple-element.11, bf16[144,16,128]{2,0,1:T(8,128)(2,1)S(1)} %get-tuple-element.12), kind=kLoop, calls=%fused_computation.1 | loop fusion | flops 2359296 | bytes 2359296 | tf_op jit(solution)/shard_map/transpose | solution.py:187
  3.5 0.0 copy-start.5
  3.5 0.0 copy-start.6
  3.5 7.2 %all-to-all-start.1 = ((bf16[16,144,256]{2,1,0:T(8,128)(2,1)}), bf16[16,144,256]{2,1,0:T(8,128)(2,1)S(1)}, u32[]{:S(2)}, u32[]{:S(2)}) async-start(bf16[16,144,256]{2,1,0:T(8,128)(2,1)} %maximum_bitcast_fusion.1), calls=%async_computation.1 | async-start | bytes 2359296 | tf_op jit(solution)/shard_map/all_to_all | solution.py:188
  10.7 0.0 copy-done.4
  10.7 0.1 copy_bitcast_fusion.5
  10.8 0.0 copy-done.5
  10.8 0.0 copy-done.6
  10.8 0.2 copy_bitcast_fusion.3
  11.0 1.5 %maximum_bitcast_fusion = bf16[16,144,384]{2,1,0:T(8,128)(2,1)} fusion(bf16[144,16,128]{2,0,1:T(8,128)(2,1)S(1)} %get-tuple-element.9, bf16[144,16,128]{2,0,1:T(8,128)(2,1)S(1)} %get-tuple-element.10, bf16[144,16,128]{2,0,1:T(8,128)(2,1)S(1)} %copy_bitcast_fusion.5), kind=kLoop, calls=%fused_computation | loop fusion | flops 5308416 | bytes 3538944 | tf_op jit(solution)/shard_map/transpose | solution.py:187
  12.5 0.0 copy-start.7
  12.5 17.4 %all-to-all-done.1 = bf16[16,144,256]{2,1,0:T(8,128)(2,1)S(1)} async-done(((bf16[16,144,256]{2,1,0:T(8,128)(2,1)}), bf16[16,144,256]{2,1,0:T(8,128)(2,1)S(1)}, u32[]{:S(2)}, u32[]{:S(2)}) %all-to-all-start.1) | async-done | bytes 1179680 | tf_op jit(solution)/shard_map/all_to_all | solution.py:188
  29.9 0.0 copy-start.3
  29.9 3.7 %all-to-all-start = ((bf16[16,144,384]{2,1,0:T(8,128)(2,1)}), bf16[16,144,384]{2,1,0:T(8,128)(2,1)S(1)}, u32[]{:S(2)}, u32[]{:S(2)}) async-start(bf16[16,144,384]{2,1,0:T(8,128)(2,1)} %maximum_bitcast_fusion), calls=%async_computation | async-start | bytes 3538944 | tf_op jit(solution)/shard_map/all_to_all | solution.py:188
  33.6 0.0 copy-done.3
  33.6 1.9 %collective-permute-start.1 = (bf16[2304,256]{1,0:T(8,128)(2,1)}, bf16[2304,256]{1,0:T(8,128)(2,1)S(1)}, u32[]{:S(2)}, u32[]{:S(2)}) collective-permute-start(bf16[2304,256]{1,0:T(8,128)(2,1)} %bitcast.41), channel_id=1, source_target_pairs={{32,0},{64,32},{96,64},{128,96},{160,128},{192,160},{224,192},{33,... | collective-permute-start | bytes 3538952 | tf_op jit(solution)/shard_map/ppermute | solution.py:30
  35.6 2.4 %collective-permute-start = (bf16[2304,256]{1,0:T(8,128)(2,1)}, bf16[2304,256]{1,0:T(8,128)(2,1)}, u32[]{:S(2)}, u32[]{:S(2)}) collective-permute-start(bf16[2304,256]{1,0:T(8,128)(2,1)} %bitcast.42), channel_id=1, source_target_pairs={{0,32},{32,64},{64,96},{96,128},{128,160},{160,192},{192,224},{1,3... | collective-permute-start | bytes 3538952 | tf_op jit(solution)/shard_map/ppermute | solution.py:29
  38.0 0.0 copy-done.7
  38.0 0.6 broadcast_subtract_fusion.ids_ref
  38.6 21.2 %all-to-all-done = bf16[16,144,384]{2,1,0:T(8,128)(2,1)S(1)} async-done(((bf16[16,144,384]{2,1,0:T(8,128)(2,1)}), bf16[16,144,384]{2,1,0:T(8,128)(2,1)S(1)}, u32[]{:S(2)}, u32[]{:S(2)}) %all-to-all-start) | async-done | bytes 1769504 | tf_op jit(solution)/shard_map/all_to_all | solution.py:188
  59.8 0.0 copy-start.1
  59.8 1.2 %copy-done.1 = bf16[16,144,384]{2,1,0:T(8,128)(2,1)} copy-done((bf16[16,144,384]{2,1,0:T(8,128)(2,1)}, bf16[16,144,384]{2,1,0:T(8,128)(2,1)S(1)}, u32[]{:S(2)}) %copy-start.1) | copy-done | bytes 1769496
  61.0 12.3 %shard_map.73 = (f32[2304,128]{1,0:T(8,128)}, f32[2304,128]{1,0:T(8,128)}) custom-call(s32[6,18]{1,0:T(8,128)} %broadcast_subtract_fusion.ids_ref, s32[6]{0:T(128)} %count_ref.3, bf16[2304,384]{1,0:T(8,128)(2,1)} %bitcast.38), custom_call_target="tpu_custom_call" | custom-call | tf_op jit(solution)/shard_map/pallas_call | solution.py:145
  73.4 0.0 collective-permute-done.1.refs_1_
  73.4 0.0 copy-start.2
  73.4 0.0 collective-permute-done.refs_0_
  73.4 1.0 copy-done.2
  74.4 20.0 %shard_map.74 = bf16[2304,128]{1,0:T(8,128)(2,1)} custom-call(s32[6,18]{1,0:T(8,128)} %broadcast_subtract_fusion.ids_ref, s32[6]{0:T(128)} %count_ref.3, bf16[2304,384]{1,0:T(8,128)(2,1)} %bitcast.39, bf16[2304,256]{1,0:T(8,128)(2,1)} %collective-permute-done.refs_0_, bf16[2304,256]{1,0:T(8,128)(2,1)} %copy-done.2, f32[2304,128]{1,0:T(8,128)} %get-tuple-element.7.refs_2_, ...), custom_call_target="tpu_custom_call" | custom-call | tf_op jit(solution)/shard_map/pallas_call | solution.py:157
  94.4 14.9 %all_to_all.29 = bf16[16,144,128]{2,1,0:T(8,128)(2,1)S(1)} all-to-all(bf16[16,144,128]{2,1,0:T(8,128)(2,1)} %bitcast.40), channel_id=1, replica_groups=mesh['patch'=8,'seq'=16,'cfg'=2] {'seq'}, dimensions={0} | all-to-all | bytes 1179648 | tf_op jit(solution)/shard_map/all_to_all | solution.py:201
  109.2 0.9 copy_bitcast_fusion
Async XLA Ops:
  0.0 1.1 copy-start
  2.3 8.4 %copy-start.4 = (bf16[144,2048]{1,0:T(8,128)(2,1)S(1)}, bf16[144,2048]{1,0:T(8,128)(2,1)}, u32[]{:S(2)}) copy-start(bf16[144,2048]{1,0:T(8,128)(2,1)} %param.7) | copy-start | bytes 1769476
  3.5 7.3 %copy-start.5 = (bf16[144,2048]{1,0:T(8,128)(2,1)S(1)}, bf16[144,2048]{1,0:T(8,128)(2,1)}, u32[]{:S(2)}) copy-start(bf16[144,2048]{1,0:T(8,128)(2,1)} %param.8) | copy-start | bytes 1769476
  3.5 7.3 %copy-start.6 = (bf16[144,2048]{1,0:T(8,128)(2,1)S(1)}, bf16[144,2048]{1,0:T(8,128)(2,1)}, u32[]{:S(2)}) copy-start(bf16[144,2048]{1,0:T(8,128)(2,1)} %param.9) | copy-start | bytes 1769476
  3.5 26.4 %all-to-all-start.1 = ((bf16[16,144,256]{2,1,0:T(8,128)(2,1)}), bf16[16,144,256]{2,1,0:T(8,128)(2,1)S(1)}, u32[]{:S(2)}, u32[]{:S(2)}) async-start(bf16[16,144,256]{2,1,0:T(8,128)(2,1)} %maximum_bitcast_fusion.1), calls=%async_computation.1 | async-start | bytes 2359296 | tf_op jit(solution)/shard_map/all_to_all | solution.py:188
  12.5 25.5 %copy-start.7 = (s32[6,18]{1,0:T(8,128)S(1)}, s32[6,18]{1,0:T(8,128)}, u32[]{:S(2)}) copy-start(s32[6,18]{1,0:T(8,128)} %param.12) | copy-start | bytes 1300
  29.9 3.7 %copy-start.3 = (bf16[16,144,256]{2,1,0:T(8,128)(2,1)}, bf16[16,144,256]{2,1,0:T(8,128)(2,1)S(1)}, u32[]{:S(2)}) copy-start(bf16[16,144,256]{2,1,0:T(8,128)(2,1)S(1)} %all-to-all-done.1) | copy-start | bytes 3538948
  29.9 29.9 %all-to-all-start = ((bf16[16,144,384]{2,1,0:T(8,128)(2,1)}), bf16[16,144,384]{2,1,0:T(8,128)(2,1)S(1)}, u32[]{:S(2)}, u32[]{:S(2)}) async-start(bf16[16,144,384]{2,1,0:T(8,128)(2,1)} %maximum_bitcast_fusion), calls=%async_computation | async-start | bytes 3538944 | tf_op jit(solution)/shard_map/all_to_all | solution.py:188
  33.6 39.7 %collective-permute-start.1 = (bf16[2304,256]{1,0:T(8,128)(2,1)}, bf16[2304,256]{1,0:T(8,128)(2,1)S(1)}, u32[]{:S(2)}, u32[]{:S(2)}) collective-permute-start(bf16[2304,256]{1,0:T(8,128)(2,1)} %bitcast.41), channel_id=1, source_target_pairs={{32,0},{64,32},{96,64},{128,96},{160,128},{192,160},{224,192},{33,... | collective-permute-start | bytes 3538952 | tf_op jit(solution)/shard_map/ppermute | solution.py:30
  35.6 37.8 %collective-permute-start = (bf16[2304,256]{1,0:T(8,128)(2,1)}, bf16[2304,256]{1,0:T(8,128)(2,1)}, u32[]{:S(2)}, u32[]{:S(2)}) collective-permute-start(bf16[2304,256]{1,0:T(8,128)(2,1)} %bitcast.42), channel_id=1, source_target_pairs={{0,32},{32,64},{64,96},{96,128},{128,160},{160,192},{192,224},{1,3... | collective-permute-start | bytes 3538952 | tf_op jit(solution)/shard_map/ppermute | solution.py:29
  59.8 1.2 %copy-start.1 = (bf16[16,144,384]{2,1,0:T(8,128)(2,1)}, bf16[16,144,384]{2,1,0:T(8,128)(2,1)S(1)}, u32[]{:S(2)}) copy-start(bf16[16,144,384]{2,1,0:T(8,128)(2,1)S(1)} %all-to-all-done) | copy-start | bytes 5308420
  73.4 1.0 copy-start.2

commit v8 on v7

--- a/solution.py
+++ b/solution.py
@@ -91,29 +91,24 @@
             k_col, v_col = width + h * HEAD_DIM, 2 * width + h * HEAD_DIM
         acc_at = slice(None) if stale_phase else head
 
-        def weights(index):
-            start = pl.multiple_of(index * TILE_TOKENS, TILE_TOKENS)
-            keys = keys_ref[pl.ds(start, TILE_TOKENS), pl.ds(k_col, HEAD_DIM)]
-            values = keys_ref[pl.ds(start, TILE_TOKENS), pl.ds(v_col, HEAD_DIM)]
+        def accumulate(indices):
+            starts = [pl.multiple_of(i * TILE_TOKENS, TILE_TOKENS) for i in indices]
+            keys = jnp.concatenate(
+                [keys_ref[pl.ds(a, TILE_TOKENS), pl.ds(k_col, HEAD_DIM)] for a in starts], axis=0
+            )
+            values = jnp.concatenate(
+                [keys_ref[pl.ds(a, TILE_TOKENS), pl.ds(v_col, HEAD_DIM)] for a in starts], axis=0
+            )
             scores = lax.dot_general(
                 query, keys, (((1,), (1,)), ((), ())), preferred_element_type=jnp.float32
             )
             weight = jnp.exp2(jnp.tanh(scores * factor) * lift - lift)
             part = weight[:, 0:HEAD_DIM]
-            for c in range(1, TILE_TOKENS // HEAD_DIM):
+            for c in range(1, weight.shape[1] // HEAD_DIM):
                 part = part + weight[:, c * HEAD_DIM:(c + 1) * HEAD_DIM]
-            return weight.astype(jnp.bfloat16), part, values
-
-        def accumulate(indices):
-            got = [weights(i) for i in indices]
-            part = got[0][1]
-            for g in got[1:]:
-                part = part + g[1]
             tot_ref[:, acc_at] += part
             acc_ref[:, acc_at] += jnp.dot(
-                jnp.concatenate([g[0] for g in got], axis=1),
-                jnp.concatenate([g[2] for g in got], axis=0),
-                preferred_element_type=jnp.float32,
+                weight.astype(jnp.bfloat16), values, preferred_element_type=jnp.float32
             )
 
         def group(p, carry):

time: 110 us -> 109 us (level); the launches traced: 110 us -> 108 us
  Pallas kernels: 32.3 us -> 30.8 us
    pallas_call x2, Pallas kernels: 32.3 us -> 30.8 us  [tile_attention(): pl.pallas_call(functools.partial(attention_kernel, local_heads, per_patch...]
  transfers between devices with their start and end apart: 4 -> 4, of which waited for: 2 -> 2; matrix products, arithmetic and copies ran while one was open for 2% -> 2% of each run, Pallas kernels for 11% -> 10%
where the time goes in v8:
time: 109 us; the launch traced here: 108 us
  waiting for transfers between devices  38.6 us (35%)
  Pallas kernels  30.8 us (28%)
  starting transfers between devices  15.2 us (14%)
  blocking collectives  14 us (13%)
  local copies, waits for them, and re-layouts  5.78 us (5%)
  other arithmetic  3.22 us (3%)
    all_to_all x2, waiting for transfers between devices, interleaved(): lax.all_to_all(joined, 'seq', split_axis=0, concat_axis=0, tiled=True)  38.6 us
    pallas_call x2, Pallas kernels, tile_attention(): pl.pallas_call(functools.partial(attention_kernel, local_heads, per_patch...  30.8 us
    all_to_all x1, blocking collectives, on_device(): lax.all_to_all(merged, 'seq', split_axis=0, concat_axis=1, tiled=True)  14 us
    all_to_all x2, starting transfers between devices, interleaved(): lax.all_to_all(joined, 'seq', split_axis=0, concat_axis=0, tiled=True)  10.9 us
    unnamed x16, local copies, waits for them, and re-layouts  3.33 us
    transpose x2, other arithmetic, interleaved(): joined = jnp.concatenate(parts, axis=2).transpose(1, 0, 2)  2.63 us
    ppermute x1, starting transfers between devices, with_halo(): before = lax.ppermute(last, axis, up)  2.41 us
  transfers between devices with their start and end apart: 4, of which 2 were waited for; matrix products, arithmetic and copies ran while one was open for 2% of the time, Pallas kernels for 10%

profile of v8, /device:TPU:128, one launch (start us, length us, event | category | flops | bytes accessed | tf_op | source)
XLA Modules:
  0.0 107.8 jit_solution(1493373526430747712)
XLA Ops:
  0.0 0.0 copy-start
  0.0 1.1 copy-done
  1.1 1.3 %copy_bitcast_fusion.1 = (bf16[144,16,128]{2,0,1:T(8,128)(2,1)S(1)}, bf16[144,16,128]{2,0,1:T(8,128)(2,1)S(1)}) fusion(bf16[144,2048]{1,0:T(8,128)(2,1)S(1)} %copy-done, bf16[144,2048]{1,0:T(8,128)(2,1)} %param.11), kind=kLoop, calls=%fused_computation.3 | loop fusion | bytes 2359296 | tf_op jit(solution)/shard_map/reshape | solution.py:181
  2.3 0.0 copy-start.4
  2.3 1.2 %maximum_bitcast_fusion.1 = bf16[16,144,256]{2,1,0:T(8,128)(2,1)} fusion(bf16[144,16,128]{2,0,1:T(8,128)(2,1)S(1)} %get-tuple-element.11, bf16[144,16,128]{2,0,1:T(8,128)(2,1)S(1)} %get-tuple-element.12), kind=kLoop, calls=%fused_computation.1 | loop fusion | flops 2359296 | bytes 2359296 | tf_op jit(solution)/shard_map/transpose | solution.py:182
  3.5 0.0 copy-start.5
  3.5 0.0 copy-start.6
  3.5 7.2 %all-to-all-start.1 = ((bf16[16,144,256]{2,1,0:T(8,128)(2,1)}), bf16[16,144,256]{2,1,0:T(8,128)(2,1)S(1)}, u32[]{:S(2)}, u32[]{:S(2)}) async-start(bf16[16,144,256]{2,1,0:T(8,128)(2,1)} %maximum_bitcast_fusion.1), calls=%async_computation.1 | async-start | bytes 2359296 | tf_op jit(solution)/shard_map/all_to_all | solution.py:183
  10.7 0.0 copy-done.4
  10.7 0.1 copy_bitcast_fusion.5
  10.8 0.0 copy-done.5
  10.8 0.0 copy-done.6
  10.8 0.2 copy_bitcast_fusion.3
  11.0 1.5 %maximum_bitcast_fusion = bf16[16,144,384]{2,1,0:T(8,128)(2,1)} fusion(bf16[144,16,128]{2,0,1:T(8,128)(2,1)S(1)} %get-tuple-element.9, bf16[144,16,128]{2,0,1:T(8,128)(2,1)S(1)} %get-tuple-element.10, bf16[144,16,128]{2,0,1:T(8,128)(2,1)S(1)} %copy_bitcast_fusion.5), kind=kLoop, calls=%fused_computation | loop fusion | flops 5308416 | bytes 3538944 | tf_op jit(solution)/shard_map/transpose | solution.py:182
  12.5 0.0 copy-start.7
  12.5 17.4 %all-to-all-done.1 = bf16[16,144,256]{2,1,0:T(8,128)(2,1)S(1)} async-done(((bf16[16,144,256]{2,1,0:T(8,128)(2,1)}), bf16[16,144,256]{2,1,0:T(8,128)(2,1)S(1)}, u32[]{:S(2)}, u32[]{:S(2)}) %all-to-all-start.1) | async-done | bytes 1179680 | tf_op jit(solution)/shard_map/all_to_all | solution.py:183
  29.9 0.0 copy-start.3
  29.9 3.7 %all-to-all-start = ((bf16[16,144,384]{2,1,0:T(8,128)(2,1)}), bf16[16,144,384]{2,1,0:T(8,128)(2,1)S(1)}, u32[]{:S(2)}, u32[]{:S(2)}) async-start(bf16[16,144,384]{2,1,0:T(8,128)(2,1)} %maximum_bitcast_fusion), calls=%async_computation | async-start | bytes 3538944 | tf_op jit(solution)/shard_map/all_to_all | solution.py:183
  33.6 0.0 copy-done.3
  33.6 1.9 %collective-permute-start.1 = (bf16[2304,256]{1,0:T(8,128)(2,1)}, bf16[2304,256]{1,0:T(8,128)(2,1)S(1)}, u32[]{:S(2)}, u32[]{:S(2)}) collective-permute-start(bf16[2304,256]{1,0:T(8,128)(2,1)} %bitcast.41), channel_id=1, source_target_pairs={{32,0},{64,32},{96,64},{128,96},{160,128},{192,160},{224,192},{33,... | collective-permute-start | bytes 3538952 | tf_op jit(solution)/shard_map/ppermute | solution.py:30
  35.6 2.4 %collective-permute-start = (bf16[2304,256]{1,0:T(8,128)(2,1)}, bf16[2304,256]{1,0:T(8,128)(2,1)}, u32[]{:S(2)}, u32[]{:S(2)}) collective-permute-start(bf16[2304,256]{1,0:T(8,128)(2,1)} %bitcast.42), channel_id=1, source_target_pairs={{0,32},{32,64},{64,96},{96,128},{128,160},{160,192},{192,224},{1,3... | collective-permute-start | bytes 3538952 | tf_op jit(solution)/shard_map/ppermute | solution.py:29
  38.0 0.0 copy-done.7
  38.0 0.6 broadcast_subtract_fusion.ids_ref
  38.6 21.2 %all-to-all-done = bf16[16,144,384]{2,1,0:T(8,128)(2,1)S(1)} async-done(((bf16[16,144,384]{2,1,0:T(8,128)(2,1)}), bf16[16,144,384]{2,1,0:T(8,128)(2,1)S(1)}, u32[]{:S(2)}, u32[]{:S(2)}) %all-to-all-start) | async-done | bytes 1769504 | tf_op jit(solution)/shard_map/all_to_all | solution.py:183
  59.8 0.0 copy-start.1
  59.8 1.2 %copy-done.1 = bf16[16,144,384]{2,1,0:T(8,128)(2,1)} copy-done((bf16[16,144,384]{2,1,0:T(8,128)(2,1)}, bf16[16,144,384]{2,1,0:T(8,128)(2,1)S(1)}, u32[]{:S(2)}) %copy-start.1) | copy-done | bytes 1769496
  61.0 10.3 %shard_map.73 = (f32[2304,128]{1,0:T(8,128)}, f32[2304,128]{1,0:T(8,128)}) custom-call(s32[6,18]{1,0:T(8,128)} %broadcast_subtract_fusion.ids_ref, s32[6]{0:T(128)} %count_ref.3, bf16[2304,384]{1,0:T(8,128)(2,1)} %bitcast.38), custom_call_target="tpu_custom_call" | custom-call | tf_op jit(solution)/shard_map/pallas_call | solution.py:140
  71.4 0.0 collective-permute-done.1.refs_1_
  71.4 0.0 copy-start.2
  71.4 0.0 collective-permute-done.refs_0_
  71.4 1.0 copy-done.2
  72.4 20.5 %shard_map.74 = bf16[2304,128]{1,0:T(8,128)(2,1)} custom-call(s32[6,18]{1,0:T(8,128)} %broadcast_subtract_fusion.ids_ref, s32[6]{0:T(128)} %count_ref.3, bf16[2304,384]{1,0:T(8,128)(2,1)} %bitcast.39, bf16[2304,256]{1,0:T(8,128)(2,1)} %collective-permute-done.refs_0_, bf16[2304,256]{1,0:T(8,128)(2,1)} %copy-done.2, f32[2304,128]{1,0:T(8,128)} %get-tuple-element.7.refs_2_, ...), custom_call_target="tpu_custom_call" | custom-call | tf_op jit(solution)/shard_map/pallas_call | solution.py:152
  92.9 14.0 %all_to_all.29 = bf16[16,144,128]{2,1,0:T(8,128)(2,1)S(1)} all-to-all(bf16[16,144,128]{2,1,0:T(8,128)(2,1)} %bitcast.40), channel_id=1, replica_groups=mesh['patch'=8,'seq'=16,'cfg'=2] {'seq'}, dimensions={0} | all-to-all | bytes 1179648 | tf_op jit(solution)/shard_map/all_to_all | solution.py:196
  106.9 0.9 copy_bitcast_fusion
Async XLA Ops:
  0.0 1.1 copy-start
  2.3 8.4 %copy-start.4 = (bf16[144,2048]{1,0:T(8,128)(2,1)S(1)}, bf16[144,2048]{1,0:T(8,128)(2,1)}, u32[]{:S(2)}) copy-start(bf16[144,2048]{1,0:T(8,128)(2,1)} %param.7) | copy-start | bytes 1769476
  3.5 7.3 %copy-start.5 = (bf16[144,2048]{1,0:T(8,128)(2,1)S(1)}, bf16[144,2048]{1,0:T(8,128)(2,1)}, u32[]{:S(2)}) copy-start(bf16[144,2048]{1,0:T(8,128)(2,1)} %param.8) | copy-start | bytes 1769476
  3.5 7.3 %copy-start.6 = (bf16[144,2048]{1,0:T(8,128)(2,1)S(1)}, bf16[144,2048]{1,0:T(8,128)(2,1)}, u32[]{:S(2)}) copy-start(bf16[144,2048]{1,0:T(8,128)(2,1)} %param.9) | copy-start | bytes 1769476
  3.5 26.4 %all-to-all-start.1 = ((bf16[16,144,256]{2,1,0:T(8,128)(2,1)}), bf16[16,144,256]{2,1,0:T(8,128)(2,1)S(1)}, u32[]{:S(2)}, u32[]{:S(2)}) async-start(bf16[16,144,256]{2,1,0:T(8,128)(2,1)} %maximum_bitcast_fusion.1), calls=%async_computation.1 | async-start | bytes 2359296 | tf_op jit(solution)/shard_map/all_to_all | solution.py:183
  12.5 25.5 %copy-start.7 = (s32[6,18]{1,0:T(8,128)S(1)}, s32[6,18]{1,0:T(8,128)}, u32[]{:S(2)}) copy-start(s32[6,18]{1,0:T(8,128)} %param.12) | copy-start | bytes 1300
  29.9 3.7 %copy-start.3 = (bf16[16,144,256]{2,1,0:T(8,128)(2,1)}, bf16[16,144,256]{2,1,0:T(8,128)(2,1)S(1)}, u32[]{:S(2)}) copy-start(bf16[16,144,256]{2,1,0:T(8,128)(2,1)S(1)} %all-to-all-done.1) | copy-start | bytes 3538948
  29.9 29.9 %all-to-all-start = ((bf16[16,144,384]{2,1,0:T(8,128)(2,1)}), bf16[16,144,384]{2,1,0:T(8,128)(2,1)S(1)}, u32[]{:S(2)}, u32[]{:S(2)}) async-start(bf16[16,144,384]{2,1,0:T(8,128)(2,1)} %maximum_bitcast_fusion), calls=%async_computation | async-start | bytes 3538944 | tf_op jit(solution)/shard_map/all_to_all | solution.py:183
  33.6 37.7 %collective-permute-start.1 = (bf16[2304,256]{1,0:T(8,128)(2,1)}, bf16[2304,256]{1,0:T(8,128)(2,1)S(1)}, u32[]{:S(2)}, u32[]{:S(2)}) collective-permute-start(bf16[2304,256]{1,0:T(8,128)(2,1)} %bitcast.41), channel_id=1, source_target_pairs={{32,0},{64,32},{96,64},{128,96},{160,128},{192,160},{224,192},{33,... | collective-permute-start | bytes 3538952 | tf_op jit(solution)/shard_map/ppermute | solution.py:30
  35.6 35.8 %collective-permute-start = (bf16[2304,256]{1,0:T(8,128)(2,1)}, bf16[2304,256]{1,0:T(8,128)(2,1)}, u32[]{:S(2)}, u32[]{:S(2)}) collective-permute-start(bf16[2304,256]{1,0:T(8,128)(2,1)} %bitcast.42), channel_id=1, source_target_pairs={{0,32},{32,64},{64,96},{96,128},{128,160},{160,192},{192,224},{1,3... | collective-permute-start | bytes 3538952 | tf_op jit(solution)/shard_map/ppermute | solution.py:29
  59.8 1.2 %copy-start.1 = (bf16[16,144,384]{2,1,0:T(8,128)(2,1)}, bf16[16,144,384]{2,1,0:T(8,128)(2,1)S(1)}, u32[]{:S(2)}) copy-start(bf16[16,144,384]{2,1,0:T(8,128)(2,1)S(1)} %all-to-all-done) | copy-start | bytes 5308420
  71.4 1.0 copy-start.2

commit v9 on v7

--- a/solution.py
+++ b/solution.py
@@ -34,8 +34,7 @@
 
 def attention_kernel(local_heads, per_patch, stale_phase, ids_ref, count_ref, fresh_ref, *refs):
     if stale_phase:
-        before_hbm, after_hbm, acc_in, tot_in, o_ref, stale_ref, copy_sem, list_ref, acc_ref, tot_ref = refs
-        keys_ref = stale_ref
+        before_in, after_in, acc_in, tot_in, o_ref, keys_ref, copy_sem, list_ref, acc_ref, tot_ref = refs
     else:
         acc_ref, tot_ref, list_ref = refs
         keys_ref = fresh_ref
@@ -49,33 +48,47 @@
 
         @pl.when(t == 0)
         def _():
-            first = pltpu.make_async_copy(before_hbm, stale_ref.at[pl.ds(0, patch_rows)], copy_sem.at[0])
-            second = pltpu.make_async_copy(
-                after_hbm, stale_ref.at[pl.ds(patch_rows, patch_rows)], copy_sem.at[1]
-            )
-            first.start()
-            second.start()
-            first.wait()
-            second.wait()
-
-    def compact(j, n):
+            copies = [
+                pltpu.make_async_copy(before_in, keys_ref.at[pl.ds(0, patch_rows)], copy_sem.at[0]),
+                pltpu.make_async_copy(
+                    fresh_ref.at[:, pl.ds(width, 2 * width)],
+                    keys_ref.at[pl.ds(patch_rows, patch_rows)],
+                    copy_sem.at[1],
+                ),
+                pltpu.make_async_copy(
+                    after_in, keys_ref.at[pl.ds(2 * patch_rows, patch_rows)], copy_sem.at[2]
+                ),
+            ]
+            for c in copies:
+                c.start()
+            for c in copies:
+                c.wait()
+
+    def own(j):
+        return ids_ref[t, j] // per_patch == 1
+
+    own_count = lax.fori_loop(0, count_ref[t], lambda j, n: n + own(j).astype(jnp.int32), jnp.int32(0))
+    first_pass = own_count - own_count % SLOT_GROUP
+
+    def compact(j, carry):
+        n, seen = carry
         u = ids_ref[t, j]
-        which = u // per_patch
-        row = u - which * per_patch
+        mine = own(j)
+        early = jnp.logical_and(mine, seen < first_pass)
         if stale_phase:
-            keep = which != 1
-            index = (which // 2) * per_patch + row
+            keep = jnp.logical_not(early)
+            index = u
         else:
-            keep = which == 1
-            index = row
+            keep = early
+            index = u - per_patch
 
         @pl.when(keep)
         def _():
             list_ref[n] = index
 
-        return n + keep.astype(jnp.int32)
-
-    used = lax.fori_loop(0, count_ref[t], compact, jnp.int32(0))
+        return n + keep.astype(jnp.int32), seen + mine.astype(jnp.int32)
+
+    used, _ = lax.fori_loop(0, count_ref[t], compact, (jnp.int32(0), jnp.int32(0)))
 
     for h in range(local_heads):
         head = pl.ds(h * HEAD_DIM, HEAD_DIM)
@@ -121,13 +134,13 @@
             return carry
 
         lax.fori_loop(0, used // SLOT_GROUP, group, 0)
-        for left in range(1, SLOT_GROUP):
-
-            @pl.when(used % SLOT_GROUP == left)
-            def _():
-                accumulate([list_ref[used - left + i] for i in range(left)])
-
         if stale_phase:
+            for left in range(1, SLOT_GROUP):
+
+                @pl.when(used % SLOT_GROUP == left)
+                def _():
+                    accumulate([list_ref[used - left + i] for i in range(left)])
+
             total = jnp.sum(tot_ref[...], axis=1, keepdims=True)
             o_ref[:, head] = (acc_ref[...] / total).astype(o_ref.dtype)
 
@@ -153,18 +166,17 @@
             scratch_shapes=[pltpu.SMEM((KEY_SLOTS,), jnp.int32)],
         ),
     )(local_ids, tile_count, fresh)
-    hbm = pl.BlockSpec(memory_space=pl.ANY)
     return pl.pallas_call(
         functools.partial(attention_kernel, local_heads, per_patch, True),
         out_shape=jax.ShapeDtypeStruct((rows, width), jnp.bfloat16),
         grid_spec=pltpu.PrefetchScalarGridSpec(
             num_scalar_prefetch=2,
             grid=(tiles,),
-            in_specs=[whole(fresh), hbm, hbm, tile, tile],
+            in_specs=[whole(fresh), whole(before), whole(after), tile, tile],
             out_specs=tile,
             scratch_shapes=[
-                pltpu.VMEM((2 * rows, before.shape[1]), before.dtype),
-                pltpu.SemaphoreType.DMA((2,)),
+                pltpu.VMEM((3 * rows, before.shape[1]), before.dtype),
+                pltpu.SemaphoreType.DMA((3,)),
                 pltpu.SMEM((KEY_SLOTS,), jnp.int32),
                 pltpu.VMEM((TILE_TOKENS, HEAD_DIM), jnp.float32),
                 pltpu.VMEM((TILE_TOKENS, HEAD_DIM), jnp.float32),

time: 110 us -> 111 us (level); the launches traced: 110 us -> 110 us
  transfers between devices with their start and end apart: 4 -> 4, of which waited for: 2 -> 2; matrix products, arithmetic and copies ran while one was open for 2% -> 2% of each run, Pallas kernels for 11% -> 8%
where the time goes in v9:
time: 111 us; the launch traced here: 110 us
  waiting for transfers between devices  38.6 us (35%)
  Pallas kernels  31.6 us (28%)
  starting transfers between devices  15.2 us (14%)
  blocking collectives  15.2 us (14%)
  local copies, waits for them, and re-layouts  5.78 us (5%)
  other arithmetic  3.22 us (3%)
    all_to_all x2, waiting for transfers between devices, interleaved(): lax.all_to_all(joined, 'seq', split_axis=0, concat_axis=0, tiled=True)  38.6 us
    pallas_call x2, Pallas kernels, tile_attention(): pl.pallas_call(functools.partial(attention_kernel, local_heads, per_patch...  31.6 us
    all_to_all x1, blocking collectives, on_device(): lax.all_to_all(merged, 'seq', split_axis=0, concat_axis=1, tiled=True)  15.2 us
    all_to_all x2, starting transfers between devices, interleaved(): lax.all_to_all(joined, 'seq', split_axis=0, concat_axis=0, tiled=True)  10.9 us
    unnamed x16, local copies, waits for them, and re-layouts  3.33 us
    transpose x2, other arithmetic, interleaved(): joined = jnp.concatenate(parts, axis=2).transpose(1, 0, 2)  2.63 us
    ppermute x1, starting transfers between devices, with_halo(): before = lax.ppermute(last, axis, up)  2.41 us
  transfers between devices with their start and end apart: 4, of which 2 were waited for; matrix products, arithmetic and copies ran while one was open for 2% of the time, Pallas kernels for 8%

profile of v9, /device:TPU:128, one launch (start us, length us, event | category | flops | bytes accessed | tf_op | source)
XLA Modules:
  0.0 109.8 jit_solution(6275958734212962238)
XLA Ops:
  0.0 0.0 copy-start
  0.0 1.1 copy-done
  1.1 1.3 %copy_bitcast_fusion.1 = (bf16[144,16,128]{2,0,1:T(8,128)(2,1)S(1)}, bf16[144,16,128]{2,0,1:T(8,128)(2,1)S(1)}) fusion(bf16[144,2048]{1,0:T(8,128)(2,1)S(1)} %copy-done, bf16[144,2048]{1,0:T(8,128)(2,1)} %param.11), kind=kLoop, calls=%fused_computation.3 | loop fusion | bytes 2359296 | tf_op jit(solution)/shard_map/reshape | solution.py:198
  2.3 0.0 copy-start.4
  2.3 1.2 %maximum_bitcast_fusion.1 = bf16[16,144,256]{2,1,0:T(8,128)(2,1)} fusion(bf16[144,16,128]{2,0,1:T(8,128)(2,1)S(1)} %get-tuple-element.11, bf16[144,16,128]{2,0,1:T(8,128)(2,1)S(1)} %get-tuple-element.12), kind=kLoop, calls=%fused_computation.1 | loop fusion | flops 2359296 | bytes 2359296 | tf_op jit(solution)/shard_map/transpose | solution.py:199
  3.5 0.0 copy-start.5
  3.5 0.0 copy-start.6
  3.5 7.2 %all-to-all-start.1 = ((bf16[16,144,256]{2,1,0:T(8,128)(2,1)}), bf16[16,144,256]{2,1,0:T(8,128)(2,1)S(1)}, u32[]{:S(2)}, u32[]{:S(2)}) async-start(bf16[16,144,256]{2,1,0:T(8,128)(2,1)} %maximum_bitcast_fusion.1), calls=%async_computation.1 | async-start | bytes 2359296 | tf_op jit(solution)/shard_map/all_to_all | solution.py:200
  10.7 0.0 copy-done.4
  10.7 0.1 copy_bitcast_fusion.5
  10.8 0.0 copy-done.5
  10.8 0.0 copy-done.6
  10.8 0.2 copy_bitcast_fusion.3
  11.0 1.5 %maximum_bitcast_fusion = bf16[16,144,384]{2,1,0:T(8,128)(2,1)} fusion(bf16[144,16,128]{2,0,1:T(8,128)(2,1)S(1)} %get-tuple-element.9, bf16[144,16,128]{2,0,1:T(8,128)(2,1)S(1)} %get-tuple-element.10, bf16[144,16,128]{2,0,1:T(8,128)(2,1)S(1)} %copy_bitcast_fusion.5), kind=kLoop, calls=%fused_computation | loop fusion | flops 5308416 | bytes 3538944 | tf_op jit(solution)/shard_map/transpose | solution.py:199
  12.5 0.0 copy-start.7
  12.5 17.4 %all-to-all-done.1 = bf16[16,144,256]{2,1,0:T(8,128)(2,1)S(1)} async-done(((bf16[16,144,256]{2,1,0:T(8,128)(2,1)}), bf16[16,144,256]{2,1,0:T(8,128)(2,1)S(1)}, u32[]{:S(2)}, u32[]{:S(2)}) %all-to-all-start.1) | async-done | bytes 1179680 | tf_op jit(solution)/shard_map/all_to_all | solution.py:200
  29.9 0.0 copy-start.3
  29.9 3.7 %all-to-all-start = ((bf16[16,144,384]{2,1,0:T(8,128)(2,1)}), bf16[16,144,384]{2,1,0:T(8,128)(2,1)S(1)}, u32[]{:S(2)}, u32[]{:S(2)}) async-start(bf16[16,144,384]{2,1,0:T(8,128)(2,1)} %maximum_bitcast_fusion), calls=%async_computation | async-start | bytes 3538944 | tf_op jit(solution)/shard_map/all_to_all | solution.py:200
  33.6 0.0 copy-done.3
  33.6 1.9 %collective-permute-start.1 = (bf16[2304,256]{1,0:T(8,128)(2,1)}, bf16[2304,256]{1,0:T(8,128)(2,1)S(1)}, u32[]{:S(2)}, u32[]{:S(2)}) collective-permute-start(bf16[2304,256]{1,0:T(8,128)(2,1)} %bitcast.41), channel_id=1, source_target_pairs={{32,0},{64,32},{96,64},{128,96},{160,128},{192,160},{224,192},{33,... | collective-permute-start | bytes 3538952 | tf_op jit(solution)/shard_map/ppermute | solution.py:30
  35.6 2.4 %collective-permute-start = (bf16[2304,256]{1,0:T(8,128)(2,1)}, bf16[2304,256]{1,0:T(8,128)(2,1)}, u32[]{:S(2)}, u32[]{:S(2)}) collective-permute-start(bf16[2304,256]{1,0:T(8,128)(2,1)} %bitcast.42), channel_id=1, source_target_pairs={{0,32},{32,64},{64,96},{96,128},{128,160},{160,192},{192,224},{1,3... | collective-permute-start | bytes 3538952 | tf_op jit(solution)/shard_map/ppermute | solution.py:29
  38.0 0.0 copy-done.7
  38.0 0.6 broadcast_subtract_fusion.ids_ref
  38.6 21.2 %all-to-all-done = bf16[16,144,384]{2,1,0:T(8,128)(2,1)S(1)} async-done(((bf16[16,144,384]{2,1,0:T(8,128)(2,1)}), bf16[16,144,384]{2,1,0:T(8,128)(2,1)S(1)}, u32[]{:S(2)}, u32[]{:S(2)}) %all-to-all-start) | async-done | bytes 1769504 | tf_op jit(solution)/shard_map/all_to_all | solution.py:200
  59.8 0.0 copy-start.1
  59.8 1.2 %copy-done.1 = bf16[16,144,384]{2,1,0:T(8,128)(2,1)} copy-done((bf16[16,144,384]{2,1,0:T(8,128)(2,1)}, bf16[16,144,384]{2,1,0:T(8,128)(2,1)S(1)}, u32[]{:S(2)}) %copy-start.1) | copy-done | bytes 1769496
  61.0 8.8 %shard_map.73 = (f32[2304,128]{1,0:T(8,128)}, f32[2304,128]{1,0:T(8,128)}) custom-call(s32[6,18]{1,0:T(8,128)} %broadcast_subtract_fusion.ids_ref, s32[6]{0:T(128)} %count_ref.3, bf16[2304,384]{1,0:T(8,128)(2,1)} %bitcast.38), custom_call_target="tpu_custom_call" | custom-call | tf_op jit(solution)/shard_map/pallas_call | solution.py:158
  69.8 0.0 collective-permute-done.1.refs_1_
  69.8 0.0 copy-start.2
  69.8 0.0 collective-permute-done.refs_0_
  69.8 1.0 copy-done.2
  70.8 22.9 %shard_map.74 = bf16[2304,128]{1,0:T(8,128)(2,1)} custom-call(s32[6,18]{1,0:T(8,128)} %broadcast_subtract_fusion.ids_ref, s32[6]{0:T(128)} %count_ref.3, bf16[2304,384]{1,0:T(8,128)(2,1)} %bitcast.39, bf16[2304,256]{1,0:T(8,128)(2,1)} %collective-permute-done.refs_0_, bf16[2304,256]{1,0:T(8,128)(2,1)} %copy-done.2, f32[2304,128]{1,0:T(8,128)} %get-tuple-element.7.refs_2_, ...), custom_call_target="tpu_custom_call" | custom-call | tf_op jit(solution)/shard_map/pallas_call | solution.py:169
  93.7 15.2 %all_to_all.29 = bf16[16,144,128]{2,1,0:T(8,128)(2,1)S(1)} all-to-all(bf16[16,144,128]{2,1,0:T(8,128)(2,1)} %bitcast.40), channel_id=1, replica_groups=mesh['patch'=8,'seq'=16,'cfg'=2] {'seq'}, dimensions={0} | all-to-all | bytes 1179648 | tf_op jit(solution)/shard_map/all_to_all | solution.py:213
  108.9 0.9 copy_bitcast_fusion
Async XLA Ops:
  0.0 1.1 copy-start
  2.3 8.4 %copy-start.4 = (bf16[144,2048]{1,0:T(8,128)(2,1)S(1)}, bf16[144,2048]{1,0:T(8,128)(2,1)}, u32[]{:S(2)}) copy-start(bf16[144,2048]{1,0:T(8,128)(2,1)} %param.7) | copy-start | bytes 1769476
  3.5 7.3 %copy-start.5 = (bf16[144,2048]{1,0:T(8,128)(2,1)S(1)}, bf16[144,2048]{1,0:T(8,128)(2,1)}, u32[]{:S(2)}) copy-start(bf16[144,2048]{1,0:T(8,128)(2,1)} %param.8) | copy-start | bytes 1769476
  3.5 7.3 %copy-start.6 = (bf16[144,2048]{1,0:T(8,128)(2,1)S(1)}, bf16[144,2048]{1,0:T(8,128)(2,1)}, u32[]{:S(2)}) copy-start(bf16[144,2048]{1,0:T(8,128)(2,1)} %param.9) | copy-start | bytes 1769476
  3.5 26.4 %all-to-all-start.1 = ((bf16[16,144,256]{2,1,0:T(8,128)(2,1)}), bf16[16,144,256]{2,1,0:T(8,128)(2,1)S(1)}, u32[]{:S(2)}, u32[]{:S(2)}) async-start(bf16[16,144,256]{2,1,0:T(8,128)(2,1)} %maximum_bitcast_fusion.1), calls=%async_computation.1 | async-start | bytes 2359296 | tf_op jit(solution)/shard_map/all_to_all | solution.py:200
  12.5 25.5 %copy-start.7 = (s32[6,18]{1,0:T(8,128)S(1)}, s32[6,18]{1,0:T(8,128)}, u32[]{:S(2)}) copy-start(s32[6,18]{1,0:T(8,128)} %param.12) | copy-start | bytes 1300
  29.9 3.7 %copy-start.3 = (bf16[16,144,256]{2,1,0:T(8,128)(2,1)}, bf16[16,144,256]{2,1,0:T(8,128)(2,1)S(1)}, u32[]{:S(2)}) copy-start(bf16[16,144,256]{2,1,0:T(8,128)(2,1)S(1)} %all-to-all-done.1) | copy-start | bytes 3538948
  29.9 29.9 %all-to-all-start = ((bf16[16,144,384]{2,1,0:T(8,128)(2,1)}), bf16[16,144,384]{2,1,0:T(8,128)(2,1)S(1)}, u32[]{:S(2)}, u32[]{:S(2)}) async-start(bf16[16,144,384]{2,1,0:T(8,128)(2,1)} %maximum_bitcast_fusion), calls=%async_computation | async-start | bytes 3538944 | tf_op jit(solution)/shard_map/all_to_all | solution.py:200
  33.6 36.2 %collective-permute-start.1 = (bf16[2304,256]{1,0:T(8,128)(2,1)}, bf16[2304,256]{1,0:T(8,128)(2,1)S(1)}, u32[]{:S(2)}, u32[]{:S(2)}) collective-permute-start(bf16[2304,256]{1,0:T(8,128)(2,1)} %bitcast.41), channel_id=1, source_target_pairs={{32,0},{64,32},{96,64},{128,96},{160,128},{192,160},{224,192},{33,... | collective-permute-start | bytes 3538952 | tf_op jit(solution)/shard_map/ppermute | solution.py:30
  35.6 34.3 %collective-permute-start = (bf16[2304,256]{1,0:T(8,128)(2,1)}, bf16[2304,256]{1,0:T(8,128)(2,1)}, u32[]{:S(2)}, u32[]{:S(2)}) collective-permute-start(bf16[2304,256]{1,0:T(8,128)(2,1)} %bitcast.42), channel_id=1, source_target_pairs={{0,32},{32,64},{64,96},{96,128},{128,160},{160,192},{192,224},{1,3... | collective-permute-start | bytes 3538952 | tf_op jit(solution)/shard_map/ppermute | solution.py:29
  59.8 1.2 %copy-start.1 = (bf16[16,144,384]{2,1,0:T(8,128)(2,1)}, bf16[16,144,384]{2,1,0:T(8,128)(2,1)S(1)}, u32[]{:S(2)}) copy-start(bf16[16,144,384]{2,1,0:T(8,128)(2,1)S(1)} %all-to-all-done) | copy-start | bytes 5308420
  69.8 1.0 copy-start.2

commit v10 on v7

--- a/solution.py
+++ b/solution.py
@@ -174,6 +174,22 @@
     )(local_ids, tile_count, fresh, before, after, acc, tot)
 
 
+def regroup_kernel(width, *refs):
+    *in_refs, o_ref = refs
+    seq_count = o_ref.shape[0]
+    for d in range(seq_count):
+        for a, ref in enumerate(in_refs):
+            o_ref[d, :, a * width:(a + 1) * width] = ref[:, d * width:(d + 1) * width]
+
+
+def regroup(arrays, seq_count, width):
+    rows = arrays[0].shape[0]
+    return pl.pallas_call(
+        functools.partial(regroup_kernel, width),
+        out_shape=jax.ShapeDtypeStruct((seq_count, rows, len(arrays) * width), arrays[0].dtype),
+    )(*arrays)
+
+
 def on_device(query, fresh_key, fresh_value, stale_key, stale_value, key_tiles, tile_count):
     seq_count = lax.axis_size("seq")
     local_heads = NUM_HEADS // seq_count
@@ -188,7 +204,9 @@
         moved = lax.all_to_all(joined, "seq", split_axis=0, concat_axis=0, tiled=True)
         return moved.reshape(patch_rows, len(arrays) * width)
 
-    stale = interleaved([stale_key, stale_value])
+    joined = regroup([stale_key, stale_value], seq_count, width)
+    stale = lax.all_to_all(joined, "seq", split_axis=0, concat_axis=0, tiled=True)
+    stale = stale.reshape(patch_rows, 2 * width)
     framed = with_halo(stale, (("patch", 0),), patch_rows)
     before = framed[:patch_rows]
     after = framed[2 * patch_rows :]

time: 110 us -> 111 us (level); the launches traced: 110 us -> 109 us
  local copies, waits for them, and re-layouts: 5.78 us -> 4.5 us
  other arithmetic: 3.22 us -> 2.06 us
    all_to_all x0 -> x1, waiting for transfers between devices: none -> 17.4 us  [on_device(): lax.all_to_all(joined, 'seq', split_axis=0, concat_axis=0, tiled=True)]
    all_to_all x2 -> x1, waiting for transfers between devices: 38.6 us -> 21.2 us  [interleaved(): lax.all_to_all(joined, 'seq', split_axis=0, concat_axis=0, tiled=True)]
    all_to_all x2 -> x1, starting transfers between devices: 10.9 us -> 3.71 us  [interleaved(): lax.all_to_all(joined, 'seq', split_axis=0, concat_axis=0, tiled=True)]
    all_to_all x0 -> x1, starting transfers between devices: none -> 7.17 us  [on_device(): lax.all_to_all(joined, 'seq', split_axis=0, concat_axis=0, tiled=True)]
    pallas_call x0 -> x1, Pallas kernels: none -> 2.59 us  [regroup(): pl.pallas_call(functools.partial(regroup_kernel, width), out_shape=jax.Sh...]
    pallas_call x2, Pallas kernels: 32.3 us -> 30.2 us  [tile_attention(): pl.pallas_call(functools.partial(attention_kernel, local_heads, per_patch...]
    reshape x3 -> x2, local copies, waits for them, and re-layouts: 1.57 us -> 0.31 us  [interleaved(): parts = [a.reshape(rows, seq_count, width) for a in arrays]]
    transpose x2 -> x1, other arithmetic: 2.63 us -> 1.47 us  [interleaved(): joined = jnp.concatenate(parts, axis=2).transpose(1, 0, 2)]
  transfers between devices with their start and end apart: 4 -> 4, of which waited for: 2 -> 2; matrix products, arithmetic and copies ran while one was open for 2% -> 2% of each run, Pallas kernels for 11% -> 9%
where the time goes in v10:
time: 111 us; the launch traced here: 109 us
  waiting for transfers between devices  38.6 us (35%)
  Pallas kernels  32.8 us (30%)
  blocking collectives  15.9 us (14%)
  starting transfers between devices  15.2 us (14%)
  local copies, waits for them, and re-layouts  4.5 us (4%)
  other arithmetic  2.06 us (2%)
    pallas_call x2, Pallas kernels, tile_attention(): pl.pallas_call(functools.partial(attention_kernel, local_heads, per_patch...  30.2 us
    all_to_all x1, waiting for transfers between devices, interleaved(): lax.all_to_all(joined, 'seq', split_axis=0, concat_axis=0, tiled=True)  21.2 us
    all_to_all x1, waiting for transfers between devices, on_device(): lax.all_to_all(joined, 'seq', split_axis=0, concat_axis=0, tiled=True)  17.4 us
    all_to_all x1, blocking collectives, on_device(): lax.all_to_all(merged, 'seq', split_axis=0, concat_axis=1, tiled=True)  15.9 us
    all_to_all x1, starting transfers between devices, on_device(): lax.all_to_all(joined, 'seq', split_axis=0, concat_axis=0, tiled=True)  7.17 us
    all_to_all x1, starting transfers between devices, interleaved(): lax.all_to_all(joined, 'seq', split_axis=0, concat_axis=0, tiled=True)  3.71 us
    unnamed x14, local copies, waits for them, and re-layouts  3.31 us
    pallas_call x1, Pallas kernels, regroup(): pl.pallas_call(functools.partial(regroup_kernel, width), out_shape=jax.Sh...  2.59 us
  transfers between devices with their start and end apart: 4, of which 2 were waited for; matrix products, arithmetic and copies ran while one was open for 2% of the time, Pallas kernels for 9%

profile of v10, /device:TPU:128, one launch (start us, length us, event | category | flops | bytes accessed | tf_op | source)
XLA Modules:
  0.0 109.1 jit_solution(8664896917833555383)
XLA Ops:
  0.0 0.0 copy-start
  0.0 0.0 copy-start.4
  0.0 2.6 %shard_map.73 = bf16[16,144,256]{2,1,0:T(8,128)(2,1)} custom-call(bf16[144,2048]{1,0:T(8,128)(2,1)} %refs_0_.1, bf16[144,2048]{1,0:T(8,128)(2,1)} %refs_1_.1), custom_call_target="tpu_custom_call" | custom-call | tf_op jit(solution)/shard_map/pallas_call | solution.py:187
  2.6 0.0 copy-start.5
  2.6 7.2 %all-to-all-start.1 = ((bf16[16,144,256]{2,1,0:T(8,128)(2,1)}), bf16[16,144,256]{2,1,0:T(8,128)(2,1)S(1)}, u32[]{:S(2)}, u32[]{:S(2)}) async-start(bf16[16,144,256]{2,1,0:T(8,128)(2,1)} %shard_map.73), calls=%async_computation.1 | async-start | bytes 2359296 | tf_op jit(solution)/shard_map/all_to_all | solution.py:208
  9.8 0.0 copy-done.4
  9.8 0.1 copy_bitcast_fusion.3
  9.9 0.0 copy-done
  9.9 0.0 copy-done.5
  9.9 0.2 copy_bitcast_fusion.1
  10.1 1.5 %maximum_bitcast_fusion = bf16[16,144,384]{2,1,0:T(8,128)(2,1)} fusion(bf16[144,16,128]{2,0,1:T(8,128)(2,1)S(1)} %get-tuple-element.9, bf16[144,16,128]{2,0,1:T(8,128)(2,1)S(1)} %get-tuple-element.10, bf16[144,16,128]{2,0,1:T(8,128)(2,1)S(1)} %copy_bitcast_fusion.3), kind=kLoop, calls=%fused_computation | loop fusion | flops 5308416 | bytes 3538944 | tf_op jit(solution)/shard_map/transpose | solution.py:203
  11.6 0.0 copy-start.6
  11.6 17.4 %all-to-all-done.1 = bf16[16,144,256]{2,1,0:T(8,128)(2,1)S(1)} async-done(((bf16[16,144,256]{2,1,0:T(8,128)(2,1)}), bf16[16,144,256]{2,1,0:T(8,128)(2,1)S(1)}, u32[]{:S(2)}, u32[]{:S(2)}) %all-to-all-start.1) | async-done | bytes 1179680 | tf_op jit(solution)/shard_map/all_to_all | solution.py:208
  29.0 0.0 copy-start.3
  29.0 1.0 copy-done.3
  30.0 3.7 %all-to-all-start = ((bf16[16,144,384]{2,1,0:T(8,128)(2,1)}), bf16[16,144,384]{2,1,0:T(8,128)(2,1)S(1)}, u32[]{:S(2)}, u32[]{:S(2)}) async-start(bf16[16,144,384]{2,1,0:T(8,128)(2,1)} %maximum_bitcast_fusion), calls=%async_computation | async-start | bytes 3538944 | tf_op jit(solution)/shard_map/all_to_all | solution.py:204
  33.8 1.9 %collective-permute-start.1 = (bf16[2304,256]{1,0:T(8,128)(2,1)}, bf16[2304,256]{1,0:T(8,128)(2,1)S(1)}, u32[]{:S(2)}, u32[]{:S(2)}) collective-permute-start(bf16[2304,256]{1,0:T(8,128)(2,1)} %bitcast.29), channel_id=1, source_target_pairs={{32,0},{64,32},{96,64},{128,96},{160,128},{192,160},{224,192},{33,... | collective-permute-start | bytes 3538952 | tf_op jit(solution)/shard_map/ppermute | solution.py:30
  35.7 2.4 %collective-permute-start = (bf16[2304,256]{1,0:T(8,128)(2,1)}, bf16[2304,256]{1,0:T(8,128)(2,1)}, u32[]{:S(2)}, u32[]{:S(2)}) collective-permute-start(bf16[2304,256]{1,0:T(8,128)(2,1)} %bitcast.30), channel_id=1, source_target_pairs={{0,32},{32,64},{64,96},{96,128},{128,160},{160,192},{192,224},{1,3... | collective-permute-start | bytes 3538952 | tf_op jit(solution)/shard_map/ppermute | solution.py:29
  38.1 0.0 copy-done.6
  38.1 0.6 broadcast_subtract_fusion.ids_ref
  38.7 21.2 %all-to-all-done = bf16[16,144,384]{2,1,0:T(8,128)(2,1)S(1)} async-done(((bf16[16,144,384]{2,1,0:T(8,128)(2,1)}), bf16[16,144,384]{2,1,0:T(8,128)(2,1)S(1)}, u32[]{:S(2)}, u32[]{:S(2)}) %all-to-all-start) | async-done | bytes 1769504 | tf_op jit(solution)/shard_map/all_to_all | solution.py:204
  59.9 0.0 copy-start.1
  59.9 1.2 %copy-done.1 = bf16[16,144,384]{2,1,0:T(8,128)(2,1)} copy-done((bf16[16,144,384]{2,1,0:T(8,128)(2,1)}, bf16[16,144,384]{2,1,0:T(8,128)(2,1)S(1)}, u32[]{:S(2)}) %copy-start.1) | copy-done | bytes 1769496
  61.2 10.3 %shard_map.74 = (f32[2304,128]{1,0:T(8,128)}, f32[2304,128]{1,0:T(8,128)}) custom-call(s32[6,18]{1,0:T(8,128)} %broadcast_subtract_fusion.ids_ref, s32[6]{0:T(128)} %count_ref.3, bf16[2304,384]{1,0:T(8,128)(2,1)} %bitcast.26), custom_call_target="tpu_custom_call" | custom-call | tf_op jit(solution)/shard_map/pallas_call | solution.py:145
  71.5 0.0 collective-permute-done.1.refs_1_
  71.5 0.0 copy-start.2
  71.5 0.0 collective-permute-done.refs_0_
  71.5 1.0 copy-done.2
  72.5 19.9 %shard_map.75 = bf16[2304,128]{1,0:T(8,128)(2,1)} custom-call(s32[6,18]{1,0:T(8,128)} %broadcast_subtract_fusion.ids_ref, s32[6]{0:T(128)} %count_ref.3, bf16[2304,384]{1,0:T(8,128)(2,1)} %bitcast.27, bf16[2304,256]{1,0:T(8,128)(2,1)} %collective-permute-done.refs_0_, bf16[2304,256]{1,0:T(8,128)(2,1)} %copy-done.2, f32[2304,128]{1,0:T(8,128)} %get-tuple-element.7.refs_2_, ...), custom_call_target="tpu_custom_call" | custom-call | tf_op jit(solution)/shard_map/pallas_call | solution.py:157
  92.4 15.9 %all_to_all.29 = bf16[16,144,128]{2,1,0:T(8,128)(2,1)S(1)} all-to-all(bf16[16,144,128]{2,1,0:T(8,128)(2,1)} %bitcast.28), channel_id=1, replica_groups=mesh['patch'=8,'seq'=16,'cfg'=2] {'seq'}, dimensions={0} | all-to-all | bytes 1179648 | tf_op jit(solution)/shard_map/all_to_all | solution.py:219
  108.2 0.9 copy_bitcast_fusion
Async XLA Ops:
  0.0 9.9 %copy-start = (bf16[144,2048]{1,0:T(8,128)(2,1)S(1)}, bf16[144,2048]{1,0:T(8,128)(2,1)}, u32[]{:S(2)}) copy-start(bf16[144,2048]{1,0:T(8,128)(2,1)} %param.8) | copy-start | bytes 1769476
  0.0 9.8 %copy-start.4 = (bf16[144,2048]{1,0:T(8,128)(2,1)S(1)}, bf16[144,2048]{1,0:T(8,128)(2,1)}, u32[]{:S(2)}) copy-start(bf16[144,2048]{1,0:T(8,128)(2,1)} %param.7) | copy-start | bytes 1769476
  2.6 7.3 %copy-start.5 = (bf16[144,2048]{1,0:T(8,128)(2,1)S(1)}, bf16[144,2048]{1,0:T(8,128)(2,1)}, u32[]{:S(2)}) copy-start(bf16[144,2048]{1,0:T(8,128)(2,1)} %param.9) | copy-start | bytes 1769476
  2.6 26.4 %all-to-all-start.1 = ((bf16[16,144,256]{2,1,0:T(8,128)(2,1)}), bf16[16,144,256]{2,1,0:T(8,128)(2,1)S(1)}, u32[]{:S(2)}, u32[]{:S(2)}) async-start(bf16[16,144,256]{2,1,0:T(8,128)(2,1)} %shard_map.73), calls=%async_computation.1 | async-start | bytes 2359296 | tf_op jit(solution)/shard_map/all_to_all | solution.py:208
  11.6 26.5 %copy-start.6 = (s32[6,18]{1,0:T(8,128)S(1)}, s32[6,18]{1,0:T(8,128)}, u32[]{:S(2)}) copy-start(s32[6,18]{1,0:T(8,128)} %param.12) | copy-start | bytes 1300
  29.0 1.0 copy-start.3
  30.0 29.9 %all-to-all-start = ((bf16[16,144,384]{2,1,0:T(8,128)(2,1)}), bf16[16,144,384]{2,1,0:T(8,128)(2,1)S(1)}, u32[]{:S(2)}, u32[]{:S(2)}) async-start(bf16[16,144,384]{2,1,0:T(8,128)(2,1)} %maximum_bitcast_fusion), calls=%async_computation | async-start | bytes 3538944 | tf_op jit(solution)/shard_map/all_to_all | solution.py:204
  33.8 37.7 %collective-permute-start.1 = (bf16[2304,256]{1,0:T(8,128)(2,1)}, bf16[2304,256]{1,0:T(8,128)(2,1)S(1)}, u32[]{:S(2)}, u32[]{:S(2)}) collective-permute-start(bf16[2304,256]{1,0:T(8,128)(2,1)} %bitcast.29), channel_id=1, source_target_pairs={{32,0},{64,32},{96,64},{128,96},{160,128},{192,160},{224,192},{33,... | collective-permute-start | bytes 3538952 | tf_op jit(solution)/shard_map/ppermute | solution.py:30
  35.7 35.8 %collective-permute-start = (bf16[2304,256]{1,0:T(8,128)(2,1)}, bf16[2304,256]{1,0:T(8,128)(2,1)}, u32[]{:S(2)}, u32[]{:S(2)}) collective-permute-start(bf16[2304,256]{1,0:T(8,128)(2,1)} %bitcast.30), channel_id=1, source_target_pairs={{0,32},{32,64},{64,96},{96,128},{128,160},{160,192},{192,224},{1,3... | collective-permute-start | bytes 3538952 | tf_op jit(solution)/shard_map/ppermute | solution.py:29
  59.9 1.2 %copy-start.1 = (bf16[16,144,384]{2,1,0:T(8,128)(2,1)}, bf16[16,144,384]{2,1,0:T(8,128)(2,1)S(1)}, u32[]{:S(2)}) copy-start(bf16[16,144,384]{2,1,0:T(8,128)(2,1)S(1)} %all-to-all-done) | copy-start | bytes 5308420
  71.5 1.0 copy-start.2

commit v11 on v10

--- a/solution.py
+++ b/solution.py
@@ -140,6 +140,9 @@
     def whole(array):
         return pl.BlockSpec(array.shape, lambda t, ids, cnt: (0, 0))
 
+    fresh = pltpu.with_memory_space_constraint(fresh, pltpu.VMEM)
+    resident = pl.BlockSpec(memory_space=pltpu.VMEM)
+
     tile = pl.BlockSpec((TILE_TOKENS, width), lambda t, ids, cnt: (t, 0))
     partial = jax.ShapeDtypeStruct((rows, width), jnp.float32)
     acc, tot = pl.pallas_call(
@@ -148,7 +151,7 @@
         grid_spec=pltpu.PrefetchScalarGridSpec(
             num_scalar_prefetch=2,
             grid=(tiles,),
-            in_specs=[whole(fresh)],
+            in_specs=[resident],
             out_specs=(tile, tile),
             scratch_shapes=[pltpu.SMEM((KEY_SLOTS,), jnp.int32)],
         ),
@@ -160,7 +163,7 @@
         grid_spec=pltpu.PrefetchScalarGridSpec(
             num_scalar_prefetch=2,
             grid=(tiles,),
-            in_specs=[whole(fresh), hbm, hbm, tile, tile],
+            in_specs=[resident, hbm, hbm, tile, tile],
             out_specs=tile,
             scratch_shapes=[
                 pltpu.VMEM((2 * rows, before.shape[1]), before.dtype),

time: 111 us -> 107 us (0.964); the launches traced: 109 us -> 106 us
  blocking collectives: 15.9 us -> 14.4 us
  local copies, waits for them, and re-layouts: 4.5 us -> 3.26 us
    all_to_all x1, blocking collectives: 15.9 us -> 14.4 us  [on_device(): lax.all_to_all(merged, 'seq', split_axis=0, concat_axis=1, tiled=True)]
    unnamed x14 -> x12, local copies, waits for them, and re-layouts: 3.31 us -> 2.07 us
  transfers between devices with their start and end apart: 4 -> 4, of which waited for: 2 -> 2; matrix products, arithmetic and copies ran while one was open for 2% -> 2% of each run, Pallas kernels for 9% -> 10%
where the time goes in v11:
time: 107 us; the launch traced here: 106 us
  waiting for transfers between devices  38.6 us (36%)
  Pallas kernels  32.8 us (31%)
  starting transfers between devices  15.2 us (14%)
  blocking collectives  14.4 us (13%)
  local copies, waits for them, and re-layouts  3.26 us (3%)
  other arithmetic  2.03 us (2%)
    pallas_call x2, Pallas kernels, tile_attention(): pl.pallas_call(functools.partial(attention_kernel, local_heads, per_patch...  30.2 us
    all_to_all x1, waiting for transfers between devices, interleaved(): lax.all_to_all(joined, 'seq', split_axis=0, concat_axis=0, tiled=True)  21.2 us
    all_to_all x1, waiting for transfers between devices, on_device(): lax.all_to_all(joined, 'seq', split_axis=0, concat_axis=0, tiled=True)  17.4 us
    all_to_all x1, blocking collectives, on_device(): lax.all_to_all(merged, 'seq', split_axis=0, concat_axis=1, tiled=True)  14.4 us
    all_to_all x1, starting transfers between devices, on_device(): lax.all_to_all(joined, 'seq', split_axis=0, concat_axis=0, tiled=True)  7.17 us
    all_to_all x1, starting transfers between devices, interleaved(): lax.all_to_all(joined, 'seq', split_axis=0, concat_axis=0, tiled=True)  3.71 us
    pallas_call x1, Pallas kernels, regroup(): pl.pallas_call(functools.partial(regroup_kernel, width), out_shape=jax.Sh...  2.57 us
    ppermute x1, starting transfers between devices, with_halo(): before = lax.ppermute(last, axis, up)  2.41 us
  transfers between devices with their start and end apart: 4, of which 2 were waited for; matrix products, arithmetic and copies ran while one was open for 2% of the time, Pallas kernels for 10%

profile of v11, /device:TPU:128, one launch (start us, length us, event | category | flops | bytes accessed | tf_op | source)
XLA Modules:
  0.0 106.4 jit_solution(3729054368689674436)
XLA Ops:
  0.0 0.0 copy-start
  0.0 0.0 copy-start.3
  0.0 2.6 %shard_map.73 = bf16[16,144,256]{2,1,0:T(8,128)(2,1)} custom-call(bf16[144,2048]{1,0:T(8,128)(2,1)} %refs_0_.1, bf16[144,2048]{1,0:T(8,128)(2,1)} %refs_1_.1), custom_call_target="tpu_custom_call" | custom-call | tf_op jit(solution)/shard_map/pallas_call | solution.py:190
  2.6 0.0 copy-start.4
  2.6 7.2 %all-to-all-start.1 = ((bf16[16,144,256]{2,1,0:T(8,128)(2,1)}), bf16[16,144,256]{2,1,0:T(8,128)(2,1)S(1)}, u32[]{:S(2)}, u32[]{:S(2)}) async-start(bf16[16,144,256]{2,1,0:T(8,128)(2,1)} %shard_map.73), calls=%async_computation.1 | async-start | bytes 2359296 | tf_op jit(solution)/shard_map/all_to_all | solution.py:211
  9.8 0.0 copy-done.3
  9.8 0.1 copy_bitcast_fusion.3
  9.9 0.0 copy-done
  9.9 0.0 copy-done.4
  9.9 0.2 copy_bitcast_fusion.1
  10.1 1.5 %maximum_bitcast_fusion = bf16[16,144,384]{2,1,0:T(8,128)(2,1)} fusion(bf16[144,16,128]{2,0,1:T(8,128)(2,1)S(1)} %get-tuple-element.9, bf16[144,16,128]{2,0,1:T(8,128)(2,1)S(1)} %get-tuple-element.10, bf16[144,16,128]{2,0,1:T(8,128)(2,1)S(1)} %copy_bitcast_fusion.3), kind=kLoop, calls=%fused_computation | loop fusion | flops 5308416 | bytes 3538944 | tf_op jit(solution)/shard_map/transpose | solution.py:206
  11.6 0.0 copy-start.5
  11.6 17.4 %all-to-all-done.1 = bf16[16,144,256]{2,1,0:T(8,128)(2,1)S(1)} async-done(((bf16[16,144,256]{2,1,0:T(8,128)(2,1)}), bf16[16,144,256]{2,1,0:T(8,128)(2,1)S(1)}, u32[]{:S(2)}, u32[]{:S(2)}) %all-to-all-start.1) | async-done | bytes 1179680 | tf_op jit(solution)/shard_map/all_to_all | solution.py:211
  29.0 0.0 copy-start.2
  29.0 1.0 copy-done.2
  30.0 3.7 %all-to-all-start = ((bf16[16,144,384]{2,1,0:T(8,128)(2,1)}), bf16[16,144,384]{2,1,0:T(8,128)(2,1)S(1)}, u32[]{:S(2)}, u32[]{:S(2)}) async-start(bf16[16,144,384]{2,1,0:T(8,128)(2,1)} %maximum_bitcast_fusion), calls=%async_computation | async-start | bytes 3538944 | tf_op jit(solution)/shard_map/all_to_all | solution.py:207
  33.7 1.9 %collective-permute-start.1 = (bf16[2304,256]{1,0:T(8,128)(2,1)}, bf16[2304,256]{1,0:T(8,128)(2,1)S(1)}, u32[]{:S(2)}, u32[]{:S(2)}) collective-permute-start(bf16[2304,256]{1,0:T(8,128)(2,1)} %bitcast.29), channel_id=1, source_target_pairs={{32,0},{64,32},{96,64},{128,96},{160,128},{192,160},{224,192},{33,... | collective-permute-start | bytes 3538952 | tf_op jit(solution)/shard_map/ppermute | solution.py:30
  35.6 2.4 %collective-permute-start = (bf16[2304,256]{1,0:T(8,128)(2,1)}, bf16[2304,256]{1,0:T(8,128)(2,1)}, u32[]{:S(2)}, u32[]{:S(2)}) collective-permute-start(bf16[2304,256]{1,0:T(8,128)(2,1)} %bitcast.30), channel_id=1, source_target_pairs={{0,32},{32,64},{64,96},{96,128},{128,160},{160,192},{192,224},{1,3... | collective-permute-start | bytes 3538952 | tf_op jit(solution)/shard_map/ppermute | solution.py:29
  38.1 0.0 copy-done.5
  38.1 0.6 broadcast_subtract_fusion.ids_ref
  38.7 21.2 %all-to-all-done = bf16[16,144,384]{2,1,0:T(8,128)(2,1)S(1)} async-done(((bf16[16,144,384]{2,1,0:T(8,128)(2,1)}), bf16[16,144,384]{2,1,0:T(8,128)(2,1)S(1)}, u32[]{:S(2)}, u32[]{:S(2)}) %all-to-all-start) | async-done | bytes 1769504 | tf_op jit(solution)/shard_map/all_to_all | solution.py:207
  59.9 10.6 %shard_map.74 = (f32[2304,128]{1,0:T(8,128)}, f32[2304,128]{1,0:T(8,128)}) custom-call(s32[6,18]{1,0:T(8,128)} %broadcast_subtract_fusion.ids_ref, s32[6]{0:T(128)} %count_ref.3, bf16[2304,384]{1,0:T(8,128)(2,1)S(1)} %bitcast.26), custom_call_target="tpu_custom_call" | custom-call | tf_op jit(solution)/shard_map/pallas_call | solution.py:148
  70.5 0.0 collective-permute-done.1.refs_1_
  70.5 0.0 copy-start.1
  70.5 0.0 collective-permute-done.refs_0_
  70.5 1.0 copy-done.1
  71.5 19.6 %shard_map.75 = bf16[2304,128]{1,0:T(8,128)(2,1)} custom-call(s32[6,18]{1,0:T(8,128)} %broadcast_subtract_fusion.ids_ref, s32[6]{0:T(128)} %count_ref.3, bf16[2304,384]{1,0:T(8,128)(2,1)S(1)} %bitcast.27, bf16[2304,256]{1,0:T(8,128)(2,1)} %collective-permute-done.refs_0_, bf16[2304,256]{1,0:T(8,128)(2,1)} %copy-done.1, ...), custom_call_target="tpu_custom_call" | custom-call | tf_op jit(solution)/shard_map/pallas_call | solution.py:160
  91.1 14.4 %all_to_all.29 = bf16[16,144,128]{2,1,0:T(8,128)(2,1)S(1)} all-to-all(bf16[16,144,128]{2,1,0:T(8,128)(2,1)} %bitcast.28), channel_id=1, replica_groups=mesh['patch'=8,'seq'=16,'cfg'=2] {'seq'}, dimensions={0} | all-to-all | bytes 1179648 | tf_op jit(solution)/shard_map/all_to_all | solution.py:222
  105.5 0.9 copy_bitcast_fusion
Async XLA Ops:
  0.0 9.9 %copy-start = (bf16[144,2048]{1,0:T(8,128)(2,1)S(1)}, bf16[144,2048]{1,0:T(8,128)(2,1)}, u32[]{:S(2)}) copy-start(bf16[144,2048]{1,0:T(8,128)(2,1)} %param.8) | copy-start | bytes 1769476
  0.0 9.8 %copy-start.3 = (bf16[144,2048]{1,0:T(8,128)(2,1)S(1)}, bf16[144,2048]{1,0:T(8,128)(2,1)}, u32[]{:S(2)}) copy-start(bf16[144,2048]{1,0:T(8,128)(2,1)} %param.7) | copy-start | bytes 1769476
  2.6 7.3 %copy-start.4 = (bf16[144,2048]{1,0:T(8,128)(2,1)S(1)}, bf16[144,2048]{1,0:T(8,128)(2,1)}, u32[]{:S(2)}) copy-start(bf16[144,2048]{1,0:T(8,128)(2,1)} %param.9) | copy-start | bytes 1769476
  2.6 26.4 %all-to-all-start.1 = ((bf16[16,144,256]{2,1,0:T(8,128)(2,1)}), bf16[16,144,256]{2,1,0:T(8,128)(2,1)S(1)}, u32[]{:S(2)}, u32[]{:S(2)}) async-start(bf16[16,144,256]{2,1,0:T(8,128)(2,1)} %shard_map.73), calls=%async_computation.1 | async-start | bytes 2359296 | tf_op jit(solution)/shard_map/all_to_all | solution.py:211
  11.6 26.5 %copy-start.5 = (s32[6,18]{1,0:T(8,128)S(1)}, s32[6,18]{1,0:T(8,128)}, u32[]{:S(2)}) copy-start(s32[6,18]{1,0:T(8,128)} %param.12) | copy-start | bytes 1300
  29.0 1.0 copy-start.2
  30.0 29.9 %all-to-all-start = ((bf16[16,144,384]{2,1,0:T(8,128)(2,1)}), bf16[16,144,384]{2,1,0:T(8,128)(2,1)S(1)}, u32[]{:S(2)}, u32[]{:S(2)}) async-start(bf16[16,144,384]{2,1,0:T(8,128)(2,1)} %maximum_bitcast_fusion), calls=%async_computation | async-start | bytes 3538944 | tf_op jit(solution)/shard_map/all_to_all | solution.py:207
  33.7 36.7 %collective-permute-start.1 = (bf16[2304,256]{1,0:T(8,128)(2,1)}, bf16[2304,256]{1,0:T(8,128)(2,1)S(1)}, u32[]{:S(2)}, u32[]{:S(2)}) collective-permute-start(bf16[2304,256]{1,0:T(8,128)(2,1)} %bitcast.29), channel_id=1, source_target_pairs={{32,0},{64,32},{96,64},{128,96},{160,128},{192,160},{224,192},{33,... | collective-permute-start | bytes 3538952 | tf_op jit(solution)/shard_map/ppermute | solution.py:30
  35.6 34.8 %collective-permute-start = (bf16[2304,256]{1,0:T(8,128)(2,1)}, bf16[2304,256]{1,0:T(8,128)(2,1)}, u32[]{:S(2)}, u32[]{:S(2)}) collective-permute-start(bf16[2304,256]{1,0:T(8,128)(2,1)} %bitcast.30), channel_id=1, source_target_pairs={{0,32},{32,64},{64,96},{96,128},{128,160},{160,192},{192,224},{1,3... | collective-permute-start | bytes 3538952 | tf_op jit(solution)/shard_map/ppermute | solution.py:29
  70.5 1.0 copy-start.1

commit v12 on v11

--- a/solution.py
+++ b/solution.py
@@ -179,17 +179,20 @@
 
 def regroup_kernel(width, *refs):
     *in_refs, o_ref = refs
-    seq_count = o_ref.shape[0]
-    for d in range(seq_count):
+    for d in range(o_ref.shape[0]):
         for a, ref in enumerate(in_refs):
             o_ref[d, :, a * width:(a + 1) * width] = ref[:, d * width:(d + 1) * width]
 
 
-def regroup(arrays, seq_count, width):
+def regroup(arrays, seq_count, width, steps=4):
     rows = arrays[0].shape[0]
+    per_step = seq_count // steps
     return pl.pallas_call(
         functools.partial(regroup_kernel, width),
         out_shape=jax.ShapeDtypeStruct((seq_count, rows, len(arrays) * width), arrays[0].dtype),
+        grid=(steps,),
+        in_specs=[pl.BlockSpec((rows, per_step * width), lambda i: (0, i))] * len(arrays),
+        out_specs=pl.BlockSpec((per_step, rows, len(arrays) * width), lambda i: (i, 0, 0)),
     )(*arrays)
 
 

time: 107 us -> 108 us (level)
  transfers between devices with their start and end apart: 4 -> 4, of which waited for: 2 -> 2; matrix products, arithmetic and copies ran while one was open for 2% -> 2% of each run, Pallas kernels for 10% -> 9%
where the time goes in v12:
time: 108 us
  waiting for transfers between devices  38.6 us (36%)
  Pallas kernels  33.4 us (31%)
  starting transfers between devices  15.2 us (14%)
  blocking collectives  15.2 us (14%)
  local copies, waits for them, and re-layouts  3.26 us (3%)
  other arithmetic  2.03 us (2%)
    pallas_call x2, Pallas kernels, tile_attention(): pl.pallas_call(functools.partial(attention_kernel, local_heads, per_patch...  29.8 us
    all_to_all x1, waiting for transfers between devices, interleaved(): lax.all_to_all(joined, 'seq', split_axis=0, concat_axis=0, tiled=True)  21.2 us
    all_to_all x1, waiting for transfers between devices, on_device(): lax.all_to_all(joined, 'seq', split_axis=0, concat_axis=0, tiled=True)  17.4 us
    all_to_all x1, blocking collectives, on_device(): lax.all_to_all(merged, 'seq', split_axis=0, concat_axis=1, tiled=True)  15.2 us
    all_to_all x1, starting transfers between devices, on_device(): lax.all_to_all(joined, 'seq', split_axis=0, concat_axis=0, tiled=True)  7.17 us
    all_to_all x1, starting transfers between devices, interleaved(): lax.all_to_all(joined, 'seq', split_axis=0, concat_axis=0, tiled=True)  3.71 us
    pallas_call x1, Pallas kernels, regroup(): pl.pallas_call(functools.partial(regroup_kernel, width), out_shape=jax.Sh...  3.62 us
    ppermute x1, starting transfers between devices, with_halo(): before = lax.ppermute(last, axis, up)  2.41 us
  transfers between devices with their start and end apart: 4, of which 2 were waited for; matrix products, arithmetic and copies ran while one was open for 2% of the time, Pallas kernels for 9%

profile of v12, /device:TPU:128, one launch (start us, length us, event | category | flops | bytes accessed | tf_op | source)
XLA Modules:
  0.0 107.9 jit_solution(14558543543068945970)
XLA Ops:
  0.0 0.0 copy-start
  0.0 0.0 copy-start.3
  0.0 3.6 %shard_map.73 = bf16[16,144,256]{2,1,0:T(8,128)(2,1)} custom-call(bf16[144,2048]{1,0:T(8,128)(2,1)} %refs_0_.1, bf16[144,2048]{1,0:T(8,128)(2,1)} %refs_1_.1), custom_call_target="tpu_custom_call" | custom-call | tf_op jit(solution)/shard_map/pallas_call | solution.py:190
  3.6 0.0 copy-start.4
  3.6 7.2 %all-to-all-start.1 = ((bf16[16,144,256]{2,1,0:T(8,128)(2,1)}), bf16[16,144,256]{2,1,0:T(8,128)(2,1)S(1)}, u32[]{:S(2)}, u32[]{:S(2)}) async-start(bf16[16,144,256]{2,1,0:T(8,128)(2,1)} %shard_map.73), calls=%async_computation.1 | async-start | bytes 2359296 | tf_op jit(solution)/shard_map/all_to_all | solution.py:214
  10.8 0.0 copy-done.3
  10.8 0.1 copy_bitcast_fusion.3
  10.9 0.0 copy-done
  10.9 0.0 copy-done.4
  10.9 0.2 copy_bitcast_fusion.1
  11.2 1.5 %maximum_bitcast_fusion = bf16[16,144,384]{2,1,0:T(8,128)(2,1)} fusion(bf16[144,16,128]{2,0,1:T(8,128)(2,1)S(1)} %get-tuple-element.9, bf16[144,16,128]{2,0,1:T(8,128)(2,1)S(1)} %get-tuple-element.10, bf16[144,16,128]{2,0,1:T(8,128)(2,1)S(1)} %copy_bitcast_fusion.3), kind=kLoop, calls=%fused_computation | loop fusion | flops 5308416 | bytes 3538944 | tf_op jit(solution)/shard_map/transpose | solution.py:209
  12.6 0.0 copy-start.5
  12.6 17.4 %all-to-all-done.1 = bf16[16,144,256]{2,1,0:T(8,128)(2,1)S(1)} async-done(((bf16[16,144,256]{2,1,0:T(8,128)(2,1)}), bf16[16,144,256]{2,1,0:T(8,128)(2,1)S(1)}, u32[]{:S(2)}, u32[]{:S(2)}) %all-to-all-start.1) | async-done | bytes 1179680 | tf_op jit(solution)/shard_map/all_to_all | solution.py:214
  30.0 0.0 copy-start.2
  30.0 1.0 copy-done.2
  31.1 3.7 %all-to-all-start = ((bf16[16,144,384]{2,1,0:T(8,128)(2,1)}), bf16[16,144,384]{2,1,0:T(8,128)(2,1)S(1)}, u32[]{:S(2)}, u32[]{:S(2)}) async-start(bf16[16,144,384]{2,1,0:T(8,128)(2,1)} %maximum_bitcast_fusion), calls=%async_computation | async-start | bytes 3538944 | tf_op jit(solution)/shard_map/all_to_all | solution.py:210
  34.8 1.9 %collective-permute-start.1 = (bf16[2304,256]{1,0:T(8,128)(2,1)}, bf16[2304,256]{1,0:T(8,128)(2,1)S(1)}, u32[]{:S(2)}, u32[]{:S(2)}) collective-permute-start(bf16[2304,256]{1,0:T(8,128)(2,1)} %bitcast.29), channel_id=1, source_target_pairs={{32,0},{64,32},{96,64},{128,96},{160,128},{192,160},{224,192},{33,... | collective-permute-start | bytes 3538952 | tf_op jit(solution)/shard_map/ppermute | solution.py:30
  36.7 2.4 %collective-permute-start = (bf16[2304,256]{1,0:T(8,128)(2,1)}, bf16[2304,256]{1,0:T(8,128)(2,1)}, u32[]{:S(2)}, u32[]{:S(2)}) collective-permute-start(bf16[2304,256]{1,0:T(8,128)(2,1)} %bitcast.30), channel_id=1, source_target_pairs={{0,32},{32,64},{64,96},{96,128},{128,160},{160,192},{192,224},{1,3... | collective-permute-start | bytes 3538952 | tf_op jit(solution)/shard_map/ppermute | solution.py:29
  39.1 0.0 copy-done.5
  39.1 0.6 broadcast_subtract_fusion.ids_ref
  39.7 21.2 %all-to-all-done = bf16[16,144,384]{2,1,0:T(8,128)(2,1)S(1)} async-done(((bf16[16,144,384]{2,1,0:T(8,128)(2,1)}), bf16[16,144,384]{2,1,0:T(8,128)(2,1)S(1)}, u32[]{:S(2)}, u32[]{:S(2)}) %all-to-all-start) | async-done | bytes 1769504 | tf_op jit(solution)/shard_map/all_to_all | solution.py:210
  60.9 10.1 %shard_map.74 = (f32[2304,128]{1,0:T(8,128)}, f32[2304,128]{1,0:T(8,128)}) custom-call(s32[6,18]{1,0:T(8,128)} %broadcast_subtract_fusion.ids_ref, s32[6]{0:T(128)} %count_ref.3, bf16[2304,384]{1,0:T(8,128)(2,1)S(1)} %bitcast.26), custom_call_target="tpu_custom_call" | custom-call | tf_op jit(solution)/shard_map/pallas_call | solution.py:148
  71.0 0.0 collective-permute-done.1.refs_1_
  71.0 0.0 copy-start.1
  71.0 0.0 collective-permute-done.refs_0_
  71.0 1.0 copy-done.1
  72.1 19.7 %shard_map.75 = bf16[2304,128]{1,0:T(8,128)(2,1)} custom-call(s32[6,18]{1,0:T(8,128)} %broadcast_subtract_fusion.ids_ref, s32[6]{0:T(128)} %count_ref.3, bf16[2304,384]{1,0:T(8,128)(2,1)S(1)} %bitcast.27, bf16[2304,256]{1,0:T(8,128)(2,1)} %collective-permute-done.refs_0_, bf16[2304,256]{1,0:T(8,128)(2,1)} %copy-done.1, ...), custom_call_target="tpu_custom_call" | custom-call | tf_op jit(solution)/shard_map/pallas_call | solution.py:160
  91.8 15.2 %all_to_all.29 = bf16[16,144,128]{2,1,0:T(8,128)(2,1)S(1)} all-to-all(bf16[16,144,128]{2,1,0:T(8,128)(2,1)} %bitcast.28), channel_id=1, replica_groups=mesh['patch'=8,'seq'=16,'cfg'=2] {'seq'}, dimensions={0} | all-to-all | bytes 1179648 | tf_op jit(solution)/shard_map/all_to_all | solution.py:225
  107.0 0.9 copy_bitcast_fusion
Async XLA Ops:
  0.0 10.9 %copy-start = (bf16[144,2048]{1,0:T(8,128)(2,1)S(1)}, bf16[144,2048]{1,0:T(8,128)(2,1)}, u32[]{:S(2)}) copy-start(bf16[144,2048]{1,0:T(8,128)(2,1)} %param.8) | copy-start | bytes 1769476
  0.0 10.8 %copy-start.3 = (bf16[144,2048]{1,0:T(8,128)(2,1)S(1)}, bf16[144,2048]{1,0:T(8,128)(2,1)}, u32[]{:S(2)}) copy-start(bf16[144,2048]{1,0:T(8,128)(2,1)} %param.7) | copy-start | bytes 1769476
  3.6 7.3 %copy-start.4 = (bf16[144,2048]{1,0:T(8,128)(2,1)S(1)}, bf16[144,2048]{1,0:T(8,128)(2,1)}, u32[]{:S(2)}) copy-start(bf16[144,2048]{1,0:T(8,128)(2,1)} %param.9) | copy-start | bytes 1769476
  3.6 26.4 %all-to-all-start.1 = ((bf16[16,144,256]{2,1,0:T(8,128)(2,1)}), bf16[16,144,256]{2,1,0:T(8,128)(2,1)S(1)}, u32[]{:S(2)}, u32[]{:S(2)}) async-start(bf16[16,144,256]{2,1,0:T(8,128)(2,1)} %shard_map.73), calls=%async_computation.1 | async-start | bytes 2359296 | tf_op jit(solution)/shard_map/all_to_all | solution.py:214
  12.6 26.5 %copy-start.5 = (s32[6,18]{1,0:T(8,128)S(1)}, s32[6,18]{1,0:T(8,128)}, u32[]{:S(2)}) copy-start(s32[6,18]{1,0:T(8,128)} %param.12) | copy-start | bytes 1300
  30.0 1.0 copy-start.2
  31.1 29.9 %all-to-all-start = ((bf16[16,144,384]{2,1,0:T(8,128)(2,1)}), bf16[16,144,384]{2,1,0:T(8,128)(2,1)S(1)}, u32[]{:S(2)}, u32[]{:S(2)}) async-start(bf16[16,144,384]{2,1,0:T(8,128)(2,1)} %maximum_bitcast_fusion), calls=%async_computation | async-start | bytes 3538944 | tf_op jit(solution)/shard_map/all_to_all | solution.py:210
  34.8 36.2 %collective-permute-start.1 = (bf16[2304,256]{1,0:T(8,128)(2,1)}, bf16[2304,256]{1,0:T(8,128)(2,1)S(1)}, u32[]{:S(2)}, u32[]{:S(2)}) collective-permute-start(bf16[2304,256]{1,0:T(8,128)(2,1)} %bitcast.29), channel_id=1, source_target_pairs={{32,0},{64,32},{96,64},{128,96},{160,128},{192,160},{224,192},{33,... | collective-permute-start | bytes 3538952 | tf_op jit(solution)/shard_map/ppermute | solution.py:30
  36.7 34.3 %collective-permute-start = (bf16[2304,256]{1,0:T(8,128)(2,1)}, bf16[2304,256]{1,0:T(8,128)(2,1)}, u32[]{:S(2)}, u32[]{:S(2)}) collective-permute-start(bf16[2304,256]{1,0:T(8,128)(2,1)} %bitcast.30), channel_id=1, source_target_pairs={{0,32},{32,64},{64,96},{96,128},{128,160},{160,192},{192,224},{1,3... | collective-permute-start | bytes 3538952 | tf_op jit(solution)/shard_map/ppermute | solution.py:29
  71.0 1.0 copy-start.1

commit v13 on v11

--- a/solution.py
+++ b/solution.py
@@ -193,6 +193,19 @@
     )(*arrays)
 
 
+def pass_kernel(x_ref, o_ref):
+    o_ref[...] = x_ref[...]
+
+
+def out_of_vmem(x):
+    x = pltpu.with_memory_space_constraint(x, pltpu.VMEM)
+    return pl.pallas_call(
+        pass_kernel,
+        out_shape=jax.ShapeDtypeStruct(x.shape, x.dtype),
+        in_specs=[pl.BlockSpec(memory_space=pltpu.VMEM)],
+    )(x)
+
+
 def on_device(query, fresh_key, fresh_value, stale_key, stale_value, key_tiles, tile_count):
     seq_count = lax.axis_size("seq")
     local_heads = NUM_HEADS // seq_count
@@ -209,7 +222,7 @@
 
     joined = regroup([stale_key, stale_value], seq_count, width)
     stale = lax.all_to_all(joined, "seq", split_axis=0, concat_axis=0, tiled=True)
-    stale = stale.reshape(patch_rows, 2 * width)
+    stale = out_of_vmem(stale.reshape(patch_rows, 2 * width))
     framed = with_halo(stale, (("patch", 0),), patch_rows)
     before = framed[:patch_rows]
     after = framed[2 * patch_rows :]

time: 107 us -> 109 us (1.019); the launches traced: 106 us -> 107 us
  waiting for transfers between devices: 38.6 us -> 36.3 us
  blocking collectives: 14.4 us -> 16.7 us
    all_to_all x1, blocking collectives: 14.4 us -> 16.7 us  [on_device(): lax.all_to_all(merged, 'seq', split_axis=0, concat_axis=1, tiled=True)]
    all_to_all x1, waiting for transfers between devices: 21.2 us -> 18.9 us  [interleaved(): lax.all_to_all(joined, 'seq', split_axis=0, concat_axis=0, tiled=True)]
    pallas_call x0 -> x1, Pallas kernels: none -> 1.11 us  [out_of_vmem(): pl.pallas_call(pass_kernel, out_shape=jax.ShapeDtypeStruct(x.shape, x.dty...]
  transfers between devices with their start and end apart: 4 -> 4, of which waited for: 2 -> 2; matrix products, arithmetic and copies ran while one was open for 2% -> 2% of each run, Pallas kernels for 10% -> 12%
where the time goes in v13:
time: 109 us; the launch traced here: 107 us
  waiting for transfers between devices  36.3 us (33%)
  Pallas kernels  33.3 us (31%)
  blocking collectives  16.7 us (15%)
  starting transfers between devices  15.9 us (15%)
  local copies, waits for them, and re-layouts  2.23 us (2%)
  other arithmetic  2.07 us (2%)
    pallas_call x2, Pallas kernels, tile_attention(): pl.pallas_call(functools.partial(attention_kernel, local_heads, per_patch...  29.6 us
    all_to_all x1, waiting for transfers between devices, interleaved(): lax.all_to_all(joined, 'seq', split_axis=0, concat_axis=0, tiled=True)  18.9 us
    all_to_all x1, waiting for transfers between devices, on_device(): lax.all_to_all(joined, 'seq', split_axis=0, concat_axis=0, tiled=True)  17.4 us
    all_to_all x1, blocking collectives, on_device(): lax.all_to_all(merged, 'seq', split_axis=0, concat_axis=1, tiled=True)  16.7 us
    all_to_all x1, starting transfers between devices, on_device(): lax.all_to_all(joined, 'seq', split_axis=0, concat_axis=0, tiled=True)  7.17 us
    all_to_all x1, starting transfers between devices, interleaved(): lax.all_to_all(joined, 'seq', split_axis=0, concat_axis=0, tiled=True)  4.4 us
    pallas_call x1, Pallas kernels, regroup(): pl.pallas_call(functools.partial(regroup_kernel, width), out_shape=jax.Sh...  2.57 us
    ppermute x1, starting transfers between devices, with_halo(): before = lax.ppermute(last, axis, up)  2.41 us
  transfers between devices with their start and end apart: 4, of which 2 were waited for; matrix products, arithmetic and copies ran while one was open for 2% of the time, Pallas kernels for 12%

profile of v13, /device:TPU:128, one launch (start us, length us, event | category | flops | bytes accessed | tf_op | source)
XLA Modules:
  0.0 106.6 jit_solution(17968515354498951129)
XLA Ops:
  0.0 0.0 copy-start
  0.0 0.0 copy-start.2
  0.0 2.6 %shard_map.73 = bf16[16,144,256]{2,1,0:T(8,128)(2,1)} custom-call(bf16[144,2048]{1,0:T(8,128)(2,1)} %refs_0_.1, bf16[144,2048]{1,0:T(8,128)(2,1)} %refs_1_.1), custom_call_target="tpu_custom_call" | custom-call | tf_op jit(solution)/shard_map/pallas_call | solution.py:190
  2.6 0.0 copy-start.3
  2.6 7.2 %all-to-all-start.1 = ((bf16[16,144,256]{2,1,0:T(8,128)(2,1)}), bf16[16,144,256]{2,1,0:T(8,128)(2,1)S(1)}, u32[]{:S(2)}, u32[]{:S(2)}) async-start(bf16[16,144,256]{2,1,0:T(8,128)(2,1)} %shard_map.73), calls=%async_computation.1 | async-start | bytes 2359296 | tf_op jit(solution)/shard_map/all_to_all | solution.py:224
  9.8 0.0 copy-done.2
  9.8 0.1 copy_bitcast_fusion.3
  9.9 0.0 copy-done
  9.9 0.0 copy-done.3
  9.9 0.2 copy_bitcast_fusion.1
  10.1 1.5 %maximum_bitcast_fusion = bf16[16,144,384]{2,1,0:T(8,128)(2,1)} fusion(bf16[144,16,128]{2,0,1:T(8,128)(2,1)S(1)} %get-tuple-element.9, bf16[144,16,128]{2,0,1:T(8,128)(2,1)S(1)} %get-tuple-element.10, bf16[144,16,128]{2,0,1:T(8,128)(2,1)S(1)} %copy_bitcast_fusion.3), kind=kLoop, calls=%fused_computation | loop fusion | flops 5308416 | bytes 3538944 | tf_op jit(solution)/shard_map/transpose | solution.py:219
  11.6 17.4 %all-to-all-done.1 = bf16[16,144,256]{2,1,0:T(8,128)(2,1)S(1)} async-done(((bf16[16,144,256]{2,1,0:T(8,128)(2,1)}), bf16[16,144,256]{2,1,0:T(8,128)(2,1)S(1)}, u32[]{:S(2)}, u32[]{:S(2)}) %all-to-all-start.1) | async-done | bytes 1179680 | tf_op jit(solution)/shard_map/all_to_all | solution.py:224
  29.0 4.4 %all-to-all-start = ((bf16[16,144,384]{2,1,0:T(8,128)(2,1)}), bf16[16,144,384]{2,1,0:T(8,128)(2,1)}, u32[]{:S(2)}, u32[]{:S(2)}) async-start(bf16[16,144,384]{2,1,0:T(8,128)(2,1)} %maximum_bitcast_fusion), calls=%async_computation | async-start | bytes 3538944 | tf_op jit(solution)/shard_map/all_to_all | solution.py:220
  33.4 0.0 copy-start.4
  33.4 1.1 %shard_map.74 = bf16[2304,256]{1,0:T(8,128)(2,1)} custom-call(bf16[2304,256]{1,0:T(8,128)(2,1)S(1)} %bitcast.26), custom_call_target="tpu_custom_call" | custom-call | tf_op jit(solution)/shard_map/pallas_call | solution.py:202
  34.5 1.9 %collective-permute-start.1 = (bf16[2304,256]{1,0:T(8,128)(2,1)}, bf16[2304,256]{1,0:T(8,128)(2,1)S(1)}, u32[]{:S(2)}, u32[]{:S(2)}) collective-permute-start(bf16[2304,256]{1,0:T(8,128)(2,1)} %shard_map.74), channel_id=1, source_target_pairs={{32,0},{64,32},{96,64},{128,96},{160,128},{192,160},{224,192},{33,... | collective-permute-start | bytes 3538952 | tf_op jit(solution)/shard_map/ppermute | solution.py:30
  36.4 2.4 %collective-permute-start = (bf16[2304,256]{1,0:T(8,128)(2,1)}, bf16[2304,256]{1,0:T(8,128)(2,1)}, u32[]{:S(2)}, u32[]{:S(2)}) collective-permute-start(bf16[2304,256]{1,0:T(8,128)(2,1)} %shard_map.74), channel_id=1, source_target_pairs={{0,32},{32,64},{64,96},{96,128},{128,160},{160,192},{192,224},{1,3... | collective-permute-start | bytes 3538952 | tf_op jit(solution)/shard_map/ppermute | solution.py:29
  38.9 0.0 copy-done.4
  38.9 0.6 broadcast_subtract_fusion.ids_ref
  39.5 18.9 %all-to-all-done = bf16[16,144,384]{2,1,0:T(8,128)(2,1)} async-done(((bf16[16,144,384]{2,1,0:T(8,128)(2,1)}), bf16[16,144,384]{2,1,0:T(8,128)(2,1)}, u32[]{:S(2)}, u32[]{:S(2)}) %all-to-all-start) | async-done | bytes 1769504 | tf_op jit(solution)/shard_map/all_to_all | solution.py:220
  58.3 11.3 %shard_map.75 = (f32[2304,128]{1,0:T(8,128)}, f32[2304,128]{1,0:T(8,128)}) custom-call(s32[6,18]{1,0:T(8,128)} %broadcast_subtract_fusion.ids_ref, s32[6]{0:T(128)} %count_ref.3, bf16[2304,384]{1,0:T(8,128)(2,1)} %bitcast.1.fresh_ref), custom_call_target="tpu_custom_call" | custom-call | tf_op jit(solution)/shard_map/pallas_call | solution.py:148
  69.7 0.0 collective-permute-done.1.refs_1_
  69.7 0.0 copy-start.1
  69.7 0.0 collective-permute-done.refs_0_
  69.7 1.0 copy-done.1
  70.7 18.3 %shard_map.76 = bf16[2304,128]{1,0:T(8,128)(2,1)} custom-call(s32[6,18]{1,0:T(8,128)} %broadcast_subtract_fusion.ids_ref, s32[6]{0:T(128)} %count_ref.3, bf16[2304,384]{1,0:T(8,128)(2,1)} %bitcast.1.fresh_ref, bf16[2304,256]{1,0:T(8,128)(2,1)} %collective-permute-done.refs_0_, bf16[2304,256]{1,0:T(8,128)(2,1)} %copy-done.1, ...), custom_call_target="tpu_custom_call" | custom-call | tf_op jit(solution)/shard_map/pallas_call | solution.py:160
  89.0 16.7 %all_to_all.29 = bf16[16,144,128]{2,1,0:T(8,128)(2,1)S(1)} all-to-all(bf16[16,144,128]{2,1,0:T(8,128)(2,1)} %bitcast.27), channel_id=1, replica_groups=mesh['patch'=8,'seq'=16,'cfg'=2] {'seq'}, dimensions={0} | all-to-all | bytes 1179648 | tf_op jit(solution)/shard_map/all_to_all | solution.py:235
  105.7 0.9 copy_bitcast_fusion
Async XLA Ops:
  0.0 9.9 %copy-start = (bf16[144,2048]{1,0:T(8,128)(2,1)S(1)}, bf16[144,2048]{1,0:T(8,128)(2,1)}, u32[]{:S(2)}) copy-start(bf16[144,2048]{1,0:T(8,128)(2,1)} %param.8) | copy-start | bytes 1769476
  0.0 9.8 %copy-start.2 = (bf16[144,2048]{1,0:T(8,128)(2,1)S(1)}, bf16[144,2048]{1,0:T(8,128)(2,1)}, u32[]{:S(2)}) copy-start(bf16[144,2048]{1,0:T(8,128)(2,1)} %param.7) | copy-start | bytes 1769476
  2.6 7.3 %copy-start.3 = (bf16[144,2048]{1,0:T(8,128)(2,1)S(1)}, bf16[144,2048]{1,0:T(8,128)(2,1)}, u32[]{:S(2)}) copy-start(bf16[144,2048]{1,0:T(8,128)(2,1)} %param.9) | copy-start | bytes 1769476
  2.6 26.4 %all-to-all-start.1 = ((bf16[16,144,256]{2,1,0:T(8,128)(2,1)}), bf16[16,144,256]{2,1,0:T(8,128)(2,1)S(1)}, u32[]{:S(2)}, u32[]{:S(2)}) async-start(bf16[16,144,256]{2,1,0:T(8,128)(2,1)} %shard_map.73), calls=%async_computation.1 | async-start | bytes 2359296 | tf_op jit(solution)/shard_map/all_to_all | solution.py:224
  29.0 29.4 %all-to-all-start = ((bf16[16,144,384]{2,1,0:T(8,128)(2,1)}), bf16[16,144,384]{2,1,0:T(8,128)(2,1)}, u32[]{:S(2)}, u32[]{:S(2)}) async-start(bf16[16,144,384]{2,1,0:T(8,128)(2,1)} %maximum_bitcast_fusion), calls=%async_computation | async-start | bytes 3538944 | tf_op jit(solution)/shard_map/all_to_all | solution.py:220
  33.4 5.5 %copy-start.4 = (s32[6,18]{1,0:T(8,128)S(1)}, s32[6,18]{1,0:T(8,128)}, u32[]{:S(2)}) copy-start(s32[6,18]{1,0:T(8,128)} %param.12) | copy-start | bytes 1300
  34.5 35.1 %collective-permute-start.1 = (bf16[2304,256]{1,0:T(8,128)(2,1)}, bf16[2304,256]{1,0:T(8,128)(2,1)S(1)}, u32[]{:S(2)}, u32[]{:S(2)}) collective-permute-start(bf16[2304,256]{1,0:T(8,128)(2,1)} %shard_map.74), channel_id=1, source_target_pairs={{32,0},{64,32},{96,64},{128,96},{160,128},{192,160},{224,192},{33,... | collective-permute-start | bytes 3538952 | tf_op jit(solution)/shard_map/ppermute | solution.py:30
  36.4 33.2 %collective-permute-start = (bf16[2304,256]{1,0:T(8,128)(2,1)}, bf16[2304,256]{1,0:T(8,128)(2,1)}, u32[]{:S(2)}, u32[]{:S(2)}) collective-permute-start(bf16[2304,256]{1,0:T(8,128)(2,1)} %shard_map.74), channel_id=1, source_target_pairs={{0,32},{32,64},{64,96},{96,128},{128,160},{160,192},{192,224},{1,3... | collective-permute-start | bytes 3538952 | tf_op jit(solution)/shard_map/ppermute | solution.py:29
  69.7 1.0 copy-start.1

commit v14 on v8

--- a/solution.py
+++ b/solution.py
@@ -135,6 +135,9 @@
     def whole(array):
         return pl.BlockSpec(array.shape, lambda t, ids, cnt: (0, 0))
 
+    fresh = pltpu.with_memory_space_constraint(fresh, pltpu.VMEM)
+    resident = pl.BlockSpec(memory_space=pltpu.VMEM)
+
     tile = pl.BlockSpec((TILE_TOKENS, width), lambda t, ids, cnt: (t, 0))
     partial = jax.ShapeDtypeStruct((rows, width), jnp.float32)
     acc, tot = pl.pallas_call(
@@ -143,7 +146,7 @@
         grid_spec=pltpu.PrefetchScalarGridSpec(
             num_scalar_prefetch=2,
             grid=(tiles,),
-            in_specs=[whole(fresh)],
+            in_specs=[resident],
             out_specs=(tile, tile),
             scratch_shapes=[pltpu.SMEM((KEY_SLOTS,), jnp.int32)],
         ),
@@ -155,7 +158,7 @@
         grid_spec=pltpu.PrefetchScalarGridSpec(
             num_scalar_prefetch=2,
             grid=(tiles,),
-            in_specs=[whole(fresh), hbm, hbm, tile, tile],
+            in_specs=[resident, hbm, hbm, tile, tile],
             out_specs=tile,
             scratch_shapes=[
                 pltpu.VMEM((2 * rows, before.shape[1]), before.dtype),
@@ -169,6 +172,22 @@
     )(local_ids, tile_count, fresh, before, after, acc, tot)
 
 
+def regroup_kernel(width, *refs):
+    *in_refs, o_ref = refs
+    seq_count = o_ref.shape[0]
+    for d in range(seq_count):
+        for a, ref in enumerate(in_refs):
+            o_ref[d, :, a * width:(a + 1) * width] = ref[:, d * width:(d + 1) * width]
+
+
+def regroup(arrays, seq_count, width):
+    rows = arrays[0].shape[0]
+    return pl.pallas_call(
+        functools.partial(regroup_kernel, width),
+        out_shape=jax.ShapeDtypeStruct((seq_count, rows, len(arrays) * width), arrays[0].dtype),
+    )(*arrays)
+
+
 def on_device(query, fresh_key, fresh_value, stale_key, stale_value, key_tiles, tile_count):
     seq_count = lax.axis_size("seq")
     local_heads = NUM_HEADS // seq_count
@@ -183,7 +202,9 @@
         moved = lax.all_to_all(joined, "seq", split_axis=0, concat_axis=0, tiled=True)
         return moved.reshape(patch_rows, len(arrays) * width)
 
-    stale = interleaved([stale_key, stale_value])
+    joined = regroup([stale_key, stale_value], seq_count, width)
+    stale = lax.all_to_all(joined, "seq", split_axis=0, concat_axis=0, tiled=True)
+    stale = stale.reshape(patch_rows, 2 * width)
     framed = with_halo(stale, (("patch", 0),), patch_rows)
     before = framed[:patch_rows]
     after = framed[2 * patch_rows :]

time: 109 us -> 107 us (0.982)
  local copies, waits for them, and re-layouts: 5.78 us -> 3.26 us
  blocking collectives: 14 us -> 16.2 us
  other arithmetic: 3.22 us -> 2.03 us
    all_to_all x0 -> x1, waiting for transfers between devices: none -> 17.4 us  [on_device(): lax.all_to_all(joined, 'seq', split_axis=0, concat_axis=0, tiled=True)]
    all_to_all x2 -> x1, waiting for transfers between devices: 38.6 us -> 21.2 us  [interleaved(): lax.all_to_all(joined, 'seq', split_axis=0, concat_axis=0, tiled=True)]
    all_to_all x2 -> x1, starting transfers between devices: 10.9 us -> 3.71 us  [interleaved(): lax.all_to_all(joined, 'seq', split_axis=0, concat_axis=0, tiled=True)]
    all_to_all x0 -> x1, starting transfers between devices: none -> 7.17 us  [on_device(): lax.all_to_all(joined, 'seq', split_axis=0, concat_axis=0, tiled=True)]
    pallas_call x2, Pallas kernels: 30.8 us -> 27.3 us  [tile_attention(): pl.pallas_call(functools.partial(attention_kernel, local_heads, per_patch...]
    pallas_call x0 -> x1, Pallas kernels: none -> 2.57 us  [regroup(): pl.pallas_call(functools.partial(regroup_kernel, width), out_shape=jax.Sh...]
    all_to_all x1, blocking collectives: 14 us -> 16.2 us  [on_device(): lax.all_to_all(merged, 'seq', split_axis=0, concat_axis=1, tiled=True)]
    reshape x3 -> x2, local copies, waits for them, and re-layouts: 1.57 us -> 0.31 us  [interleaved(): parts = [a.reshape(rows, seq_count, width) for a in arrays]]
  transfers between devices with their start and end apart: 4 -> 4, of which waited for: 2 -> 2; matrix products, arithmetic and copies ran while one was open for 2% -> 2% of each run, Pallas kernels for 10% -> 9%
where the time goes in v14:
time: 107 us; the launch traced here: 105 us
  waiting for transfers between devices  38.6 us (36%)
  Pallas kernels  29.8 us (28%)
  blocking collectives  16.2 us (15%)
  starting transfers between devices  15.2 us (14%)
  local copies, waits for them, and re-layouts  3.26 us (3%)
  other arithmetic  2.03 us (2%)
    pallas_call x2, Pallas kernels, tile_attention(): pl.pallas_call(functools.partial(attention_kernel, local_heads, per_patch...  27.3 us
    all_to_all x1, waiting for transfers between devices, interleaved(): lax.all_to_all(joined, 'seq', split_axis=0, concat_axis=0, tiled=True)  21.2 us
    all_to_all x1, waiting for transfers between devices, on_device(): lax.all_to_all(joined, 'seq', split_axis=0, concat_axis=0, tiled=True)  17.4 us
    all_to_all x1, blocking collectives, on_device(): lax.all_to_all(merged, 'seq', split_axis=0, concat_axis=1, tiled=True)  16.2 us
    all_to_all x1, starting transfers between devices, on_device(): lax.all_to_all(joined, 'seq', split_axis=0, concat_axis=0, tiled=True)  7.17 us
    all_to_all x1, starting transfers between devices, interleaved(): lax.all_to_all(joined, 'seq', split_axis=0, concat_axis=0, tiled=True)  3.71 us
    pallas_call x1, Pallas kernels, regroup(): pl.pallas_call(functools.partial(regroup_kernel, width), out_shape=jax.Sh...  2.57 us
    ppermute x1, starting transfers between devices, with_halo(): before = lax.ppermute(last, axis, up)  2.41 us
  transfers between devices with their start and end apart: 4, of which 2 were waited for; matrix products, arithmetic and copies ran while one was open for 2% of the time, Pallas kernels for 9%

profile of v14, /device:TPU:128, one launch (start us, length us, event | category | flops | bytes accessed | tf_op | source)
XLA Modules:
  0.0 105.3 jit_solution(8347279543579627112)
XLA Ops:
  0.0 0.0 copy-start
  0.0 0.0 copy-start.3
  0.0 2.6 %shard_map.73 = bf16[16,144,256]{2,1,0:T(8,128)(2,1)} custom-call(bf16[144,2048]{1,0:T(8,128)(2,1)} %refs_0_.1, bf16[144,2048]{1,0:T(8,128)(2,1)} %refs_1_.1), custom_call_target="tpu_custom_call" | custom-call | tf_op jit(solution)/shard_map/pallas_call | solution.py:185
  2.6 0.0 copy-start.4
  2.6 7.2 %all-to-all-start.1 = ((bf16[16,144,256]{2,1,0:T(8,128)(2,1)}), bf16[16,144,256]{2,1,0:T(8,128)(2,1)S(1)}, u32[]{:S(2)}, u32[]{:S(2)}) async-start(bf16[16,144,256]{2,1,0:T(8,128)(2,1)} %shard_map.73), calls=%async_computation.1 | async-start | bytes 2359296 | tf_op jit(solution)/shard_map/all_to_all | solution.py:206
  9.8 0.0 copy-done.3
  9.8 0.1 copy_bitcast_fusion.3
  9.9 0.0 copy-done
  9.9 0.0 copy-done.4
  9.9 0.2 copy_bitcast_fusion.1
  10.1 1.5 %maximum_bitcast_fusion = bf16[16,144,384]{2,1,0:T(8,128)(2,1)} fusion(bf16[144,16,128]{2,0,1:T(8,128)(2,1)S(1)} %get-tuple-element.9, bf16[144,16,128]{2,0,1:T(8,128)(2,1)S(1)} %get-tuple-element.10, bf16[144,16,128]{2,0,1:T(8,128)(2,1)S(1)} %copy_bitcast_fusion.3), kind=kLoop, calls=%fused_computation | loop fusion | flops 5308416 | bytes 3538944 | tf_op jit(solution)/shard_map/transpose | solution.py:201
  11.6 0.0 copy-start.5
  11.6 17.4 %all-to-all-done.1 = bf16[16,144,256]{2,1,0:T(8,128)(2,1)S(1)} async-done(((bf16[16,144,256]{2,1,0:T(8,128)(2,1)}), bf16[16,144,256]{2,1,0:T(8,128)(2,1)S(1)}, u32[]{:S(2)}, u32[]{:S(2)}) %all-to-all-start.1) | async-done | bytes 1179680 | tf_op jit(solution)/shard_map/all_to_all | solution.py:206
  29.0 0.0 copy-start.2
  29.0 1.0 copy-done.2
  30.0 3.7 %all-to-all-start = ((bf16[16,144,384]{2,1,0:T(8,128)(2,1)}), bf16[16,144,384]{2,1,0:T(8,128)(2,1)S(1)}, u32[]{:S(2)}, u32[]{:S(2)}) async-start(bf16[16,144,384]{2,1,0:T(8,128)(2,1)} %maximum_bitcast_fusion), calls=%async_computation | async-start | bytes 3538944 | tf_op jit(solution)/shard_map/all_to_all | solution.py:202
  33.7 1.9 %collective-permute-start.1 = (bf16[2304,256]{1,0:T(8,128)(2,1)}, bf16[2304,256]{1,0:T(8,128)(2,1)S(1)}, u32[]{:S(2)}, u32[]{:S(2)}) collective-permute-start(bf16[2304,256]{1,0:T(8,128)(2,1)} %bitcast.29), channel_id=1, source_target_pairs={{32,0},{64,32},{96,64},{128,96},{160,128},{192,160},{224,192},{33,... | collective-permute-start | bytes 3538952 | tf_op jit(solution)/shard_map/ppermute | solution.py:30
  35.6 2.4 %collective-permute-start = (bf16[2304,256]{1,0:T(8,128)(2,1)}, bf16[2304,256]{1,0:T(8,128)(2,1)}, u32[]{:S(2)}, u32[]{:S(2)}) collective-permute-start(bf16[2304,256]{1,0:T(8,128)(2,1)} %bitcast.30), channel_id=1, source_target_pairs={{0,32},{32,64},{64,96},{96,128},{128,160},{160,192},{192,224},{1,3... | collective-permute-start | bytes 3538952 | tf_op jit(solution)/shard_map/ppermute | solution.py:29
  38.1 0.0 copy-done.5
  38.1 0.6 broadcast_subtract_fusion.ids_ref
  38.7 21.2 %all-to-all-done = bf16[16,144,384]{2,1,0:T(8,128)(2,1)S(1)} async-done(((bf16[16,144,384]{2,1,0:T(8,128)(2,1)}), bf16[16,144,384]{2,1,0:T(8,128)(2,1)S(1)}, u32[]{:S(2)}, u32[]{:S(2)}) %all-to-all-start) | async-done | bytes 1769504 | tf_op jit(solution)/shard_map/all_to_all | solution.py:202
  59.9 9.3 %shard_map.74 = (f32[2304,128]{1,0:T(8,128)}, f32[2304,128]{1,0:T(8,128)}) custom-call(s32[6,18]{1,0:T(8,128)} %broadcast_subtract_fusion.ids_ref, s32[6]{0:T(128)} %count_ref.3, bf16[2304,384]{1,0:T(8,128)(2,1)S(1)} %bitcast.26), custom_call_target="tpu_custom_call" | custom-call | tf_op jit(solution)/shard_map/pallas_call | solution.py:143
  69.2 0.0 collective-permute-done.1.refs_1_
  69.2 0.0 copy-start.1
  69.2 0.0 collective-permute-done.refs_0_
  69.2 1.0 copy-done.1
  70.2 17.9 %shard_map.75 = bf16[2304,128]{1,0:T(8,128)(2,1)} custom-call(s32[6,18]{1,0:T(8,128)} %broadcast_subtract_fusion.ids_ref, s32[6]{0:T(128)} %count_ref.3, bf16[2304,384]{1,0:T(8,128)(2,1)S(1)} %bitcast.27, bf16[2304,256]{1,0:T(8,128)(2,1)} %collective-permute-done.refs_0_, bf16[2304,256]{1,0:T(8,128)(2,1)} %copy-done.1, ...), custom_call_target="tpu_custom_call" | custom-call | tf_op jit(solution)/shard_map/pallas_call | solution.py:155
  88.2 16.2 %all_to_all.29 = bf16[16,144,128]{2,1,0:T(8,128)(2,1)S(1)} all-to-all(bf16[16,144,128]{2,1,0:T(8,128)(2,1)} %bitcast.28), channel_id=1, replica_groups=mesh['patch'=8,'seq'=16,'cfg'=2] {'seq'}, dimensions={0} | all-to-all | bytes 1179648 | tf_op jit(solution)/shard_map/all_to_all | solution.py:217
  104.4 0.9 copy_bitcast_fusion
Async XLA Ops:
  0.0 9.9 %copy-start = (bf16[144,2048]{1,0:T(8,128)(2,1)S(1)}, bf16[144,2048]{1,0:T(8,128)(2,1)}, u32[]{:S(2)}) copy-start(bf16[144,2048]{1,0:T(8,128)(2,1)} %param.8) | copy-start | bytes 1769476
  0.0 9.8 %copy-start.3 = (bf16[144,2048]{1,0:T(8,128)(2,1)S(1)}, bf16[144,2048]{1,0:T(8,128)(2,1)}, u32[]{:S(2)}) copy-start(bf16[144,2048]{1,0:T(8,128)(2,1)} %param.7) | copy-start | bytes 1769476
  2.6 7.3 %copy-start.4 = (bf16[144,2048]{1,0:T(8,128)(2,1)S(1)}, bf16[144,2048]{1,0:T(8,128)(2,1)}, u32[]{:S(2)}) copy-start(bf16[144,2048]{1,0:T(8,128)(2,1)} %param.9) | copy-start | bytes 1769476
  2.6 26.4 %all-to-all-start.1 = ((bf16[16,144,256]{2,1,0:T(8,128)(2,1)}), bf16[16,144,256]{2,1,0:T(8,128)(2,1)S(1)}, u32[]{:S(2)}, u32[]{:S(2)}) async-start(bf16[16,144,256]{2,1,0:T(8,128)(2,1)} %shard_map.73), calls=%async_computation.1 | async-start | bytes 2359296 | tf_op jit(solution)/shard_map/all_to_all | solution.py:206
  11.6 26.5 %copy-start.5 = (s32[6,18]{1,0:T(8,128)S(1)}, s32[6,18]{1,0:T(8,128)}, u32[]{:S(2)}) copy-start(s32[6,18]{1,0:T(8,128)} %param.12) | copy-start | bytes 1300
  29.0 1.0 copy-start.2
  30.0 29.9 %all-to-all-start = ((bf16[16,144,384]{2,1,0:T(8,128)(2,1)}), bf16[16,144,384]{2,1,0:T(8,128)(2,1)S(1)}, u32[]{:S(2)}, u32[]{:S(2)}) async-start(bf16[16,144,384]{2,1,0:T(8,128)(2,1)} %maximum_bitcast_fusion), calls=%async_computation | async-start | bytes 3538944 | tf_op jit(solution)/shard_map/all_to_all | solution.py:202
  33.7 35.5 %collective-permute-start.1 = (bf16[2304,256]{1,0:T(8,128)(2,1)}, bf16[2304,256]{1,0:T(8,128)(2,1)S(1)}, u32[]{:S(2)}, u32[]{:S(2)}) collective-permute-start(bf16[2304,256]{1,0:T(8,128)(2,1)} %bitcast.29), channel_id=1, source_target_pairs={{32,0},{64,32},{96,64},{128,96},{160,128},{192,160},{224,192},{33,... | collective-permute-start | bytes 3538952 | tf_op jit(solution)/shard_map/ppermute | solution.py:30
  35.6 33.5 %collective-permute-start = (bf16[2304,256]{1,0:T(8,128)(2,1)}, bf16[2304,256]{1,0:T(8,128)(2,1)}, u32[]{:S(2)}, u32[]{:S(2)}) collective-permute-start(bf16[2304,256]{1,0:T(8,128)(2,1)} %bitcast.30), channel_id=1, source_target_pairs={{0,32},{32,64},{64,96},{96,128},{128,160},{160,192},{192,224},{1,3... | collective-permute-start | bytes 3538952 | tf_op jit(solution)/shard_map/ppermute | solution.py:29
  69.2 1.0 copy-start.1

commit v15 on v11

--- a/solution.py
+++ b/solution.py
@@ -141,6 +141,7 @@
         return pl.BlockSpec(array.shape, lambda t, ids, cnt: (0, 0))
 
     fresh = pltpu.with_memory_space_constraint(fresh, pltpu.VMEM)
+    after = pltpu.with_memory_space_constraint(after, pltpu.VMEM)
     resident = pl.BlockSpec(memory_space=pltpu.VMEM)
 
     tile = pl.BlockSpec((TILE_TOKENS, width), lambda t, ids, cnt: (t, 0))
@@ -163,7 +164,7 @@
         grid_spec=pltpu.PrefetchScalarGridSpec(
             num_scalar_prefetch=2,
             grid=(tiles,),
-            in_specs=[resident, hbm, hbm, tile, tile],
+            in_specs=[resident, hbm, resident, tile, tile],
             out_specs=tile,
             scratch_shapes=[
                 pltpu.VMEM((2 * rows, before.shape[1]), before.dtype),

time: 107 us -> 107 us (level)
  blocking collectives: 14.4 us -> 15.9 us
    all_to_all x1, blocking collectives: 14.4 us -> 15.9 us  [on_device(): lax.all_to_all(merged, 'seq', split_axis=0, concat_axis=1, tiled=True)]
where the time goes in v15:
time: 107 us; the launch traced here: 106 us
  waiting for transfers between devices  38.6 us (36%)
  Pallas kernels  31.8 us (30%)
  blocking collectives  15.9 us (15%)
  starting transfers between devices  15.2 us (14%)
  local copies, waits for them, and re-layouts  2.23 us (2%)
  other arithmetic  2.04 us (2%)
    pallas_call x2, Pallas kernels, tile_attention(): pl.pallas_call(functools.partial(attention_kernel, local_heads, per_patch...  29.3 us
    all_to_all x1, waiting for transfers between devices, interleaved(): lax.all_to_all(joined, 'seq', split_axis=0, concat_axis=0, tiled=True)  21.2 us
    all_to_all x1, waiting for transfers between devices, on_device(): lax.all_to_all(joined, 'seq', split_axis=0, concat_axis=0, tiled=True)  17.4 us
    all_to_all x1, blocking collectives, on_device(): lax.all_to_all(merged, 'seq', split_axis=0, concat_axis=1, tiled=True)  15.9 us
    all_to_all x1, starting transfers between devices, on_device(): lax.all_to_all(joined, 'seq', split_axis=0, concat_axis=0, tiled=True)  7.17 us
    all_to_all x1, starting transfers between devices, interleaved(): lax.all_to_all(joined, 'seq', split_axis=0, concat_axis=0, tiled=True)  3.71 us
    pallas_call x1, Pallas kernels, regroup(): pl.pallas_call(functools.partial(regroup_kernel, width), out_shape=jax.Sh...  2.57 us
    ppermute x1, starting transfers between devices, with_halo(): before = lax.ppermute(last, axis, up)  2.41 us
  transfers between devices with their start and end apart: 4, of which 2 were waited for; matrix products, arithmetic and copies ran while one was open for 2% of the time, Pallas kernels for 10%

profile of v15, /device:TPU:128, one launch (start us, length us, event | category | flops | bytes accessed | tf_op | source)
XLA Modules:
  0.0 105.9 jit_solution(3751109094899973217)
XLA Ops:
  0.0 0.0 copy-start
  0.0 0.0 copy-start.2
  0.0 2.6 %shard_map.73 = bf16[16,144,256]{2,1,0:T(8,128)(2,1)} custom-call(bf16[144,2048]{1,0:T(8,128)(2,1)} %refs_0_.1, bf16[144,2048]{1,0:T(8,128)(2,1)} %refs_1_.1), custom_call_target="tpu_custom_call" | custom-call | tf_op jit(solution)/shard_map/pallas_call | solution.py:191
  2.6 0.0 copy-start.3
  2.6 7.2 %all-to-all-start.1 = ((bf16[16,144,256]{2,1,0:T(8,128)(2,1)}), bf16[16,144,256]{2,1,0:T(8,128)(2,1)S(1)}, u32[]{:S(2)}, u32[]{:S(2)}) async-start(bf16[16,144,256]{2,1,0:T(8,128)(2,1)} %shard_map.73), calls=%async_computation.1 | async-start | bytes 2359296 | tf_op jit(solution)/shard_map/all_to_all | solution.py:212
  9.8 0.0 copy-done.2
  9.8 0.1 copy_bitcast_fusion.3
  9.9 0.0 copy-done
  9.9 0.0 copy-done.3
  9.9 0.2 copy_bitcast_fusion.1
  10.1 1.4 %maximum_bitcast_fusion = bf16[16,144,384]{2,1,0:T(8,128)(2,1)} fusion(bf16[144,16,128]{2,0,1:T(8,128)(2,1)S(1)} %get-tuple-element.9, bf16[144,16,128]{2,0,1:T(8,128)(2,1)S(1)} %get-tuple-element.10, bf16[144,16,128]{2,0,1:T(8,128)(2,1)S(1)} %copy_bitcast_fusion.3), kind=kLoop, calls=%fused_computation | loop fusion | flops 5308416 | bytes 3538944 | tf_op jit(solution)/shard_map/transpose | solution.py:207
  11.6 0.0 copy-start.4
  11.6 17.4 %all-to-all-done.1 = bf16[16,144,256]{2,1,0:T(8,128)(2,1)S(1)} async-done(((bf16[16,144,256]{2,1,0:T(8,128)(2,1)}), bf16[16,144,256]{2,1,0:T(8,128)(2,1)S(1)}, u32[]{:S(2)}, u32[]{:S(2)}) %all-to-all-start.1) | async-done | bytes 1179680 | tf_op jit(solution)/shard_map/all_to_all | solution.py:212
  29.0 0.0 copy-start.1
  29.0 1.0 copy-done.1
  30.0 3.7 %all-to-all-start = ((bf16[16,144,384]{2,1,0:T(8,128)(2,1)}), bf16[16,144,384]{2,1,0:T(8,128)(2,1)S(1)}, u32[]{:S(2)}, u32[]{:S(2)}) async-start(bf16[16,144,384]{2,1,0:T(8,128)(2,1)} %maximum_bitcast_fusion), calls=%async_computation | async-start | bytes 3538944 | tf_op jit(solution)/shard_map/all_to_all | solution.py:208
  33.7 1.9 %collective-permute-start.1 = (bf16[2304,256]{1,0:T(8,128)(2,1)}, bf16[2304,256]{1,0:T(8,128)(2,1)S(1)}, u32[]{:S(2)}, u32[]{:S(2)}) collective-permute-start(bf16[2304,256]{1,0:T(8,128)(2,1)} %bitcast.29), channel_id=1, source_target_pairs={{32,0},{64,32},{96,64},{128,96},{160,128},{192,160},{224,192},{33,... | collective-permute-start | bytes 3538952 | tf_op jit(solution)/shard_map/ppermute | solution.py:30
  35.7 2.4 %collective-permute-start = (bf16[2304,256]{1,0:T(8,128)(2,1)}, bf16[2304,256]{1,0:T(8,128)(2,1)}, u32[]{:S(2)}, u32[]{:S(2)}) collective-permute-start(bf16[2304,256]{1,0:T(8,128)(2,1)} %bitcast.30), channel_id=1, source_target_pairs={{0,32},{32,64},{64,96},{96,128},{128,160},{160,192},{192,224},{1,3... | collective-permute-start | bytes 3538952 | tf_op jit(solution)/shard_map/ppermute | solution.py:29
  38.1 0.0 copy-done.4
  38.1 0.6 broadcast_subtract_fusion.ids_ref
  38.7 21.2 %all-to-all-done = bf16[16,144,384]{2,1,0:T(8,128)(2,1)S(1)} async-done(((bf16[16,144,384]{2,1,0:T(8,128)(2,1)}), bf16[16,144,384]{2,1,0:T(8,128)(2,1)S(1)}, u32[]{:S(2)}, u32[]{:S(2)}) %all-to-all-start) | async-done | bytes 1769504 | tf_op jit(solution)/shard_map/all_to_all | solution.py:208
  59.9 10.1 %shard_map.74 = (f32[2304,128]{1,0:T(8,128)}, f32[2304,128]{1,0:T(8,128)}) custom-call(s32[6,18]{1,0:T(8,128)} %broadcast_subtract_fusion.ids_ref, s32[6]{0:T(128)} %count_ref.3, bf16[2304,384]{1,0:T(8,128)(2,1)S(1)} %bitcast.26), custom_call_target="tpu_custom_call" | custom-call | tf_op jit(solution)/shard_map/pallas_call | solution.py:149
  70.0 0.0 collective-permute-done.1.refs_1_
  70.0 0.0 collective-permute-done.refs_0_
  70.0 19.1 %shard_map.75 = bf16[2304,128]{1,0:T(8,128)(2,1)} custom-call(s32[6,18]{1,0:T(8,128)} %broadcast_subtract_fusion.ids_ref, s32[6]{0:T(128)} %count_ref.3, bf16[2304,384]{1,0:T(8,128)(2,1)S(1)} %bitcast.27, bf16[2304,256]{1,0:T(8,128)(2,1)} %collective-permute-done.refs_0_, bf16[2304,256]{1,0:T(8,128)(2,1)S(1)} %collective-permute-done.1.refs_1_, ...), custom_call_target="tpu_custom_call" | custom-call | tf_op jit(solution)/shard_map/pallas_call | solution.py:161
  89.2 15.9 %all_to_all.29 = bf16[16,144,128]{2,1,0:T(8,128)(2,1)S(1)} all-to-all(bf16[16,144,128]{2,1,0:T(8,128)(2,1)} %bitcast.28), channel_id=1, replica_groups=mesh['patch'=8,'seq'=16,'cfg'=2] {'seq'}, dimensions={0} | all-to-all | bytes 1179648 | tf_op jit(solution)/shard_map/all_to_all | solution.py:223
  105.0 0.9 copy_bitcast_fusion
Async XLA Ops:
  0.0 9.9 %copy-start = (bf16[144,2048]{1,0:T(8,128)(2,1)S(1)}, bf16[144,2048]{1,0:T(8,128)(2,1)}, u32[]{:S(2)}) copy-start(bf16[144,2048]{1,0:T(8,128)(2,1)} %param.8) | copy-start | bytes 1769476
  0.0 9.8 %copy-start.2 = (bf16[144,2048]{1,0:T(8,128)(2,1)S(1)}, bf16[144,2048]{1,0:T(8,128)(2,1)}, u32[]{:S(2)}) copy-start(bf16[144,2048]{1,0:T(8,128)(2,1)} %param.7) | copy-start | bytes 1769476
  2.6 7.3 %copy-start.3 = (bf16[144,2048]{1,0:T(8,128)(2,1)S(1)}, bf16[144,2048]{1,0:T(8,128)(2,1)}, u32[]{:S(2)}) copy-start(bf16[144,2048]{1,0:T(8,128)(2,1)} %param.9) | copy-start | bytes 1769476
  2.6 26.4 %all-to-all-start.1 = ((bf16[16,144,256]{2,1,0:T(8,128)(2,1)}), bf16[16,144,256]{2,1,0:T(8,128)(2,1)S(1)}, u32[]{:S(2)}, u32[]{:S(2)}) async-start(bf16[16,144,256]{2,1,0:T(8,128)(2,1)} %shard_map.73), calls=%async_computation.1 | async-start | bytes 2359296 | tf_op jit(solution)/shard_map/all_to_all | solution.py:212
  11.6 26.5 %copy-start.4 = (s32[6,18]{1,0:T(8,128)S(1)}, s32[6,18]{1,0:T(8,128)}, u32[]{:S(2)}) copy-start(s32[6,18]{1,0:T(8,128)} %param.12) | copy-start | bytes 1300
  29.0 1.0 copy-start.1
  30.0 29.9 %all-to-all-start = ((bf16[16,144,384]{2,1,0:T(8,128)(2,1)}), bf16[16,144,384]{2,1,0:T(8,128)(2,1)S(1)}, u32[]{:S(2)}, u32[]{:S(2)}) async-start(bf16[16,144,384]{2,1,0:T(8,128)(2,1)} %maximum_bitcast_fusion), calls=%async_computation | async-start | bytes 3538944 | tf_op jit(solution)/shard_map/all_to_all | solution.py:208
  33.7 36.3 %collective-permute-start.1 = (bf16[2304,256]{1,0:T(8,128)(2,1)}, bf16[2304,256]{1,0:T(8,128)(2,1)S(1)}, u32[]{:S(2)}, u32[]{:S(2)}) collective-permute-start(bf16[2304,256]{1,0:T(8,128)(2,1)} %bitcast.29), channel_id=1, source_target_pairs={{32,0},{64,32},{96,64},{128,96},{160,128},{192,160},{224,192},{33,... | collective-permute-start | bytes 3538952 | tf_op jit(solution)/shard_map/ppermute | solution.py:30
  35.7 34.4 %collective-permute-start = (bf16[2304,256]{1,0:T(8,128)(2,1)}, bf16[2304,256]{1,0:T(8,128)(2,1)}, u32[]{:S(2)}, u32[]{:S(2)}) collective-permute-start(bf16[2304,256]{1,0:T(8,128)(2,1)} %bitcast.30), channel_id=1, source_target_pairs={{0,32},{32,64},{64,96},{96,128},{128,160},{160,192},{192,224},{1,3... | collective-permute-start | bytes 3538952 | tf_op jit(solution)/shard_map/ppermute | solution.py:29

commit v16 on v15

--- a/solution.py
+++ b/solution.py
@@ -179,18 +179,30 @@
 
 
 def regroup_kernel(width, *refs):
-    *in_refs, o_ref = refs
-    seq_count = o_ref.shape[0]
-    for d in range(seq_count):
+    *in_refs, o_ref, sems = refs
+    copies = []
+    for d in range(o_ref.shape[0]):
         for a, ref in enumerate(in_refs):
-            o_ref[d, :, a * width:(a + 1) * width] = ref[:, d * width:(d + 1) * width]
+            copy = pltpu.make_async_copy(
+                ref.at[:, pl.ds(d * width, width)],
+                o_ref.at[d, :, pl.ds(a * width, width)],
+                sems.at[d * len(in_refs) + a],
+            )
+            copy.start()
+            copies.append(copy)
+    for copy in copies:
+        copy.wait()
 
 
 def regroup(arrays, seq_count, width):
     rows = arrays[0].shape[0]
+    anywhere = pl.BlockSpec(memory_space=pl.ANY)
     return pl.pallas_call(
         functools.partial(regroup_kernel, width),
         out_shape=jax.ShapeDtypeStruct((seq_count, rows, len(arrays) * width), arrays[0].dtype),
+        in_specs=[anywhere] * len(arrays),
+        out_specs=anywhere,
+        scratch_shapes=[pltpu.SemaphoreType.DMA((seq_count * len(arrays),))],
     )(*arrays)
 
 

time: 107 us -> 142 us (1.33); the launches traced: 106 us -> 139 us
  Pallas kernels: 31.8 us -> 65.3 us
    pallas_call x1, Pallas kernels: 2.57 us -> 37.1 us  [regroup(): pl.pallas_call(functools.partial(regroup_kernel, width), out_shape=jax.Sh...]
  transfers between devices with their start and end apart: 4 -> 4, of which waited for: 2 -> 2; matrix products, arithmetic and copies ran while one was open for 2% -> 2% of each run, Pallas kernels for 10% -> 7%
where the time goes in v16:
time: 142 us; the launch traced here: 139 us
  Pallas kernels  65.3 us (46%)
  waiting for transfers between devices  38.6 us (27%)
  blocking collectives  15.7 us (11%)
  starting transfers between devices  15.2 us (11%)
  local copies, waits for them, and re-layouts  2.23 us (2%)
  other arithmetic  2.04 us (1%)
    pallas_call x1, Pallas kernels, regroup(): pl.pallas_call(functools.partial(regroup_kernel, width), out_shape=jax.Sh...  37.1 us
    pallas_call x2, Pallas kernels, tile_attention(): pl.pallas_call(functools.partial(attention_kernel, local_heads, per_patch...  28.2 us
    all_to_all x1, waiting for transfers between devices, interleaved(): lax.all_to_all(joined, 'seq', split_axis=0, concat_axis=0, tiled=True)  21.2 us
    all_to_all x1, waiting for transfers between devices, on_device(): lax.all_to_all(joined, 'seq', split_axis=0, concat_axis=0, tiled=True)  17.4 us
    all_to_all x1, blocking collectives, on_device(): lax.all_to_all(merged, 'seq', split_axis=0, concat_axis=1, tiled=True)  15.7 us
    all_to_all x1, starting transfers between devices, on_device(): lax.all_to_all(joined, 'seq', split_axis=0, concat_axis=0, tiled=True)  7.18 us
    all_to_all x1, starting transfers between devices, interleaved(): lax.all_to_all(joined, 'seq', split_axis=0, concat_axis=0, tiled=True)  3.71 us
  transfers between devices with their start and end apart: 4, of which 2 were waited for; matrix products, arithmetic and copies ran while one was open for 2% of the time, Pallas kernels for 7%

profile of v16, /device:TPU:128, one launch (start us, length us, event | category | flops | bytes accessed | tf_op | source)
XLA Modules:
  0.0 139.2 jit_solution(18212718938729432978)
XLA Ops:
  0.0 0.0 copy-start
  0.0 0.0 copy-start.2
  0.0 37.1 %shard_map.73 = bf16[16,144,256]{2,1,0:T(8,128)(2,1)} custom-call(bf16[144,2048]{1,0:T(8,128)(2,1)} %refs_0_.1, bf16[144,2048]{1,0:T(8,128)(2,1)} %refs_1_.1), custom_call_target="tpu_custom_call" | custom-call | tf_op jit(solution)/shard_map/pallas_call | solution.py:200
  37.1 0.0 copy-start.3
  37.1 7.2 %all-to-all-start.1 = ((bf16[16,144,256]{2,1,0:T(8,128)(2,1)}), bf16[16,144,256]{2,1,0:T(8,128)(2,1)S(1)}, u32[]{:S(2)}, u32[]{:S(2)}) async-start(bf16[16,144,256]{2,1,0:T(8,128)(2,1)} %shard_map.73), calls=%async_computation.1 | async-start | bytes 2359296 | tf_op jit(solution)/shard_map/all_to_all | solution.py:224
  44.3 0.0 copy-done.2
  44.3 0.1 copy_bitcast_fusion.3
  44.5 0.0 copy-done
  44.5 0.0 copy-done.3
  44.5 0.2 copy_bitcast_fusion.1
  44.7 1.4 %maximum_bitcast_fusion = bf16[16,144,384]{2,1,0:T(8,128)(2,1)} fusion(bf16[144,16,128]{2,0,1:T(8,128)(2,1)S(1)} %get-tuple-element.9, bf16[144,16,128]{2,0,1:T(8,128)(2,1)S(1)} %get-tuple-element.10, bf16[144,16,128]{2,0,1:T(8,128)(2,1)S(1)} %copy_bitcast_fusion.3), kind=kLoop, calls=%fused_computation | loop fusion | flops 5308416 | bytes 3538944 | tf_op jit(solution)/shard_map/transpose | solution.py:219
  46.1 0.0 copy-start.4
  46.1 17.4 %all-to-all-done.1 = bf16[16,144,256]{2,1,0:T(8,128)(2,1)S(1)} async-done(((bf16[16,144,256]{2,1,0:T(8,128)(2,1)}), bf16[16,144,256]{2,1,0:T(8,128)(2,1)S(1)}, u32[]{:S(2)}, u32[]{:S(2)}) %all-to-all-start.1) | async-done | bytes 1179680 | tf_op jit(solution)/shard_map/all_to_all | solution.py:224
  63.6 0.0 copy-start.1
  63.6 1.0 copy-done.1
  64.6 3.7 %all-to-all-start = ((bf16[16,144,384]{2,1,0:T(8,128)(2,1)}), bf16[16,144,384]{2,1,0:T(8,128)(2,1)S(1)}, u32[]{:S(2)}, u32[]{:S(2)}) async-start(bf16[16,144,384]{2,1,0:T(8,128)(2,1)} %maximum_bitcast_fusion), calls=%async_computation | async-start | bytes 3538944 | tf_op jit(solution)/shard_map/all_to_all | solution.py:220
  68.3 1.9 %collective-permute-start.1 = (bf16[2304,256]{1,0:T(8,128)(2,1)}, bf16[2304,256]{1,0:T(8,128)(2,1)S(1)}, u32[]{:S(2)}, u32[]{:S(2)}) collective-permute-start(bf16[2304,256]{1,0:T(8,128)(2,1)} %bitcast.29), channel_id=1, source_target_pairs={{32,0},{64,32},{96,64},{128,96},{160,128},{192,160},{224,192},{33,... | collective-permute-start | bytes 3538952 | tf_op jit(solution)/shard_map/ppermute | solution.py:30
  70.2 2.4 %collective-permute-start = (bf16[2304,256]{1,0:T(8,128)(2,1)}, bf16[2304,256]{1,0:T(8,128)(2,1)}, u32[]{:S(2)}, u32[]{:S(2)}) collective-permute-start(bf16[2304,256]{1,0:T(8,128)(2,1)} %bitcast.30), channel_id=1, source_target_pairs={{0,32},{32,64},{64,96},{96,128},{128,160},{160,192},{192,224},{1,3... | collective-permute-start | bytes 3538952 | tf_op jit(solution)/shard_map/ppermute | solution.py:29
  72.7 0.0 copy-done.4
  72.7 0.6 broadcast_subtract_fusion.ids_ref
  73.3 21.2 %all-to-all-done = bf16[16,144,384]{2,1,0:T(8,128)(2,1)S(1)} async-done(((bf16[16,144,384]{2,1,0:T(8,128)(2,1)}), bf16[16,144,384]{2,1,0:T(8,128)(2,1)S(1)}, u32[]{:S(2)}, u32[]{:S(2)}) %all-to-all-start) | async-done | bytes 1769504 | tf_op jit(solution)/shard_map/all_to_all | solution.py:220
  94.5 10.3 %shard_map.74 = (f32[2304,128]{1,0:T(8,128)}, f32[2304,128]{1,0:T(8,128)}) custom-call(s32[6,18]{1,0:T(8,128)} %broadcast_subtract_fusion.ids_ref, s32[6]{0:T(128)} %count_ref.3, bf16[2304,384]{1,0:T(8,128)(2,1)S(1)} %bitcast.26), custom_call_target="tpu_custom_call" | custom-call | tf_op jit(solution)/shard_map/pallas_call | solution.py:149
  104.8 0.0 collective-permute-done.1.refs_1_
  104.8 0.0 collective-permute-done.refs_0_
  104.8 17.9 %shard_map.75 = bf16[2304,128]{1,0:T(8,128)(2,1)} custom-call(s32[6,18]{1,0:T(8,128)} %broadcast_subtract_fusion.ids_ref, s32[6]{0:T(128)} %count_ref.3, bf16[2304,384]{1,0:T(8,128)(2,1)S(1)} %bitcast.27, bf16[2304,256]{1,0:T(8,128)(2,1)} %collective-permute-done.refs_0_, bf16[2304,256]{1,0:T(8,128)(2,1)S(1)} %collective-permute-done.1.refs_1_, ...), custom_call_target="tpu_custom_call" | custom-call | tf_op jit(solution)/shard_map/pallas_call | solution.py:161
  122.7 15.7 %all_to_all.29 = bf16[16,144,128]{2,1,0:T(8,128)(2,1)S(1)} all-to-all(bf16[16,144,128]{2,1,0:T(8,128)(2,1)} %bitcast.28), channel_id=1, replica_groups=mesh['patch'=8,'seq'=16,'cfg'=2] {'seq'}, dimensions={0} | all-to-all | bytes 1179648 | tf_op jit(solution)/shard_map/all_to_all | solution.py:235
  138.4 0.9 copy_bitcast_fusion
Async XLA Ops:
  0.0 44.5 %copy-start = (bf16[144,2048]{1,0:T(8,128)(2,1)S(1)}, bf16[144,2048]{1,0:T(8,128)(2,1)}, u32[]{:S(2)}) copy-start(bf16[144,2048]{1,0:T(8,128)(2,1)} %param.8) | copy-start | bytes 1769476
  0.0 44.3 %copy-start.2 = (bf16[144,2048]{1,0:T(8,128)(2,1)S(1)}, bf16[144,2048]{1,0:T(8,128)(2,1)}, u32[]{:S(2)}) copy-start(bf16[144,2048]{1,0:T(8,128)(2,1)} %param.7) | copy-start | bytes 1769476
  37.1 7.3 %copy-start.3 = (bf16[144,2048]{1,0:T(8,128)(2,1)S(1)}, bf16[144,2048]{1,0:T(8,128)(2,1)}, u32[]{:S(2)}) copy-start(bf16[144,2048]{1,0:T(8,128)(2,1)} %param.9) | copy-start | bytes 1769476
  37.1 26.4 %all-to-all-start.1 = ((bf16[16,144,256]{2,1,0:T(8,128)(2,1)}), bf16[16,144,256]{2,1,0:T(8,128)(2,1)S(1)}, u32[]{:S(2)}, u32[]{:S(2)}) async-start(bf16[16,144,256]{2,1,0:T(8,128)(2,1)} %shard_map.73), calls=%async_computation.1 | async-start | bytes 2359296 | tf_op jit(solution)/shard_map/all_to_all | solution.py:224
  46.1 26.5 %copy-start.4 = (s32[6,18]{1,0:T(8,128)S(1)}, s32[6,18]{1,0:T(8,128)}, u32[]{:S(2)}) copy-start(s32[6,18]{1,0:T(8,128)} %param.12) | copy-start | bytes 1300
  63.6 1.0 copy-start.1
  64.6 29.9 %all-to-all-start = ((bf16[16,144,384]{2,1,0:T(8,128)(2,1)}), bf16[16,144,384]{2,1,0:T(8,128)(2,1)S(1)}, u32[]{:S(2)}, u32[]{:S(2)}) async-start(bf16[16,144,384]{2,1,0:T(8,128)(2,1)} %maximum_bitcast_fusion), calls=%async_computation | async-start | bytes 3538944 | tf_op jit(solution)/shard_map/all_to_all | solution.py:220
  68.3 36.5 %collective-permute-start.1 = (bf16[2304,256]{1,0:T(8,128)(2,1)}, bf16[2304,256]{1,0:T(8,128)(2,1)S(1)}, u32[]{:S(2)}, u32[]{:S(2)}) collective-permute-start(bf16[2304,256]{1,0:T(8,128)(2,1)} %bitcast.29), channel_id=1, source_target_pairs={{32,0},{64,32},{96,64},{128,96},{160,128},{192,160},{224,192},{33,... | collective-permute-start | bytes 3538952 | tf_op jit(solution)/shard_map/ppermute | solution.py:30
  70.2 34.6 %collective-permute-start = (bf16[2304,256]{1,0:T(8,128)(2,1)}, bf16[2304,256]{1,0:T(8,128)(2,1)}, u32[]{:S(2)}, u32[]{:S(2)}) collective-permute-start(bf16[2304,256]{1,0:T(8,128)(2,1)} %bitcast.30), channel_id=1, source_target_pairs={{0,32},{32,64},{64,96},{96,128},{128,160},{160,192},{192,224},{1,3... | collective-permute-start | bytes 3538952 | tf_op jit(solution)/shard_map/ppermute | solution.py:29

commit v17 on v14

--- a/solution.py
+++ b/solution.py
@@ -136,6 +136,7 @@
         return pl.BlockSpec(array.shape, lambda t, ids, cnt: (0, 0))
 
     fresh = pltpu.with_memory_space_constraint(fresh, pltpu.VMEM)
+    after = pltpu.with_memory_space_constraint(after, pltpu.VMEM)
     resident = pl.BlockSpec(memory_space=pltpu.VMEM)
 
     tile = pl.BlockSpec((TILE_TOKENS, width), lambda t, ids, cnt: (t, 0))
@@ -158,7 +159,7 @@
         grid_spec=pltpu.PrefetchScalarGridSpec(
             num_scalar_prefetch=2,
             grid=(tiles,),
-            in_specs=[resident, hbm, hbm, tile, tile],
+            in_specs=[resident, hbm, resident, tile, tile],
             out_specs=tile,
             scratch_shapes=[
                 pltpu.VMEM((2 * rows, before.shape[1]), before.dtype),

time: 107 us -> 106 us (level)
  Pallas kernels: 29.8 us -> 31.4 us
    pallas_call x2, Pallas kernels: 27.3 us -> 28.8 us  [tile_attention(): pl.pallas_call(functools.partial(attention_kernel, local_heads, per_patch...]
  transfers between devices with their start and end apart: 4 -> 4, of which waited for: 2 -> 2; matrix products, arithmetic and copies ran while one was open for 2% -> 2% of each run, Pallas kernels for 9% -> 10%
where the time goes in v17:
time: 106 us; the launch traced here: 105 us
  waiting for transfers between devices  38.6 us (36%)
  Pallas kernels  31.4 us (30%)
  blocking collectives  15.7 us (15%)
  starting transfers between devices  15.2 us (14%)
  local copies, waits for them, and re-layouts  2.23 us (2%)
  other arithmetic  2.04 us (2%)
    pallas_call x2, Pallas kernels, tile_attention(): pl.pallas_call(functools.partial(attention_kernel, local_heads, per_patch...  28.8 us
    all_to_all x1, waiting for transfers between devices, interleaved(): lax.all_to_all(joined, 'seq', split_axis=0, concat_axis=0, tiled=True)  21.2 us
    all_to_all x1, waiting for transfers between devices, on_device(): lax.all_to_all(joined, 'seq', split_axis=0, concat_axis=0, tiled=True)  17.4 us
    all_to_all x1, blocking collectives, on_device(): lax.all_to_all(merged, 'seq', split_axis=0, concat_axis=1, tiled=True)  15.7 us
    all_to_all x1, starting transfers between devices, on_device(): lax.all_to_all(joined, 'seq', split_axis=0, concat_axis=0, tiled=True)  7.17 us
    all_to_all x1, starting transfers between devices, interleaved(): lax.all_to_all(joined, 'seq', split_axis=0, concat_axis=0, tiled=True)  3.71 us
    pallas_call x1, Pallas kernels, regroup(): pl.pallas_call(functools.partial(regroup_kernel, width), out_shape=jax.Sh...  2.57 us
    ppermute x1, starting transfers between devices, with_halo(): before = lax.ppermute(last, axis, up)  2.41 us
  transfers between devices with their start and end apart: 4, of which 2 were waited for; matrix products, arithmetic and copies ran while one was open for 2% of the time, Pallas kernels for 10%

profile of v17, /device:TPU:128, one launch (start us, length us, event | category | flops | bytes accessed | tf_op | source)
XLA Modules:
  0.0 105.3 jit_solution(1977126883280748169)
XLA Ops:
  0.0 0.0 copy-start
  0.0 0.0 copy-start.2
  0.0 2.6 %shard_map.73 = bf16[16,144,256]{2,1,0:T(8,128)(2,1)} custom-call(bf16[144,2048]{1,0:T(8,128)(2,1)} %refs_0_.1, bf16[144,2048]{1,0:T(8,128)(2,1)} %refs_1_.1), custom_call_target="tpu_custom_call" | custom-call | tf_op jit(solution)/shard_map/pallas_call | solution.py:186
  2.6 0.0 copy-start.3
  2.6 7.2 %all-to-all-start.1 = ((bf16[16,144,256]{2,1,0:T(8,128)(2,1)}), bf16[16,144,256]{2,1,0:T(8,128)(2,1)S(1)}, u32[]{:S(2)}, u32[]{:S(2)}) async-start(bf16[16,144,256]{2,1,0:T(8,128)(2,1)} %shard_map.73), calls=%async_computation.1 | async-start | bytes 2359296 | tf_op jit(solution)/shard_map/all_to_all | solution.py:207
  9.8 0.0 copy-done.2
  9.8 0.1 copy_bitcast_fusion.3
  9.9 0.0 copy-done
  9.9 0.0 copy-done.3
  9.9 0.2 copy_bitcast_fusion.1
  10.1 1.4 %maximum_bitcast_fusion = bf16[16,144,384]{2,1,0:T(8,128)(2,1)} fusion(bf16[144,16,128]{2,0,1:T(8,128)(2,1)S(1)} %get-tuple-element.9, bf16[144,16,128]{2,0,1:T(8,128)(2,1)S(1)} %get-tuple-element.10, bf16[144,16,128]{2,0,1:T(8,128)(2,1)S(1)} %copy_bitcast_fusion.3), kind=kLoop, calls=%fused_computation | loop fusion | flops 5308416 | bytes 3538944 | tf_op jit(solution)/shard_map/transpose | solution.py:202
  11.6 0.0 copy-start.4
  11.6 17.4 %all-to-all-done.1 = bf16[16,144,256]{2,1,0:T(8,128)(2,1)S(1)} async-done(((bf16[16,144,256]{2,1,0:T(8,128)(2,1)}), bf16[16,144,256]{2,1,0:T(8,128)(2,1)S(1)}, u32[]{:S(2)}, u32[]{:S(2)}) %all-to-all-start.1) | async-done | bytes 1179680 | tf_op jit(solution)/shard_map/all_to_all | solution.py:207
  29.0 0.0 copy-start.1
  29.0 1.0 copy-done.1
  30.0 3.7 %all-to-all-start = ((bf16[16,144,384]{2,1,0:T(8,128)(2,1)}), bf16[16,144,384]{2,1,0:T(8,128)(2,1)S(1)}, u32[]{:S(2)}, u32[]{:S(2)}) async-start(bf16[16,144,384]{2,1,0:T(8,128)(2,1)} %maximum_bitcast_fusion), calls=%async_computation | async-start | bytes 3538944 | tf_op jit(solution)/shard_map/all_to_all | solution.py:203
  33.7 1.9 %collective-permute-start.1 = (bf16[2304,256]{1,0:T(8,128)(2,1)}, bf16[2304,256]{1,0:T(8,128)(2,1)S(1)}, u32[]{:S(2)}, u32[]{:S(2)}) collective-permute-start(bf16[2304,256]{1,0:T(8,128)(2,1)} %bitcast.29), channel_id=1, source_target_pairs={{32,0},{64,32},{96,64},{128,96},{160,128},{192,160},{224,192},{33,... | collective-permute-start | bytes 3538952 | tf_op jit(solution)/shard_map/ppermute | solution.py:30
  35.7 2.4 %collective-permute-start = (bf16[2304,256]{1,0:T(8,128)(2,1)}, bf16[2304,256]{1,0:T(8,128)(2,1)}, u32[]{:S(2)}, u32[]{:S(2)}) collective-permute-start(bf16[2304,256]{1,0:T(8,128)(2,1)} %bitcast.30), channel_id=1, source_target_pairs={{0,32},{32,64},{64,96},{96,128},{128,160},{160,192},{192,224},{1,3... | collective-permute-start | bytes 3538952 | tf_op jit(solution)/shard_map/ppermute | solution.py:29
  38.1 0.0 copy-done.4
  38.1 0.6 broadcast_subtract_fusion.ids_ref
  38.7 21.2 %all-to-all-done = bf16[16,144,384]{2,1,0:T(8,128)(2,1)S(1)} async-done(((bf16[16,144,384]{2,1,0:T(8,128)(2,1)}), bf16[16,144,384]{2,1,0:T(8,128)(2,1)S(1)}, u32[]{:S(2)}, u32[]{:S(2)}) %all-to-all-start) | async-done | bytes 1769504 | tf_op jit(solution)/shard_map/all_to_all | solution.py:203
  59.9 10.2 %shard_map.74 = (f32[2304,128]{1,0:T(8,128)}, f32[2304,128]{1,0:T(8,128)}) custom-call(s32[6,18]{1,0:T(8,128)} %broadcast_subtract_fusion.ids_ref, s32[6]{0:T(128)} %count_ref.3, bf16[2304,384]{1,0:T(8,128)(2,1)S(1)} %bitcast.26), custom_call_target="tpu_custom_call" | custom-call | tf_op jit(solution)/shard_map/pallas_call | solution.py:144
  70.1 0.0 collective-permute-done.1.refs_1_
  70.1 0.0 collective-permute-done.refs_0_
  70.1 18.6 %shard_map.75 = bf16[2304,128]{1,0:T(8,128)(2,1)} custom-call(s32[6,18]{1,0:T(8,128)} %broadcast_subtract_fusion.ids_ref, s32[6]{0:T(128)} %count_ref.3, bf16[2304,384]{1,0:T(8,128)(2,1)S(1)} %bitcast.27, bf16[2304,256]{1,0:T(8,128)(2,1)} %collective-permute-done.refs_0_, bf16[2304,256]{1,0:T(8,128)(2,1)S(1)} %collective-permute-done.1.refs_1_, ...), custom_call_target="tpu_custom_call" | custom-call | tf_op jit(solution)/shard_map/pallas_call | solution.py:156
  88.7 15.7 %all_to_all.29 = bf16[16,144,128]{2,1,0:T(8,128)(2,1)S(1)} all-to-all(bf16[16,144,128]{2,1,0:T(8,128)(2,1)} %bitcast.28), channel_id=1, replica_groups=mesh['patch'=8,'seq'=16,'cfg'=2] {'seq'}, dimensions={0} | all-to-all | bytes 1179648 | tf_op jit(solution)/shard_map/all_to_all | solution.py:218
  104.4 0.9 copy_bitcast_fusion
Async XLA Ops:
  0.0 9.9 %copy-start = (bf16[144,2048]{1,0:T(8,128)(2,1)S(1)}, bf16[144,2048]{1,0:T(8,128)(2,1)}, u32[]{:S(2)}) copy-start(bf16[144,2048]{1,0:T(8,128)(2,1)} %param.8) | copy-start | bytes 1769476
  0.0 9.8 %copy-start.2 = (bf16[144,2048]{1,0:T(8,128)(2,1)S(1)}, bf16[144,2048]{1,0:T(8,128)(2,1)}, u32[]{:S(2)}) copy-start(bf16[144,2048]{1,0:T(8,128)(2,1)} %param.7) | copy-start | bytes 1769476
  2.6 7.3 %copy-start.3 = (bf16[144,2048]{1,0:T(8,128)(2,1)S(1)}, bf16[144,2048]{1,0:T(8,128)(2,1)}, u32[]{:S(2)}) copy-start(bf16[144,2048]{1,0:T(8,128)(2,1)} %param.9) | copy-start | bytes 1769476
  2.6 26.4 %all-to-all-start.1 = ((bf16[16,144,256]{2,1,0:T(8,128)(2,1)}), bf16[16,144,256]{2,1,0:T(8,128)(2,1)S(1)}, u32[]{:S(2)}, u32[]{:S(2)}) async-start(bf16[16,144,256]{2,1,0:T(8,128)(2,1)} %shard_map.73), calls=%async_computation.1 | async-start | bytes 2359296 | tf_op jit(solution)/shard_map/all_to_all | solution.py:207
  11.6 26.5 %copy-start.4 = (s32[6,18]{1,0:T(8,128)S(1)}, s32[6,18]{1,0:T(8,128)}, u32[]{:S(2)}) copy-start(s32[6,18]{1,0:T(8,128)} %param.12) | copy-start | bytes 1300
  29.0 1.0 copy-start.1
  30.0 29.9 %all-to-all-start = ((bf16[16,144,384]{2,1,0:T(8,128)(2,1)}), bf16[16,144,384]{2,1,0:T(8,128)(2,1)S(1)}, u32[]{:S(2)}, u32[]{:S(2)}) async-start(bf16[16,144,384]{2,1,0:T(8,128)(2,1)} %maximum_bitcast_fusion), calls=%async_computation | async-start | bytes 3538944 | tf_op jit(solution)/shard_map/all_to_all | solution.py:203
  33.7 36.4 %collective-permute-start.1 = (bf16[2304,256]{1,0:T(8,128)(2,1)}, bf16[2304,256]{1,0:T(8,128)(2,1)S(1)}, u32[]{:S(2)}, u32[]{:S(2)}) collective-permute-start(bf16[2304,256]{1,0:T(8,128)(2,1)} %bitcast.29), channel_id=1, source_target_pairs={{32,0},{64,32},{96,64},{128,96},{160,128},{192,160},{224,192},{33,... | collective-permute-start | bytes 3538952 | tf_op jit(solution)/shard_map/ppermute | solution.py:30
  35.7 34.5 %collective-permute-start = (bf16[2304,256]{1,0:T(8,128)(2,1)}, bf16[2304,256]{1,0:T(8,128)(2,1)}, u32[]{:S(2)}, u32[]{:S(2)}) collective-permute-start(bf16[2304,256]{1,0:T(8,128)(2,1)} %bitcast.30), channel_id=1, source_target_pairs={{0,32},{32,64},{64,96},{96,128},{128,160},{160,192},{192,224},{1,3... | collective-permute-start | bytes 3538952 | tf_op jit(solution)/shard_map/ppermute | solution.py:29
